TPU v7x, 512 devices: a whole 4x4x16 slice. The times are simulated.
512 devices in a mesh: seq: 64 (over y, z_lo, core), tp: 8 (over z_hi, x).
Axes of the slice: x: 4, y: 4, z: 16 (z_hi: 2, z_lo: 8; z = z_hi * 8 + z_lo), core: 2. Of those that a mesh axis runs over, the one named last changes fastest.
Arguments:
- tokens: bfloat16 [16384, 4096], P('seq', 'tp'), may hold values from -6 to 6
- ln_gain: float32 [4096], replicated, may hold values from 0.1 to 1.9
- ln_bias: float32 [4096], replicated, may hold values from -3 to 3
- w_qkv: bfloat16 [4096, 16, 3, 128], P('seq', 'tp'), may hold values from -3 to 3
- w_out: bfloat16 [16, 128, 4096], P('tp', None, 'seq'), may hold values from -0.25 to 0.25
- layer_scale: float32 [4096], P('tp'), may hold values from 0.5 to 2
- grids: int32 [14], replicated, may hold values from 24 to 40, as said below
- offsets: int32 [15], replicated, may hold values from 0 to 15302, as said below
Outputs:
- merged: bfloat16 [16384, 4, 4096], P('seq', None, 'tp')
Inputs may be any that keep to these rules, and one draw needn't show every extreme that they name: `grids`: every side is even and some image has side exactly 40. Of images 2k and 2k + 1, one side is drawn and the other is the largest even side of at most 40 whose square keeps the two squares' sum within 2176. offsets[0] = 0 and offsets[s + 1] = offsets[s] + 5 + grids[s] * grids[s].
All inputs are finite; a program needn't handle non-finite values.
Results may differ from a plain program's by a relative error of at most 0.015.
Values may be sent and summed in bfloat16 or wider, within the bound.
No kernel may reach another device: no remote copies, remote signals or barrier semaphores. Data moves between devices by JAX's collectives and lax.ppermute only.
A program may use at most 64 MiB of HBM per device.

v0:
```python
import math

import jax
import jax.numpy as jnp
from jax import lax
from jax.sharding import PartitionSpec as P

HALO = 48
REACH = 7


def from_behind(shard, axis, by):
    count = lax.axis_size(axis)
    pairs = [(i, i + by) for i in range(count) if 0 <= i + by < count]
    return lax.ppermute(shard, axis, pairs)


def layout_rows(row_ids, offsets, grids, row_count):
    images = grids.shape[0]
    image_ends = offsets[1:]
    segment = jnp.sum((row_ids[:, None] >= image_ends[None, :]).astype(jnp.int32), axis=1)
    inside = (row_ids >= 0) & (row_ids < row_count) & (segment < images)
    onehot = (
        jnp.minimum(segment, images - 1)[:, None] == jnp.arange(images, dtype=jnp.int32)[None, :]
    ).astype(jnp.int32)
    image_start = jnp.sum(onehot * offsets[None, :-1], axis=1)
    grid_side = jnp.sum(onehot * grids[None, :], axis=1)
    position = row_ids - image_start
    is_patch = inside & (position >= 5)
    patch_index = jnp.maximum(position - 5, 0)
    return (segment, inside, is_patch, patch_index // grid_side, patch_index % grid_side, grid_side)


def rotate(vectors, is_patch, grid_row, grid_col, grid_side):
    quarter = vectors.shape[-1] // 4
    frequency = 2.0 * math.pi * jnp.power(100.0, -jnp.arange(quarter, dtype=jnp.float32) / quarter)
    side_float = grid_side.astype(jnp.float32)
    coord_row = (2 * grid_row + 1).astype(jnp.float32) / side_float - 1.0
    coord_col = (2 * grid_col + 1).astype(jnp.float32) / side_float - 1.0
    angles_row = jnp.where(is_patch[:, None], coord_row[:, None] * frequency[None, :], 0.0)
    angles_col = jnp.where(is_patch[:, None], coord_col[:, None] * frequency[None, :], 0.0)

    def rotate_half(block_vals, angles):
        first_half = block_vals[..., :quarter]
        second_half = block_vals[..., quarter:]
        cosine = jnp.cos(angles)[:, None, :]
        sine_part = jnp.sin(angles)[:, None, :]
        return jnp.concatenate(
            [
                first_half * cosine - second_half * sine_part,
                second_half * cosine + first_half * sine_part,
            ],
            axis=-1,
        )

    return jnp.concatenate(
        [
            rotate_half(vectors[..., : 2 * quarter], angles_row),
            rotate_half(vectors[..., 2 * quarter :], angles_col),
        ],
        axis=-1,
    )


def attend_blocks(query_matrix, kv_blocks, key_segment, key_inside, query_segment, query_inside):
    logit_scale_factor = 1.0 / math.sqrt(query_matrix.shape[-1])
    rows_here = query_matrix.shape[0]
    heads_here = query_matrix.shape[1]

    def block_scores(block_of_keys, segment_block, inside_block):
        attention_logits = (
            jnp.einsum(
                "ecn,dcn->ced", query_matrix, block_of_keys, preferred_element_type=jnp.float32
            )
            * logit_scale_factor
        )
        allowed = (
            query_inside[:, None]
            & inside_block[None, :]
            & (query_segment[:, None] == segment_block[None, :])
        )
        return (jnp.where(allowed[None], attention_logits, -1e30), allowed)

    def max_step(carry, input_block_rows):
        row_max, row_total = carry
        masked, allowed = block_scores(
            input_block_rows[0][:, 0], input_block_rows[1], input_block_rows[2]
        )
        new_max = jnp.maximum(row_max, jnp.max(masked, axis=2, keepdims=True))
        exp_terms = jnp.where(allowed[None], jnp.exp(masked - new_max), 0.0)
        row_total = row_total * jnp.exp(row_max - new_max) + jnp.sum(
            exp_terms, axis=2, keepdims=True
        )
        return ((new_max, row_total), None)

    start_max = jnp.full((heads_here, rows_here, 1), -1e30, jnp.float32)
    start_total = jnp.zeros((heads_here, rows_here, 1), jnp.float32)
    (row_max, row_total), _ = lax.scan(
        max_step, (start_max, start_total), (kv_blocks, key_segment, key_inside)
    )
    row_total = jnp.where(query_inside[None, :, None], row_total, 1.0)

    def sum_step(running, input_block_rows):
        masked, allowed = block_scores(
            input_block_rows[0][:, 0], input_block_rows[1], input_block_rows[2]
        )
        exp_terms = jnp.where(allowed[None], jnp.exp(masked - row_max), 0.0)
        softmax_probabilities = (exp_terms / row_total).astype(jnp.bfloat16)
        return (
            running
            + jnp.einsum(
                "vgm,mvb->gvb",
                softmax_probabilities,
                input_block_rows[0][:, 1],
                preferred_element_type=jnp.float32,
            ),
            None,
        )

    start_sum = jnp.zeros((rows_here, heads_here, query_matrix.shape[2]), jnp.float32)
    attended_output, _ = lax.scan(sum_step, start_sum, (kv_blocks, key_segment, key_inside))
    attended_output = jnp.where(query_inside[:, None, None], attended_output, 0.0)
    return attended_output.astype(jnp.bfloat16)


def body(tokens, ln_gain, ln_bias, w_qkv, w_out, layer_scale, grids, offsets):
    rows_here = tokens.shape[0]
    row_count = rows_here * lax.axis_size("seq")
    first_row = lax.axis_index("seq") * rows_here
    gathered = lax.all_gather(tokens, "tp", axis=1, tiled=True)
    widened = gathered.astype(jnp.float32)
    average = jnp.mean(widened, axis=-1, keepdims=True)
    spread_sq = jnp.mean(jnp.square(widened - average), axis=-1, keepdims=True)
    normed = ((widened - average) * lax.rsqrt(spread_sq + 1e-06) * ln_gain + ln_bias).astype(
        jnp.bfloat16
    )
    qkv_sums = jnp.einsum(
        "td,dhcf->thcf",
        normed,
        lax.all_gather(w_qkv, "seq", axis=0, tiled=True),
        preferred_element_type=jnp.float32,
    )
    row_ids = first_row + jnp.arange(rows_here, dtype=jnp.int32)
    segment, inside, is_patch, grid_row, grid_col, grid_side = layout_rows(
        row_ids, offsets, grids, row_count
    )
    query_matrix = rotate(qkv_sums[:, :, 0], is_patch, grid_row, grid_col, grid_side).astype(
        jnp.bfloat16
    )
    roped_keys = rotate(qkv_sums[:, :, 1], is_patch, grid_row, grid_col, grid_side).astype(
        jnp.bfloat16
    )
    values = qkv_sums[:, :, 2].astype(jnp.bfloat16)
    key_value = jnp.stack([roped_keys, values], axis=1)
    block_count = 2 * REACH + 1
    pieces = []
    for block_slot in range(block_count):
        distance = REACH - block_slot
        if distance == 0:
            pieces.append(key_value)
        else:
            pieces.append(from_behind(key_value, "seq", distance))
    kv_blocks = jnp.stack(pieces, axis=0)
    key_rows = first_row - REACH * rows_here + jnp.arange(block_count * rows_here, dtype=jnp.int32)
    key_layout = layout_rows(key_rows, offsets, grids, row_count)
    key_segment = key_layout[0].reshape(block_count, rows_here)
    key_inside = key_layout[1].reshape(block_count, rows_here)
    attended_output = attend_blocks(
        query_matrix, kv_blocks, key_segment, key_inside, segment, inside
    )
    projected = jnp.einsum(
        "thf,hfc->tc",
        attended_output,
        lax.all_gather(w_out, "seq", axis=2, tiled=True),
        preferred_element_type=jnp.float32,
    )
    head_share = lax.psum_scatter(
        projected.astype(jnp.bfloat16), "tp", scatter_dimension=1, tiled=True
    ).astype(jnp.float32)
    layer_out = (tokens.astype(jnp.float32) + layer_scale * head_share).astype(jnp.bfloat16)
    next_rows = from_behind(layer_out[:HALO], "seq", -1)
    extended = jnp.concatenate([layer_out, next_rows], axis=0)
    is_corner = is_patch & (grid_row % 2 == 0) & (grid_col % 2 == 0)
    local_ids = jnp.arange(rows_here, dtype=jnp.int32)
    corner_index = jnp.stack(
        [local_ids, local_ids + 1, local_ids + grid_side, local_ids + grid_side + 1], axis=1
    )
    corner_index = jnp.clip(corner_index, 0, extended.shape[0] - 1)
    merged = jnp.take(extended, corner_index, axis=0)
    return jnp.where(is_corner[:, None, None], merged, jnp.zeros_like(merged))


def solution(mesh):
    placed = (
        P("seq", "tp"),
        P(),
        P(),
        P("seq", "tp", None, None),
        P("tp", None, "seq"),
        P("tp"),
        P(),
        P(),
    )
    return jax.shard_map(
        body, mesh=mesh, in_specs=placed, out_specs=P("seq", None, "tp"), check_vma=False
    )
```

profile of v0, /device:TPU:1, one launch (start us, length us, event | category | flops | bytes accessed | tf_op | source)
XLA Modules:
  0.0 669.1 jit_solution(13033573889273032923)
XLA Ops:
  12.0 115.7 %all-gather.4.cloned.1.call-done = bf16[256,4096]{1,0:T(8,128)(2,1)} async-done(((bf16[256,512]{1,0:T(8,128)(2,1)}), bf16[256,4096]{1,0:T(8,128)(2,1)}) %all-gather.4.cloned.1.call-update) | async-done | bytes 2097168 | tf_op jit(solution)/shard_map/all_gather | solution.py:130
  132.1 122.1 %all-gather.6.cloned.1.call-done = bf16[4096,2,3,128]{3,0,2,1:T(8,128)(2,1)} async-done(((bf16[64,2,3,128]{3,0,2,1:T(8,128)(2,1)}), bf16[4096,2,3,128]{3,0,2,1:T(8,128)(2,1)}) %all-gather.6.cloned.1.call-update) | async-done | bytes 6291472 | tf_op jit(solution)/shard_map/all_gather | solution.py:140
  254.3 5.7 fusion.29
  260.2 6.1 collective-permute-start
  268.7 3.8 collective-permute-start.2
  272.5 4.0 collective-permute-start.3
  276.4 3.2 collective-permute-start.4
  279.9 20.5 %collective-permute-start.5 = (bf16[256,2,2,128]{0,3,2,1:T(8,128)(2,1)S(1)}, bf16[256,2,2,128]{0,3,2,1:T(8,128)(2,1)S(1)}, u32[]{:S(2)}, u32[]{:S(2)}) collective-permute-start(bf16[256,2,2,128]{0,3,2,1:T(8,128)(2,1)S(1)} %pad_maximum_fusion.1), channel_id=1, source_target_pairs={{0,16},{8,24},{16,32},{24,40},{32,48},{40,56},{48,64},{56,72},{64,... | collective-permute-start | bytes 786440 | tf_op jit(solution)/shard_map/ppermute | solution.py:15
  301.1 5.2 collective-permute-start.6
  318.5 22.9 %collective-permute-done.7 = bf16[256,2,2,128]{0,3,2,1:T(8,128)(2,1)S(1)} collective-permute-done((bf16[256,2,2,128]{0,3,2,1:T(8,128)(2,1)S(1)}, bf16[256,2,2,128]{0,3,2,1:T(8,128)(2,1)S(1)}, u32[]{:S(2)}, u32[]{:S(2)}) %collective-permute-start.7) | collective-permute-done | bytes 262176 | tf_op jit(solution)/shard_map/ppermute | solution.py:15
  343.4 3.6 collective-permute-done.8
  349.0 21.4 %collective-permute-done.9 = bf16[256,2,2,128]{0,3,2,1:T(8,128)(2,1)S(1)} collective-permute-done((bf16[256,2,2,128]{0,3,2,1:T(8,128)(2,1)S(1)}, bf16[256,2,2,128]{0,3,2,1:T(8,128)(2,1)S(1)}, u32[]{:S(2)}, u32[]{:S(2)}) %collective-permute-start.9) | collective-permute-done | bytes 262176 | tf_op jit(solution)/shard_map/ppermute | solution.py:15
  371.8 27.3 %collective-permute-done.11 = bf16[256,2,2,128]{0,3,2,1:T(8,128)(2,1)S(1)} collective-permute-done((bf16[256,2,2,128]{0,3,2,1:T(8,128)(2,1)S(1)}, bf16[256,2,2,128]{0,3,2,1:T(8,128)(2,1)S(1)}, u32[]{:S(2)}, u32[]{:S(2)}) %collective-permute-start.11) | collective-permute-done | bytes 262176 | tf_op jit(solution)/shard_map/ppermute | solution.py:15
  399.8 11.2 %collective-permute-done.12 = bf16[256,2,2,128]{0,3,2,1:T(8,128)(2,1)S(1)} collective-permute-done((bf16[256,2,2,128]{0,3,2,1:T(8,128)(2,1)S(1)}, bf16[256,2,2,128]{0,3,2,1:T(8,128)(2,1)S(1)}, u32[]{:S(2)}, u32[]{:S(2)}) %collective-permute-start.12) | collective-permute-done | bytes 262176 | tf_op jit(solution)/shard_map/ppermute | solution.py:15
  411.8 28.7 %collective-permute-done.13 = bf16[256,2,2,128]{0,3,2,1:T(8,128)(2,1)S(1)} collective-permute-done((bf16[256,2,2,128]{0,3,2,1:T(8,128)(2,1)S(1)}, bf16[256,2,2,128]{0,3,2,1:T(8,128)(2,1)S(1)}, u32[]{:S(2)}, u32[]{:S(2)}) %collective-permute-start.13) | collective-permute-done | bytes 262176 | tf_op jit(solution)/shard_map/ppermute | solution.py:15
  441.2 6.3 copy.44
  447.5 24.1 %while.24 = (s32[]{:T(128)}, f32[2,256,1]{1,0,2:T(2,128)S(1)}, f32[2,256,1]{1,0,2:T(2,128)S(1)}, pred[256]{0:T(512)(128)(4,1)S(1)}, pred[15,256]{1,0:T(8,128)(4,...) while((s32[]{:T(128)}, f32[2,256,1]{1,0,2:T(2,128)S(1)}, ...), condition=%wide.region_9.10_spmd.clone, body=%wide.region_6.9_spmd.clone.sunk | while | flops 34540032 | bytes 2063492 | solution.py:98
  471.6 25.9 %while.25 = (s32[]{:T(128)}, f32[256,2,128]{0,2,1:T(8,128)S(1)}, bf16[15,256,2,2,128]{4,1,3,2,0:T(8,128)(2,1)}, pred[256]{0:T(512)(128)(4,1)S(1)}, pred[15,256]{...) while((s32[]{:T(128)}, f32[256,2,128]{0,2,1:T(8,128)S(1)}, ...), condition=%wide.region_11.12_spmd.clone, body=%wide.region_10.11_spmd.clone.sunk | while | flops 68222976 | bytes 1582219 | solution.py:121
  497.5 5.0 all-gather.8.cloned.1.call-done
  502.5 3.7 fusion.21
  506.6 142.4 %reduce-scatter.2.cloned.1.call-done = bf16[256,512]{1,0:T(8,128)(2,1)} async-done(((bf16[256,4096]{1,0:T(8,128)(2,1)}), bf16[256,512]{1,0:T(8,128)(2,1)}) %reduce-scatter.2.cloned.1.call-update) | async-done | bytes 262160 | tf_op jit(solution)/shard_map/reduce_scatter | solution.py:177
  650.1 4.2 collective-permute-start.14
  655.5 4.0 gather_fusion
  659.8 2.8 select_select_fusion
  (305 shorter events, 84.3 us)
Async XLA Ops:
  6.5 247.8 %copy-start.4 = (f32[4096]{0:T(1024)S(1)}, f32[4096]{0:T(1024)}, u32[]{:S(2)}) copy-start(f32[4096]{0:T(1024)} %param.13) | copy-start | bytes 49156
  6.5 247.8 %copy-start.3 = (f32[4096]{0:T(1024)S(1)}, f32[4096]{0:T(1024)}, u32[]{:S(2)}) copy-start(f32[4096]{0:T(1024)} %param.14) | copy-start | bytes 49156
  6.5 121.2 %all-gather.4.cloned.1.call-start = ((), (), s32[]{:S(2)}) async-start(), calls=%async_computation.1 | async-start | bytes 2359296 | tf_op jit(solution)/shard_map/all_gather | solution.py:130
  7.3 247.0 %all-gather.6.cloned.1.call-start = ((), (), s32[]{:S(2)}) async-start(), calls=%async_computation.2 | async-start | bytes 6389760 | tf_op jit(solution)/shard_map/all_gather | solution.py:140
  8.9 493.6 %all-gather.8.cloned.1.call-start = ((), (), s32[]{:S(2)}) async-start(), calls=%async_computation.3 | async-start | bytes 2129920 | tf_op jit(solution)/shard_map/all_gather | solution.py:174
  9.6 639.4 %reduce-scatter.2.cloned.1.call-start = ((), (), s32[]{:S(2)}) async-start(), calls=%async_computation.4 | async-start | bytes 2359296 | tf_op jit(solution)/shard_map/reduce_scatter | solution.py:177
  127.7 126.5 %copy-start = (bf16[256,4096]{1,0:T(8,128)(2,1)S(1)}, bf16[256,4096]{1,0:T(8,128)(2,1)}, u32[]{:S(2)}) copy-start(bf16[256,4096]{1,0:T(8,128)(2,1)} %all-gather.4.cloned.1.call-done) | copy-start | bytes 6291460
  260.2 19.7 %collective-permute-start = (bf16[256,2,2,128]{0,3,2,1:T(8,128)(2,1)S(1)}, bf16[256,2,2,128]{0,3,2,1:T(8,128)(2,1)S(1)}, u32[]{:S(2)}, u32[]{:S(2)}) collective-permute-start(bf16[256,2,2,128]{0,3,2,1:T(8,128)(2,1)S(1)} %pad_maximum_fusion.1), channel_id=1, source_target_pairs={{0,56},{8,64},{16,72},{24,80},{32,88},{40,96},{48,104},{56,112},{6... | collective-permute-start | bytes 786440 | tf_op jit(solution)/shard_map/ppermute | solution.py:15
  266.3 34.8 %collective-permute-start.1 = (bf16[256,2,2,128]{0,3,2,1:T(8,128)(2,1)S(1)}, bf16[256,2,2,128]{0,3,2,1:T(8,128)(2,1)S(1)}, u32[]{:S(2)}, u32[]{:S(2)}) collective-permute-start(bf16[256,2,2,128]{0,3,2,1:T(8,128)(2,1)S(1)} %pad_maximum_fusion.1), channel_id=1, source_target_pairs={{0,48},{8,56},{16,64},{24,72},{32,80},{40,88},{48,96},{56,104},{64... | collective-permute-start | bytes 786440 | tf_op jit(solution)/shard_map/ppermute | solution.py:15
  268.7 38.4 %collective-permute-start.2 = (bf16[256,2,2,128]{0,3,2,1:T(8,128)(2,1)S(1)}, bf16[256,2,2,128]{0,3,2,1:T(8,128)(2,1)S(1)}, u32[]{:S(2)}, u32[]{:S(2)}) collective-permute-start(bf16[256,2,2,128]{0,3,2,1:T(8,128)(2,1)S(1)} %pad_maximum_fusion.1), channel_id=1, source_target_pairs={{0,40},{8,48},{16,56},{24,64},{32,72},{40,80},{48,88},{56,96},{64,... | collective-permute-start | bytes 786440 | tf_op jit(solution)/shard_map/ppermute | solution.py:15
  272.5 37.2 %collective-permute-start.3 = (bf16[256,2,2,128]{0,3,2,1:T(8,128)(2,1)S(1)}, bf16[256,2,2,128]{0,3,2,1:T(8,128)(2,1)S(1)}, u32[]{:S(2)}, u32[]{:S(2)}) collective-permute-start(bf16[256,2,2,128]{0,3,2,1:T(8,128)(2,1)S(1)} %pad_maximum_fusion.1), channel_id=1, source_target_pairs={{0,32},{8,40},{16,48},{24,56},{32,64},{40,72},{48,80},{56,88},{64,... | collective-permute-start | bytes 786440 | tf_op jit(solution)/shard_map/ppermute | solution.py:15
  276.4 35.3 %collective-permute-start.4 = (bf16[256,2,2,128]{0,3,2,1:T(8,128)(2,1)S(1)}, bf16[256,2,2,128]{0,3,2,1:T(8,128)(2,1)S(1)}, u32[]{:S(2)}, u32[]{:S(2)}) collective-permute-start(bf16[256,2,2,128]{0,3,2,1:T(8,128)(2,1)S(1)} %pad_maximum_fusion.1), channel_id=1, source_target_pairs={{0,24},{8,32},{16,40},{24,48},{32,56},{40,64},{48,72},{56,80},{64,... | collective-permute-start | bytes 786440 | tf_op jit(solution)/shard_map/ppermute | solution.py:15
  279.9 33.9 %collective-permute-start.5 = (bf16[256,2,2,128]{0,3,2,1:T(8,128)(2,1)S(1)}, bf16[256,2,2,128]{0,3,2,1:T(8,128)(2,1)S(1)}, u32[]{:S(2)}, u32[]{:S(2)}) collective-permute-start(bf16[256,2,2,128]{0,3,2,1:T(8,128)(2,1)S(1)} %pad_maximum_fusion.1), channel_id=1, source_target_pairs={{0,16},{8,24},{16,32},{24,40},{32,48},{40,56},{48,64},{56,72},{64,... | collective-permute-start | bytes 786440 | tf_op jit(solution)/shard_map/ppermute | solution.py:15
  301.1 14.7 %collective-permute-start.6 = (bf16[256,2,2,128]{0,3,2,1:T(8,128)(2,1)S(1)}, bf16[256,2,2,128]{0,3,2,1:T(8,128)(2,1)S(1)}, u32[]{:S(2)}, u32[]{:S(2)}) collective-permute-start(bf16[256,2,2,128]{0,3,2,1:T(8,128)(2,1)S(1)} %pad_maximum_fusion.1), channel_id=1, source_target_pairs={{0,8},{8,16},{16,24},{24,32},{32,40},{40,48},{48,56},{56,64},{64,7... | collective-permute-start | bytes 786440 | tf_op jit(solution)/shard_map/ppermute | solution.py:15
  307.1 34.3 %collective-permute-start.7 = (bf16[256,2,2,128]{0,3,2,1:T(8,128)(2,1)S(1)}, bf16[256,2,2,128]{0,3,2,1:T(8,128)(2,1)S(1)}, u32[]{:S(2)}, u32[]{:S(2)}) collective-permute-start(bf16[256,2,2,128]{0,3,2,1:T(8,128)(2,1)S(1)} %pad_maximum_fusion.1), channel_id=1, source_target_pairs={{8,0},{16,8},{24,16},{32,24},{40,32},{48,40},{56,48},{64,56},{72,6... | collective-permute-start | bytes 786440 | tf_op jit(solution)/shard_map/ppermute | solution.py:15
  309.7 37.3 %collective-permute-start.8 = (bf16[256,2,2,128]{0,3,2,1:T(8,128)(2,1)S(1)}, bf16[256,2,2,128]{0,3,2,1:T(8,128)(2,1)S(1)}, u32[]{:S(2)}, u32[]{:S(2)}) collective-permute-start(bf16[256,2,2,128]{0,3,2,1:T(8,128)(2,1)S(1)} %pad_maximum_fusion.1), channel_id=1, source_target_pairs={{16,0},{24,8},{32,16},{40,24},{48,32},{56,40},{64,48},{72,56},{80,... | collective-permute-start | bytes 786440 | tf_op jit(solution)/shard_map/ppermute | solution.py:15
  311.7 58.6 %collective-permute-start.9 = (bf16[256,2,2,128]{0,3,2,1:T(8,128)(2,1)S(1)}, bf16[256,2,2,128]{0,3,2,1:T(8,128)(2,1)S(1)}, u32[]{:S(2)}, u32[]{:S(2)}) collective-permute-start(bf16[256,2,2,128]{0,3,2,1:T(8,128)(2,1)S(1)} %pad_maximum_fusion.1), channel_id=1, source_target_pairs={{24,0},{32,8},{40,16},{48,24},{56,32},{64,40},{72,48},{80,56},{88,... | collective-permute-start | bytes 786440 | tf_op jit(solution)/shard_map/ppermute | solution.py:15
  313.7 57.4 %collective-permute-start.10 = (bf16[256,2,2,128]{0,3,2,1:T(8,128)(2,1)S(1)}, bf16[256,2,2,128]{0,3,2,1:T(8,128)(2,1)S(1)}, u32[]{:S(2)}, u32[]{:S(2)}) collective-permute-start(bf16[256,2,2,128]{0,3,2,1:T(8,128)(2,1)S(1)} %pad_maximum_fusion.1), channel_id=1, source_target_pairs={{32,0},{40,8},{48,16},{56,24},{64,32},{72,40},{80,48},{88,56},{96,... | collective-permute-start | bytes 786440 | tf_op jit(solution)/shard_map/ppermute | solution.py:15
  315.8 83.4 %collective-permute-start.11 = (bf16[256,2,2,128]{0,3,2,1:T(8,128)(2,1)S(1)}, bf16[256,2,2,128]{0,3,2,1:T(8,128)(2,1)S(1)}, u32[]{:S(2)}, u32[]{:S(2)}) collective-permute-start(bf16[256,2,2,128]{0,3,2,1:T(8,128)(2,1)S(1)} %pad_maximum_fusion.1), channel_id=1, source_target_pairs={{40,0},{48,8},{56,16},{64,24},{72,32},{80,40},{88,48},{96,56},{104... | collective-permute-start | bytes 786440 | tf_op jit(solution)/shard_map/ppermute | solution.py:15
  341.4 69.7 %collective-permute-start.12 = (bf16[256,2,2,128]{0,3,2,1:T(8,128)(2,1)S(1)}, bf16[256,2,2,128]{0,3,2,1:T(8,128)(2,1)S(1)}, u32[]{:S(2)}, u32[]{:S(2)}) collective-permute-start(bf16[256,2,2,128]{0,3,2,1:T(8,128)(2,1)S(1)} %pad_maximum_fusion.1), channel_id=1, source_target_pairs={{48,0},{56,8},{64,16},{72,24},{80,32},{88,40},{96,48},{104,56},{11... | collective-permute-start | bytes 786440 | tf_op jit(solution)/shard_map/ppermute | solution.py:15
  347.0 93.5 %collective-permute-start.13 = (bf16[256,2,2,128]{0,3,2,1:T(8,128)(2,1)S(1)}, bf16[256,2,2,128]{0,3,2,1:T(8,128)(2,1)S(1)}, u32[]{:S(2)}, u32[]{:S(2)}) collective-permute-start(bf16[256,2,2,128]{0,3,2,1:T(8,128)(2,1)S(1)} %pad_maximum_fusion.1), channel_id=1, source_target_pairs={{56,0},{64,8},{72,16},{80,24},{88,32},{96,40},{104,48},{112,56},{1... | collective-permute-start | bytes 786440 | tf_op jit(solution)/shard_map/ppermute | solution.py:15
  497.5 151.5 %copy-start.1 = (bf16[256,512]{1,0:T(8,128)(2,1)S(1)}, bf16[256,512]{1,0:T(8,128)(2,1)}, u32[]{:S(2)}) copy-start(bf16[256,512]{1,0:T(8,128)(2,1)} %param.12) | copy-start | bytes 786436
  497.5 151.5 %copy-start.2 = (f32[512]{0:T(512)S(1)}, f32[512]{0:T(512)}, u32[]{:S(2)}) copy-start(f32[512]{0:T(512)} %param.17) | copy-start | bytes 6148
  650.1 5.4 collective-permute-start.14
Sparse Core Ops, SparseCore 0:
  10.4 117.3 all-gather.3
  129.9 124.3 all-gather.5
  256.5 246.0 all-gather.7
  507.0 141.9 reduce-scatter.1
where the time goes:
time: 671 us; the launch traced here: 669 us
  waiting for transfers between devices  503 us (75%)
  starting transfers between devices  59.1 us (9%)
  local copies, waits for them, and re-layouts  54.2 us (8%)
  matrix products  21 us (3%)
  other arithmetic  17 us (3%)
  between operations  13.6 us (2%)
    reduce_scatter x1, waiting for transfers between devices, body(): lax.psum_scatter(projected.astype(jnp.bfloat16), 'tp', scatter_dimension=...  142 us
    all_gather x1, waiting for transfers between devices, body(): lax.all_gather(w_qkv, 'seq', axis=0, tiled=True)  122 us
    ppermute x15, waiting for transfers between devices, from_behind(): return lax.ppermute(shard, axis, pairs)  116 us
    all_gather x1, waiting for transfers between devices, body(): gathered = lax.all_gather(tokens, 'tp', axis=1, tiled=True)  116 us
    ppermute x15, starting transfers between devices, from_behind(): return lax.ppermute(shard, axis, pairs)  58.9 us
    squeeze x30, local copies, waits for them, and re-layouts, attend_blocks(): lax.scan(max_step, (start_max, start_total), (kv_blocks, key_segment, key...  29.2 us
    unnamed x27, local copies, waits for them, and re-layouts  17.4 us
  transfers between devices with their start and end apart: 19, of which 11 were waited for; matrix products, arithmetic and copies ran while one was open for 12% of the time, Pallas kernels for 0%

commit v1 on v0

--- a/solution.py
+++ b/solution.py
@@ -1,9 +1,10 @@
+import functools
 import math
 
 import jax
 import jax.numpy as jnp
 from jax import lax
-from jax.sharding import PartitionSpec as P
+from jax.sharding import Mesh, PartitionSpec as P
 
 HALO = 48
 REACH = 7
@@ -123,23 +124,55 @@
     return attended_output.astype(jnp.bfloat16)
 
 
-def body(tokens, ln_gain, ln_bias, w_qkv, w_out, layer_scale, grids, offsets):
+SEQ = ("y", "zl", "c")
+TP = ("zh", "x")
+
+
+def ring(shard, axis, size, by):
+    return lax.ppermute(shard, axis, [(i, (i + by) % size) for i in range(size)])
+
+
+def chain(shard, axis, size, by):
+    pairs = [(i, i + by) for i in range(size) if 0 <= i + by < size]
+    return lax.ppermute(shard, axis, pairs)
+
+
+def body(sizes, tokens, ln_gain, ln_bias, w_qkv, w_out, layer_scale, grids, offsets):
+    n_y, n_zl, n_c, n_zh, n_x = sizes
+    n_seq = n_y * n_zl * n_c
     rows_here = tokens.shape[0]
-    row_count = rows_here * lax.axis_size("seq")
-    first_row = lax.axis_index("seq") * rows_here
-    gathered = lax.all_gather(tokens, "tp", axis=1, tiled=True)
+    row_count = rows_here * n_seq
+    c = lax.axis_index("c")
+    zh = lax.axis_index("zh")
+    x = lax.axis_index("x")
+    seq_index = (lax.axis_index("y") * n_zl + lax.axis_index("zl")) * n_c + c
+    first_row = seq_index * rows_here
+
+    wq_mine = lax.all_gather(w_qkv, ("y", "zl"), axis=0, tiled=False)
+    wo_mine = lax.all_gather(w_out, ("y", "zl"), axis=2, tiled=False)
+    wq_other = ring(wq_mine, "c", n_c, 1)
+    wo_other = ring(wo_mine, "c", n_c, 1)
+
+    partner = ring(tokens, "zh", n_zh, 1)
+    pair = jnp.stack([tokens, partner])
+    received = [pair] + [ring(pair, "x", n_x, s) for s in range(1, n_x)]
+    by_shift = jnp.stack(received)
+    by_x = jnp.take(by_shift, (x - jnp.arange(n_x)) % n_x, axis=0)
+    by_zh = jnp.where(zh == 0, by_x, by_x[:, ::-1])
+    gathered = jnp.transpose(by_zh, (2, 1, 0, 3)).reshape(rows_here, -1)
+
     widened = gathered.astype(jnp.float32)
     average = jnp.mean(widened, axis=-1, keepdims=True)
     spread_sq = jnp.mean(jnp.square(widened - average), axis=-1, keepdims=True)
     normed = ((widened - average) * lax.rsqrt(spread_sq + 1e-06) * ln_gain + ln_bias).astype(
         jnp.bfloat16
     )
+    normed_v = normed.reshape(rows_here, n_y * n_zl, n_c, -1)
+    normed_mine = lax.dynamic_index_in_dim(normed_v, c, axis=2, keepdims=False)
+    normed_other = lax.dynamic_index_in_dim(normed_v, 1 - c, axis=2, keepdims=False)
     qkv_sums = jnp.einsum(
-        "td,dhcf->thcf",
-        normed,
-        lax.all_gather(w_qkv, "seq", axis=0, tiled=True),
-        preferred_element_type=jnp.float32,
-    )
+        "tjd,jdhcf->thcf", normed_mine, wq_mine, preferred_element_type=jnp.float32
+    ) + jnp.einsum("tjd,jdhcf->thcf", normed_other, wq_other, preferred_element_type=jnp.float32)
     row_ids = first_row + jnp.arange(rows_here, dtype=jnp.int32)
     segment, inside, is_patch, grid_row, grid_col, grid_side = layout_rows(
         row_ids, offsets, grids, row_count
@@ -153,13 +186,15 @@
     values = qkv_sums[:, :, 2].astype(jnp.bfloat16)
     key_value = jnp.stack([roped_keys, values], axis=1)
     block_count = 2 * REACH + 1
-    pieces = []
-    for block_slot in range(block_count):
-        distance = REACH - block_slot
-        if distance == 0:
-            pieces.append(key_value)
-        else:
-            pieces.append(from_behind(key_value, "seq", distance))
+    pieces = [None] * block_count
+    pieces[REACH] = key_value
+    from_left = key_value
+    from_right = key_value
+    for distance in range(1, REACH + 1):
+        from_left = chain(from_left, SEQ, n_seq, 1)
+        from_right = chain(from_right, SEQ, n_seq, -1)
+        pieces[REACH - distance] = from_left
+        pieces[REACH + distance] = from_right
     kv_blocks = jnp.stack(pieces, axis=0)
     key_rows = first_row - REACH * rows_here + jnp.arange(block_count * rows_here, dtype=jnp.int32)
     key_layout = layout_rows(key_rows, offsets, grids, row_count)
@@ -168,17 +203,26 @@
     attended_output = attend_blocks(
         query_matrix, kv_blocks, key_segment, key_inside, segment, inside
     )
-    projected = jnp.einsum(
-        "thf,hfc->tc",
-        attended_output,
-        lax.all_gather(w_out, "seq", axis=2, tiled=True),
-        preferred_element_type=jnp.float32,
-    )
-    head_share = lax.psum_scatter(
-        projected.astype(jnp.bfloat16), "tp", scatter_dimension=1, tiled=True
-    ).astype(jnp.float32)
+    proj_mine = jnp.einsum(
+        "thf,hfjd->tjd", attended_output, wo_mine, preferred_element_type=jnp.float32
+    ).astype(jnp.bfloat16)
+    proj_other = jnp.einsum(
+        "thf,hfjd->tjd", attended_output, wo_other, preferred_element_type=jnp.float32
+    ).astype(jnp.bfloat16)
+    first_half = jnp.where(c == 0, proj_mine, proj_other)
+    second_half = jnp.where(c == 0, proj_other, proj_mine)
+    share = jnp.stack([first_half, second_half], axis=2).reshape(rows_here, n_zh, n_x, -1)
+
+    total = lax.dynamic_index_in_dim(share, x, axis=2, keepdims=False).astype(jnp.float32)
+    for s in range(1, n_x):
+        outgoing = lax.dynamic_index_in_dim(share, (x + s) % n_x, axis=2, keepdims=False)
+        total = total + ring(outgoing, "x", n_x, s).astype(jnp.float32)
+    keep = lax.dynamic_index_in_dim(total, zh, axis=1, keepdims=False)
+    give = lax.dynamic_index_in_dim(total, 1 - zh, axis=1, keepdims=False)
+    head_share = keep + ring(give.astype(jnp.bfloat16), "zh", n_zh, 1).astype(jnp.float32)
+
     layer_out = (tokens.astype(jnp.float32) + layer_scale * head_share).astype(jnp.bfloat16)
-    next_rows = from_behind(layer_out[:HALO], "seq", -1)
+    next_rows = chain(layer_out[:HALO], SEQ, n_seq, -1)
     extended = jnp.concatenate([layer_out, next_rows], axis=0)
     is_corner = is_patch & (grid_row % 2 == 0) & (grid_col % 2 == 0)
     local_ids = jnp.arange(rows_here, dtype=jnp.int32)
@@ -191,16 +235,26 @@
 
 
 def solution(mesh):
+    n_seq, n_tp = mesh.devices.shape
+    n_c = 2
+    n_y = 4
+    n_zh = 2
+    sizes = (n_y, n_seq // (n_y * n_c), n_c, n_zh, n_tp // n_zh)
+    split = Mesh(mesh.devices.reshape(sizes), ("y", "zl", "c", "zh", "x"))
     placed = (
-        P("seq", "tp"),
-        P(),
-        P(),
-        P("seq", "tp", None, None),
-        P("tp", None, "seq"),
-        P("tp"),
+        P(SEQ, TP),
+        P(),
+        P(),
+        P(SEQ, TP, None, None),
+        P(TP, None, SEQ),
+        P(TP),
         P(),
         P(),
     )
     return jax.shard_map(
-        body, mesh=mesh, in_specs=placed, out_specs=P("seq", None, "tp"), check_vma=False
-    )
+        functools.partial(body, sizes),
+        mesh=split,
+        in_specs=placed,
+        out_specs=P(SEQ, None, TP),
+        check_vma=False,
+    )

time: 671 us -> 647 us (0.964)
  waiting for transfers between devices: 503 us -> 364 us
  starting transfers between devices: 59.1 us -> 140 us
  local copies, waits for them, and re-layouts: 54.2 us -> 78.6 us
    reduce_scatter x1 -> x0, waiting for transfers between devices: 142 us -> none  [body(): lax.psum_scatter(projected.astype(jnp.bfloat16), 'tp', scatter_dimension=...]
    ppermute x15 -> x25, starting transfers between devices: 58.9 us -> 140 us  [the longest x10 98.4 us: ring(): lax.ppermute(shard, axis, [(i, (i + by) % size) for i in range(size)])]
    all_gather x3 -> x2, waiting for transfers between devices: 243 us -> 316 us  [the longest x1 190 us: body(): wq_mine = lax.all_gather(w_qkv, ('y', 'zl'), axis=0, tiled=False)]
    ppermute x15 -> x25, waiting for transfers between devices: 116 us -> 48.1 us  [the longest x10 25.8 us: ring(): lax.ppermute(shard, axis, [(i, (i + by) % size) for i in range(size)])]
    unnamed x27 -> x35, local copies, waits for them, and re-layouts: 17.4 us -> 25.5 us
  transfers between devices with their start and end apart: 19 -> 27, of which waited for: 11 -> 15; matrix products, arithmetic and copies ran while one was open for 12% -> 17% of each run, Pallas kernels for 0% -> 0%
where the time goes in v1:
time: 647 us; the launch traced here: 642 us
  waiting for transfers between devices  364 us (56%)
  starting transfers between devices  140 us (22%)
  local copies, waits for them, and re-layouts  78.6 us (12%)
  other arithmetic  23.7 us (4%)
  matrix products  19.1 us (3%)
  between operations  14.3 us (2%)
    all_gather x1, waiting for transfers between devices, body(): wq_mine = lax.all_gather(w_qkv, ('y', 'zl'), axis=0, tiled=False)  190 us
    all_gather x1, waiting for transfers between devices, body(): wo_mine = lax.all_gather(w_out, ('y', 'zl'), axis=2, tiled=False)  125 us
    ppermute x10, starting transfers between devices, ring(): lax.ppermute(shard, axis, [(i, (i + by) % size) for i in range(size)])  98.4 us
    ppermute x15, starting transfers between devices, chain(): return lax.ppermute(shard, axis, pairs)  41.7 us
    squeeze x30, local copies, waits for them, and re-layouts, attend_blocks(): lax.scan(max_step, (start_max, start_total), (kv_blocks, key_segment, key...  29.3 us
    ppermute x10, waiting for transfers between devices, ring(): lax.ppermute(shard, axis, [(i, (i + by) % size) for i in range(size)])  25.8 us
    unnamed x35, local copies, waits for them, and re-layouts  25.5 us
    ppermute x15, waiting for transfers between devices, chain(): return lax.ppermute(shard, axis, pairs)  22.3 us
  transfers between devices with their start and end apart: 27, of which 15 were waited for; matrix products, arithmetic and copies ran while one was open for 17% of the time, Pallas kernels for 0%

profile of v1, /device:TPU:1, one launch (start us, length us, event | category | flops | bytes accessed | tf_op | source)
XLA Modules:
  0.0 641.6 jit_solution(7102759682695565062)
XLA Ops:
  7.3 16.3 %collective-permute-start = (bf16[256,512]{1,0:T(8,128)(2,1)}, bf16[256,512]{1,0:T(8,128)(2,1)S(1)}, u32[]{:S(2)}, u32[]{:S(2)}) collective-permute-start(bf16[256,512]{1,0:T(8,128)(2,1)} %param.12), channel_id=1, source_target_pairs={{0,4},{4,0},{1,5},{5,1},{2,6},{6,2},{3,7},{7,3},{8,12},{12,8},{9,1... | collective-permute-start | bytes 786440 | tf_op jit(solution)/shard_map/ppermute | solution.py:132
  30.2 3.8 collective-permute-start.1
  33.9 4.4 collective-permute-start.2
  41.4 190.2 %all-gather.5.cloned.1.call-done = bf16[2048,2,3,128]{3,1,2,0:T(2,128)(2,1)} async-done(((bf16[64,2,3,128]{3,1,2,0:T(2,128)(2,1)}), bf16[2048,2,3,128]{3,1,2,0:T(2,128)(2,1)}) %all-gather.5.cloned.1.call-update) | async-done | bytes 3145744 | tf_op jit(solution)/shard_map/all_gather | solution.py:151
  231.6 4.0 copy.79
  235.6 23.9 %collective-permute-start.4 = (bf16[32,64,2,3,128]{4,1,0,3,2:T(8,128)(2,1)}, bf16[32,64,2,3,128]{4,1,0,3,2:T(8,128)(2,1)}, u32[]{:S(2)}, u32[]{:S(2)}) collective-permute-start(bf16[32,64,2,3,128]{4,1,0,3,2:T(8,128)(2,1)} %bitcast), channel_id=1, source_target_pairs={{0,8},{8,0},{1,9},{9,1},{2,10},{10,2},{3,11},{11,3},{4,12},{12,4},... | collective-permute-start | bytes 9437192 | tf_op jit(solution)/shard_map/ppermute | solution.py:132
  268.7 5.3 copy.78
  289.7 4.4 collective-permute-start.6
  298.0 4.4 collective-permute-start.7
  306.1 4.0 collective-permute-start.8
  323.0 3.7 collective-permute-start.10
  327.0 125.3 %all-gather.7.cloned.1.call-done = bf16[2,128,2048]{1,2,0:T(8,128)(2,1)} async-done(((bf16[2,128,64]{1,2,0:T(8,128)(2,1)}), bf16[2,128,2048]{1,2,0:T(8,128)(2,1)}) %all-gather.7.cloned.1.call-update) | async-done | bytes 1048592 | tf_op jit(solution)/shard_map/all_gather | solution.py:152
  454.7 25.4 %collective-permute-start.19 = (bf16[2,128,32,64]{1,3,0,2:T(8,128)(2,1)}, bf16[2,128,32,64]{1,3,0,2:T(8,128)(2,1)S(1)}, u32[]{:S(2)}, u32[]{:S(2)}) collective-permute-start(bf16[2,128,32,64]{1,3,0,2:T(8,128)(2,1)} %copy.87), channel_id=1, source_target_pairs={{0,8},{8,0},{1,9},{9,1},{2,10},{10,2},{3,11},{11,3},{4,12},{12,4},... | collective-permute-start | bytes 3145736 | tf_op jit(solution)/shard_map/ppermute | solution.py:132
  485.8 5.0 collective-permute-done.17
  511.4 6.3 copy.84
  517.7 24.1 %while.24 = (s32[]{:T(128)}, f32[2,256,1]{1,0,2:T(2,128)S(1)}, f32[2,256,1]{1,0,2:T(2,128)S(1)}, pred[256]{0:T(512)(128)(4,1)S(1)}, pred[15,256]{1,0:T(8,128)(4,...) while((s32[]{:T(128)}, f32[2,256,1]{1,0,2:T(2,128)S(1)}, ...), condition=%wide.region_9.10_spmd.clone, body=%wide.region_6.9_spmd.clone.sunk | while | flops 34540032 | bytes 2063492 | solution.py:99
  541.8 26.0 %while.25 = (s32[]{:T(128)}, f32[256,2,128]{0,2,1:T(8,128)S(1)}, bf16[15,256,2,2,128]{4,1,3,2,0:T(8,128)(2,1)}, pred[256]{0:T(512)(128)(4,1)S(1)}, pred[15,256]{...) while((s32[]{:T(128)}, f32[256,2,128]{0,2,1:T(8,128)S(1)}, ...), condition=%wide.region_11.12_spmd.clone, body=%wide.region_10.11_spmd.clone.sunk | while | flops 68222976 | bytes 1582219 | solution.py:122
  572.7 4.2 collective-permute-start.21
  580.5 5.7 collective-permute-done.20
  586.2 6.5 %collective-permute-done.21 = bf16[256,2,512]{2,0,1:T(8,128)(2,1)} collective-permute-done((bf16[256,2,512]{2,0,1:T(8,128)(2,1)S(1)}, bf16[256,2,512]{2,0,1:T(8,128)(2,1)}, u32[]{:S(2)}, u32[]{:S(2)}) %collective-permute-start.21) | collective-permute-done | bytes 524320 | tf_op jit(solution)/shard_map/ppermute | solution.py:132
  596.6 11.4 %collective-permute-start.23 = (bf16[256,512]{1,0:T(8,128)(2,1)S(1)}, bf16[256,512]{1,0:T(8,128)(2,1)S(1)}, u32[]{:S(2)}, u32[]{:S(2)}) collective-permute-start(bf16[256,512]{1,0:T(8,128)(2,1)S(1)} %fusion.33), channel_id=1, source_target_pairs={{0,4},{4,0},{1,5},{5,1},{2,6},{6,2},{3,7},{7,3},{8,12},{12,8},{9,1... | collective-permute-start | bytes 786440 | tf_op jit(solution)/shard_map/ppermute | solution.py:132
  608.4 9.8 %collective-permute-done.23 = bf16[256,512]{1,0:T(8,128)(2,1)S(1)} collective-permute-done((bf16[256,512]{1,0:T(8,128)(2,1)S(1)}, bf16[256,512]{1,0:T(8,128)(2,1)S(1)}, u32[]{:S(2)}, u32[]{:S(2)}) %collective-permute-start.23) | collective-permute-done | bytes 262176 | tf_op jit(solution)/shard_map/ppermute | solution.py:132
  620.5 7.2 %collective-permute-done.24 = bf16[48,512]{1,0:T(8,128)(2,1)S(1)} collective-permute-done((bf16[48,512]{1,0:T(8,128)(2,1)S(1)}, bf16[48,512]{1,0:T(8,128)(2,1)S(1)}, u32[]{:S(2)}, u32[]{:S(2)}) %collective-permute-start.24) | collective-permute-done | bytes 49184 | tf_op jit(solution)/shard_map/ppermute | solution.py:137
  627.7 4.0 gather_fusion.1
  (350 shorter events, 150.7 us)
Async XLA Ops:
  6.5 225.1 %all-gather.5.cloned.1.call-start = ((), (), s32[]{:S(2)}) async-start(), calls=%async_computation | async-start | bytes 3244032 | tf_op jit(solution)/shard_map/all_gather | solution.py:151
  7.3 445.1 %all-gather.7.cloned.1.call-start = ((), (), s32[]{:S(2)}) async-start(), calls=%async_computation.1 | async-start | bytes 1081344 | tf_op jit(solution)/shard_map/all_gather | solution.py:152
  7.3 21.8 %collective-permute-start = (bf16[256,512]{1,0:T(8,128)(2,1)}, bf16[256,512]{1,0:T(8,128)(2,1)S(1)}, u32[]{:S(2)}, u32[]{:S(2)}) collective-permute-start(bf16[256,512]{1,0:T(8,128)(2,1)} %param.12), channel_id=1, source_target_pairs={{0,4},{4,0},{1,5},{5,1},{2,6},{6,2},{3,7},{7,3},{8,12},{12,8},{9,1... | collective-permute-start | bytes 786440 | tf_op jit(solution)/shard_map/ppermute | solution.py:132
  30.2 229.7 %collective-permute-start.1 = (bf16[2,256,512]{2,1,0:T(8,128)(2,1)S(1)}, bf16[2,256,512]{2,1,0:T(8,128)(2,1)S(1)}, u32[]{:S(2)}, u32[]{:S(2)}) collective-permute-start(bf16[2,256,512]{2,1,0:T(8,128)(2,1)S(1)} %get-tuple-element.322), channel_id=1, source_target_pairs={{0,1},{1,2},{2,3},{3,0},{4,5},{5,6},{6,7},{7,4},{8,9},{9,10},{10,1... | collective-permute-start | bytes 1572872 | tf_op jit(solution)/shard_map/ppermute | solution.py:132
  33.9 225.9 %collective-permute-start.2 = (bf16[2,256,512]{2,1,0:T(8,128)(2,1)S(1)}, bf16[2,256,512]{2,1,0:T(8,128)(2,1)S(1)}, u32[]{:S(2)}, u32[]{:S(2)}) collective-permute-start(bf16[2,256,512]{2,1,0:T(8,128)(2,1)S(1)} %get-tuple-element.322), channel_id=1, source_target_pairs={{0,2},{1,3},{2,0},{3,1},{4,6},{5,7},{6,4},{7,5},{8,10},{9,11},{10,... | collective-permute-start | bytes 1572872 | tf_op jit(solution)/shard_map/ppermute | solution.py:132
  38.3 221.6 %collective-permute-start.3 = (bf16[2,256,512]{2,1,0:T(8,128)(2,1)S(1)}, bf16[2,256,512]{2,1,0:T(8,128)(2,1)S(1)}, u32[]{:S(2)}, u32[]{:S(2)}) collective-permute-start(bf16[2,256,512]{2,1,0:T(8,128)(2,1)S(1)} %get-tuple-element.322), channel_id=1, source_target_pairs={{0,3},{1,0},{2,1},{3,2},{4,7},{5,4},{6,5},{7,6},{8,11},{9,8},{10,9... | collective-permute-start | bytes 1572872 | tf_op jit(solution)/shard_map/ppermute | solution.py:132
  235.6 45.3 %collective-permute-start.4 = (bf16[32,64,2,3,128]{4,1,0,3,2:T(8,128)(2,1)}, bf16[32,64,2,3,128]{4,1,0,3,2:T(8,128)(2,1)}, u32[]{:S(2)}, u32[]{:S(2)}) collective-permute-start(bf16[32,64,2,3,128]{4,1,0,3,2:T(8,128)(2,1)} %bitcast), channel_id=1, source_target_pairs={{0,8},{8,0},{1,9},{9,1},{2,10},{10,2},{3,11},{11,3},{4,12},{12,4},... | collective-permute-start | bytes 9437192 | tf_op jit(solution)/shard_map/ppermute | solution.py:132
  286.3 8.6 %collective-permute-start.12 = (bf16[256,2,2,128]{0,3,2,1:T(8,128)(2,1)S(1)}, bf16[256,2,2,128]{0,3,2,1:T(8,128)(2,1)S(1)}, u32[]{:S(2)}, u32[]{:S(2)}) collective-permute-start(bf16[256,2,2,128]{0,3,2,1:T(8,128)(2,1)S(1)} %pad_maximum_fusion.4), channel_id=1, source_target_pairs={{8,0},{16,8},{24,16},{32,24},{40,32},{48,40},{56,48},{64,56},{72,6... | collective-permute-start | bytes 786440 | tf_op jit(solution)/shard_map/ppermute | solution.py:137
  294.9 9.2 %collective-permute-start.13 = (bf16[256,2,2,128]{0,3,2,1:T(8,128)(2,1)S(1)}, bf16[256,2,2,128]{0,3,2,1:T(8,128)(2,1)S(1)}, u32[]{:S(2)}, u32[]{:S(2)}) collective-permute-start(bf16[256,2,2,128]{0,3,2,1:T(8,128)(2,1)S(1)} %collective-permute-done.12), channel_id=1, source_target_pairs={{8,0},{16,8},{24,16},{32,24},{40,32},{48,40},{56,48},{64,56},{72,6... | collective-permute-start | bytes 786440 | tf_op jit(solution)/shard_map/ppermute | solution.py:137
  304.2 8.5 %collective-permute-start.14 = (bf16[256,2,2,128]{0,3,2,1:T(8,128)(2,1)S(1)}, bf16[256,2,2,128]{0,3,2,1:T(8,128)(2,1)S(1)}, u32[]{:S(2)}, u32[]{:S(2)}) collective-permute-start(bf16[256,2,2,128]{0,3,2,1:T(8,128)(2,1)S(1)} %collective-permute-done.13), channel_id=1, source_target_pairs={{8,0},{16,8},{24,16},{32,24},{40,32},{48,40},{56,48},{64,56},{72,6... | collective-permute-start | bytes 786440 | tf_op jit(solution)/shard_map/ppermute | solution.py:137
  306.1 8.5 %collective-permute-start.8 = (bf16[256,2,2,128]{0,3,2,1:T(8,128)(2,1)S(1)}, bf16[256,2,2,128]{0,3,2,1:T(8,128)(2,1)S(1)}, u32[]{:S(2)}, u32[]{:S(2)}) collective-permute-start(bf16[256,2,2,128]{0,3,2,1:T(8,128)(2,1)S(1)} %collective-permute-done.7), channel_id=1, source_target_pairs={{0,8},{8,16},{16,24},{24,32},{32,40},{40,48},{48,56},{56,64},{64,7... | collective-permute-start | bytes 786440 | tf_op jit(solution)/shard_map/ppermute | solution.py:137
  312.6 8.5 %collective-permute-start.15 = (bf16[256,2,2,128]{0,3,2,1:T(8,128)(2,1)S(1)}, bf16[256,2,2,128]{0,3,2,1:T(8,128)(2,1)}, u32[]{:S(2)}, u32[]{:S(2)}) collective-permute-start(bf16[256,2,2,128]{0,3,2,1:T(8,128)(2,1)S(1)} %collective-permute-done.14), channel_id=1, source_target_pairs={{8,0},{16,8},{24,16},{32,24},{40,32},{48,40},{56,48},{64,56},{72,6... | collective-permute-start | bytes 786440 | tf_op jit(solution)/shard_map/ppermute | solution.py:137
  314.6 8.5 %collective-permute-start.9 = (bf16[256,2,2,128]{0,3,2,1:T(8,128)(2,1)S(1)}, bf16[256,2,2,128]{0,3,2,1:T(8,128)(2,1)}, u32[]{:S(2)}, u32[]{:S(2)}) collective-permute-start(bf16[256,2,2,128]{0,3,2,1:T(8,128)(2,1)S(1)} %collective-permute-done.8), channel_id=1, source_target_pairs={{0,8},{8,16},{16,24},{24,32},{32,40},{40,48},{48,56},{56,64},{64,7... | collective-permute-start | bytes 786440 | tf_op jit(solution)/shard_map/ppermute | solution.py:137
  321.1 158.9 %collective-permute-start.16 = (bf16[256,2,2,128]{0,3,2,1:T(8,128)(2,1)}, bf16[256,2,2,128]{0,3,2,1:T(8,128)(2,1)}, u32[]{:S(2)}, u32[]{:S(2)}) collective-permute-start(bf16[256,2,2,128]{0,3,2,1:T(8,128)(2,1)} %collective-permute-done.15), channel_id=1, source_target_pairs={{8,0},{16,8},{24,16},{32,24},{40,32},{48,40},{56,48},{64,56},{72,6... | collective-permute-start | bytes 786440 | tf_op jit(solution)/shard_map/ppermute | solution.py:137
  323.0 158.9 %collective-permute-start.10 = (bf16[256,2,2,128]{0,3,2,1:T(8,128)(2,1)}, bf16[256,2,2,128]{0,3,2,1:T(8,128)(2,1)}, u32[]{:S(2)}, u32[]{:S(2)}) collective-permute-start(bf16[256,2,2,128]{0,3,2,1:T(8,128)(2,1)} %collective-permute-done.9), channel_id=1, source_target_pairs={{0,8},{8,16},{16,24},{24,32},{32,40},{40,48},{48,56},{56,64},{64,7... | collective-permute-start | bytes 786440 | tf_op jit(solution)/shard_map/ppermute | solution.py:137
  454.7 113.6 %collective-permute-start.19 = (bf16[2,128,32,64]{1,3,0,2:T(8,128)(2,1)}, bf16[2,128,32,64]{1,3,0,2:T(8,128)(2,1)S(1)}, u32[]{:S(2)}, u32[]{:S(2)}) collective-permute-start(bf16[2,128,32,64]{1,3,0,2:T(8,128)(2,1)} %copy.87), channel_id=1, source_target_pairs={{0,8},{8,0},{1,9},{9,1},{2,10},{10,2},{3,11},{11,3},{4,12},{12,4},... | collective-permute-start | bytes 3145736 | tf_op jit(solution)/shard_map/ppermute | solution.py:132
  480.0 10.8 %collective-permute-start.17 = (bf16[256,2,2,128]{0,3,2,1:T(8,128)(2,1)}, bf16[256,2,2,128]{0,3,2,1:T(8,128)(2,1)}, u32[]{:S(2)}, u32[]{:S(2)}) collective-permute-start(bf16[256,2,2,128]{0,3,2,1:T(8,128)(2,1)} %collective-permute-done.16), channel_id=1, source_target_pairs={{8,0},{16,8},{24,16},{32,24},{40,32},{48,40},{56,48},{64,56},{72,6... | collective-permute-start | bytes 786440 | tf_op jit(solution)/shard_map/ppermute | solution.py:137
  482.0 11.0 %collective-permute-start.11 = (bf16[256,2,2,128]{0,3,2,1:T(8,128)(2,1)}, bf16[256,2,2,128]{0,3,2,1:T(8,128)(2,1)}, u32[]{:S(2)}, u32[]{:S(2)}) collective-permute-start(bf16[256,2,2,128]{0,3,2,1:T(8,128)(2,1)} %collective-permute-done.10), channel_id=1, source_target_pairs={{0,8},{8,16},{16,24},{24,32},{32,40},{40,48},{48,56},{56,64},{64,7... | collective-permute-start | bytes 786440 | tf_op jit(solution)/shard_map/ppermute | solution.py:137
  490.9 19.8 %collective-permute-start.18 = (bf16[256,2,2,128]{0,3,2,1:T(8,128)(2,1)}, bf16[256,2,2,128]{0,3,2,1:T(8,128)(2,1)S(1)}, u32[]{:S(2)}, u32[]{:S(2)}) collective-permute-start(bf16[256,2,2,128]{0,3,2,1:T(8,128)(2,1)} %collective-permute-done.17), channel_id=1, source_target_pairs={{8,0},{16,8},{24,16},{32,24},{40,32},{48,40},{56,48},{64,56},{72,6... | collective-permute-start | bytes 786440 | tf_op jit(solution)/shard_map/ppermute | solution.py:137
  569.6 16.6 %collective-permute-start.20 = (bf16[256,2,512]{2,0,1:T(8,128)(2,1)S(1)}, bf16[256,2,512]{2,0,1:T(8,128)(2,1)}, u32[]{:S(2)}, u32[]{:S(2)}) collective-permute-start(bf16[256,2,512]{2,0,1:T(8,128)(2,1)S(1)} %bitcast.233), channel_id=1, source_target_pairs={{0,1},{1,2},{2,3},{3,0},{4,5},{5,6},{6,7},{7,4},{8,9},{9,10},{10,1... | collective-permute-start | bytes 1572872 | tf_op jit(solution)/shard_map/ppermute | solution.py:132
  572.7 19.9 %collective-permute-start.21 = (bf16[256,2,512]{2,0,1:T(8,128)(2,1)S(1)}, bf16[256,2,512]{2,0,1:T(8,128)(2,1)}, u32[]{:S(2)}, u32[]{:S(2)}) collective-permute-start(bf16[256,2,512]{2,0,1:T(8,128)(2,1)S(1)} %bitcast.234), channel_id=1, source_target_pairs={{0,2},{1,3},{2,0},{3,1},{4,6},{5,7},{6,4},{7,5},{8,10},{9,11},{10,... | collective-permute-start | bytes 1572872 | tf_op jit(solution)/shard_map/ppermute | solution.py:132
  577.2 17.8 %collective-permute-start.22 = (bf16[256,2,512]{2,0,1:T(8,128)(2,1)S(1)}, bf16[256,2,512]{2,0,1:T(8,128)(2,1)}, u32[]{:S(2)}, u32[]{:S(2)}) collective-permute-start(bf16[256,2,512]{2,0,1:T(8,128)(2,1)S(1)} %bitcast.235), channel_id=1, source_target_pairs={{0,3},{1,0},{2,1},{3,2},{4,7},{5,4},{6,5},{7,6},{8,11},{9,8},{10,9... | collective-permute-start | bytes 1572872 | tf_op jit(solution)/shard_map/ppermute | solution.py:132
  596.6 21.6 %collective-permute-start.23 = (bf16[256,512]{1,0:T(8,128)(2,1)S(1)}, bf16[256,512]{1,0:T(8,128)(2,1)S(1)}, u32[]{:S(2)}, u32[]{:S(2)}) collective-permute-start(bf16[256,512]{1,0:T(8,128)(2,1)S(1)} %fusion.33), channel_id=1, source_target_pairs={{0,4},{4,0},{1,5},{5,1},{2,6},{6,2},{3,7},{7,3},{8,12},{12,8},{9,1... | collective-permute-start | bytes 786440 | tf_op jit(solution)/shard_map/ppermute | solution.py:132
  618.4 9.3 %collective-permute-start.24 = (bf16[48,512]{1,0:T(8,128)(2,1)S(1)}, bf16[48,512]{1,0:T(8,128)(2,1)S(1)}, u32[]{:S(2)}, u32[]{:S(2)}) collective-permute-start(bf16[48,512]{1,0:T(8,128)(2,1)S(1)} %slice.100), channel_id=1, source_target_pairs={{8,0},{16,8},{24,16},{32,24},{40,32},{48,40},{56,48},{64,56},{72,6... | collective-permute-start | bytes 147464 | tf_op jit(solution)/shard_map/ppermute | solution.py:137
  (12 other events, 312.3 us)
Sparse Core Ops, SparseCore 0:
  9.4 222.1 all-gather.4
  233.7 218.6 all-gather.6

commit v2 on v1

--- a/solution.py
+++ b/solution.py
@@ -137,6 +137,23 @@
     return lax.ppermute(shard, axis, pairs)
 
 
+def gather_seq_blocks(local, n_y, n_zl):
+    zl = lax.axis_index("zl")
+    y = lax.axis_index("y")
+    left, right = local, local
+    lefts, rights = [], []
+    for _ in range(1, n_zl):
+        left = chain(left, "zl", n_zl, 1)
+        right = chain(right, "zl", n_zl, -1)
+        lefts.append(left)
+        rights.append(right)
+    every = jnp.stack(lefts[::-1] + [local] + rights)
+    line = lax.dynamic_slice_in_dim(every, n_zl - 1 - zl, n_zl, axis=0)
+    by_shift = jnp.stack([line] + [ring(line, "y", n_y, s) for s in range(1, n_y)])
+    by_y = jnp.take(by_shift, (y - jnp.arange(n_y)) % n_y, axis=0)
+    return by_y.reshape(n_y * n_zl, *local.shape)
+
+
 def body(sizes, tokens, ln_gain, ln_bias, w_qkv, w_out, layer_scale, grids, offsets):
     n_y, n_zl, n_c, n_zh, n_x = sizes
     n_seq = n_y * n_zl * n_c
@@ -148,8 +165,8 @@
     seq_index = (lax.axis_index("y") * n_zl + lax.axis_index("zl")) * n_c + c
     first_row = seq_index * rows_here
 
-    wq_mine = lax.all_gather(w_qkv, ("y", "zl"), axis=0, tiled=False)
-    wo_mine = lax.all_gather(w_out, ("y", "zl"), axis=2, tiled=False)
+    wq_mine = gather_seq_blocks(w_qkv, n_y, n_zl)
+    wo_mine = jnp.transpose(gather_seq_blocks(w_out, n_y, n_zl), (1, 2, 0, 3))
     wq_other = ring(wq_mine, "c", n_c, 1)
     wo_other = ring(wo_mine, "c", n_c, 1)
 

time: 647 us -> 492 us (0.76)
  the two profiles are of different devices: /device:TPU:1 before, /device:TPU:15 now
where the time goes in v2:
time: 492 us; the launch traced here: 487 us
  starting transfers between devices  235 us (48%)
  local copies, waits for them, and re-layouts  117 us (24%)
  waiting for transfers between devices  76 us (15%)
  other arithmetic  36 us (7%)
  matrix products  19.1 us (4%)
    ppermute x43, starting transfers between devices, chain(): return lax.ppermute(shard, axis, pairs)  170 us
    ppermute x16, starting transfers between devices, ring(): lax.ppermute(shard, axis, [(i, (i + by) % size) for i in range(size)])  65 us
    ppermute x16, waiting for transfers between devices, ring(): lax.ppermute(shard, axis, [(i, (i + by) % size) for i in range(size)])  47.7 us
    unnamed x133, local copies, waits for them, and re-layouts  34 us
    squeeze x30, local copies, waits for them, and re-layouts, attend_blocks(): lax.scan(max_step, (start_max, start_total), (kv_blocks, key_segment, key...  29.2 us
    ppermute x43, waiting for transfers between devices, chain(): return lax.ppermute(shard, axis, pairs)  28.3 us
    dynamic_slice x60, local copies, waits for them, and re-layouts, attend_blocks(): lax.scan(max_step, (start_max, start_total), (kv_blocks, key_segment, key...  22 us
    gather x3, local copies, waits for them, and re-layouts, gather_seq_blocks(): by_y = jnp.take(by_shift, (y - jnp.arange(n_y)) % n_y, axis=0)  11.5 us
  transfers between devices with their start and end apart: 59, of which 11 were waited for; matrix products, arithmetic and copies ran while one was open for 33% of the time, Pallas kernels for 0%

profile of v2, /device:TPU:15, one launch (start us, length us, event | category | flops | bytes accessed | tf_op | source)
XLA Modules:
  0.0 486.9 jit_solution(12145209185940876636)
XLA Ops:
  10.5 14.4 %collective-permute-start = (bf16[256,512]{1,0:T(8,128)(2,1)}, bf16[256,512]{1,0:T(8,128)(2,1)S(1)}, u32[]{:S(2)}, u32[]{:S(2)}) collective-permute-start(bf16[256,512]{1,0:T(8,128)(2,1)} %param.12), channel_id=1, source_target_pairs={{0,4},{4,0},{1,5},{5,1},{2,6},{6,2},{3,7},{7,3},{8,12},{12,8},{9,1... | collective-permute-start | bytes 786440 | tf_op jit(solution)/shard_map/ppermute | solution.py:132
  33.0 15.5 %collective-permute-done.37 = bf16[2,128,64]{1,2,0:T(8,128)(2,1)S(1)} collective-permute-done((bf16[2,128,64]{1,2,0:T(8,128)(2,1)S(1)}, bf16[2,128,64]{1,2,0:T(8,128)(2,1)S(1)}, u32[]{:S(2)}, u32[]{:S(2)}) %collective-permute-start.37) | collective-permute-done | bytes 32800 | tf_op jit(solution)/shard_map/ppermute | solution.py:137
  69.9 5.8 %collective-permute-start.41 = (bf16[2,128,64]{1,2,0:T(8,128)(2,1)S(1)}, bf16[2,128,64]{1,2,0:T(8,128)(2,1)S(1)}, u32[]{:S(2)}, u32[]{:S(2)}) collective-permute-start(bf16[2,128,64]{1,2,0:T(8,128)(2,1)S(1)} %collective-permute-done.40), channel_id=1, source_target_pairs={{0,16},{16,32},{32,48},{48,64},{64,80},{80,96},{96,112},{1,17},{17... | collective-permute-start | bytes 98312 | tf_op jit(solution)/shard_map/ppermute | solution.py:137
  75.7 4.6 collective-permute-start.6
  83.0 4.6 collective-permute-start.42
  97.7 4.6 collective-permute-start.8
  104.3 5.2 %collective-permute-start.9 = (bf16[64,2,3,128]{3,1,2,0:T(2,128)(2,1)S(1)}, bf16[64,2,3,128]{3,1,2,0:T(2,128)(2,1)S(1)}, u32[]{:S(2)}, u32[]{:S(2)}) collective-permute-start(bf16[64,2,3,128]{3,1,2,0:T(2,128)(2,1)S(1)} %collective-permute-done.8), channel_id=1, source_target_pairs={{0,16},{16,32},{32,48},{48,64},{64,80},{80,96},{96,112},{1,17},{17... | collective-permute-start | bytes 294920 | tf_op jit(solution)/shard_map/ppermute | solution.py:137
  144.6 21.7 %collective-permute-done.20 = bf16[8,64,2,3,128]{4,2,3,1,0:T(2,128)(2,1)S(1)} collective-permute-done((bf16[8,64,2,3,128]{4,2,3,1,0:T(2,128)(2,1)S(1)}, bf16[8,64,2,3,128]{4,2,3,1,0:T(2,128)(2,1)S(1)}, u32[]{:S(2)}, u32[]{:S(2)}) %collective-permute-start.20) | collective-permute-done | bytes 786464 | tf_op jit(solution)/shard_map/ppermute | solution.py:132
  166.2 5.8 %pad_maximum_fusion = bf16[4,8,64,2,3,128]{5,3,4,2,1,0:T(2,128)(2,1)S(1)} fusion(bf16[1,8,64,2,3,128]{5,3,4,2,1,0:T(2,128)(2,1)S(1)} %bitcast.307, bf16[1,8,64,2,3,128]{5,3,4,2,1,0:T(2,128)(2,1)S(1)} %bitcast.306, bf16[1,8,64,2,3,128]{5,3,4,2,1,0:T(2,128)(2,1)S(1)} %bitcast.305, bf16[1,8,64,2,3,128]{5,3,4,2,1,0:T(2,128)(2,1)S(1)} %fusion.81), kind=kLoop, calls=%fused_computation.49 | loop fusion | flops 4718592 | bytes 6291456 | tf_op jit(solution)/shard_map/stack | solution.py:152
  172.0 7.9 %gather_fusion.1 = bf16[4,8,64,2,3,128]{5,3,4,2,1,0:T(2,128)(2,1)} fusion(bf16[4,8,64,2,3,128]{5,3,4,2,1,0:T(2,128)(2,1)S(1)} %pad_maximum_fusion, s32[1024]{0:T(1024)S(1)} %pad_clamp_fusion), kind=kCustom, calls=%fused_computation.1 | custom fusion | bytes 6291472 | tf_op jit(solution)/shard_map/jit(_take)/gather | solution.py:153
  195.4 5.3 %copy.53 = f32[256,2,4,512]{0,3,2,1:T(8,128)} copy(f32[256,2,4,512]{3,0,1,2:T(8,128)} %convert_bitcast_fusion) | data formatting | bytes 8388608 | tf_op jit(solution)/shard_map/convert_element_type | solution.py:181
  212.0 4.6 collective-permute-start.22
  224.6 9.0 %collective-permute-start.30 = (bf16[256,2,2,128]{0,3,2,1:T(8,128)(2,1)S(1)}, bf16[256,2,2,128]{0,3,2,1:T(8,128)(2,1)S(1)}, u32[]{:S(2)}, u32[]{:S(2)}) collective-permute-start(bf16[256,2,2,128]{0,3,2,1:T(8,128)(2,1)S(1)} %collective-permute-done.29), channel_id=1, source_target_pairs={{8,0},{16,8},{24,16},{32,24},{40,32},{48,40},{56,48},{64,56},{72,6... | collective-permute-start | bytes 786440 | tf_op jit(solution)/shard_map/ppermute | solution.py:137
  236.3 13.3 %collective-permute-start.31 = (bf16[256,2,2,128]{0,3,2,1:T(8,128)(2,1)S(1)}, bf16[256,2,2,128]{0,3,2,1:T(8,128)(2,1)S(1)}, u32[]{:S(2)}, u32[]{:S(2)}) collective-permute-start(bf16[256,2,2,128]{0,3,2,1:T(8,128)(2,1)S(1)} %collective-permute-done.30), channel_id=1, source_target_pairs={{8,0},{16,8},{24,16},{32,24},{40,32},{48,40},{56,48},{64,56},{72,6... | collective-permute-start | bytes 786440 | tf_op jit(solution)/shard_map/ppermute | solution.py:137
  260.8 13.1 %collective-permute-start.32 = (bf16[256,2,2,128]{0,3,2,1:T(8,128)(2,1)S(1)}, bf16[256,2,2,128]{0,3,2,1:T(8,128)(2,1)}, u32[]{:S(2)}, u32[]{:S(2)}) collective-permute-start(bf16[256,2,2,128]{0,3,2,1:T(8,128)(2,1)S(1)} %collective-permute-done.31), channel_id=1, source_target_pairs={{8,0},{16,8},{24,16},{32,24},{40,32},{48,40},{56,48},{64,56},{72,6... | collective-permute-start | bytes 786440 | tf_op jit(solution)/shard_map/ppermute | solution.py:137
  279.7 11.2 %collective-permute-start.33 = (bf16[256,2,2,128]{0,3,2,1:T(8,128)(2,1)}, bf16[256,2,2,128]{0,3,2,1:T(8,128)(2,1)}, u32[]{:S(2)}, u32[]{:S(2)}) collective-permute-start(bf16[256,2,2,128]{0,3,2,1:T(8,128)(2,1)} %collective-permute-done.32), channel_id=1, source_target_pairs={{8,0},{16,8},{24,16},{32,24},{40,32},{48,40},{56,48},{64,56},{72,6... | collective-permute-start | bytes 786440 | tf_op jit(solution)/shard_map/ppermute | solution.py:137
  293.0 11.3 %collective-permute-start.53 = (bf16[2,128,32,64]{1,3,0,2:T(8,128)(2,1)S(1)}, bf16[2,128,32,64]{1,3,0,2:T(8,128)(2,1)S(1)}, u32[]{:S(2)}, u32[]{:S(2)}) collective-permute-start(bf16[2,128,32,64]{1,3,0,2:T(8,128)(2,1)S(1)} %bitcast.301), channel_id=1, source_target_pairs={{0,8},{8,0},{1,9},{9,1},{2,10},{10,2},{3,11},{11,3},{4,12},{12,4},... | collective-permute-start | bytes 3145736 | tf_op jit(solution)/shard_map/ppermute | solution.py:132
  315.2 6.7 %collective-permute-start.35 = (bf16[256,2,2,128]{0,3,2,1:T(8,128)(2,1)}, bf16[256,2,2,128]{0,3,2,1:T(8,128)(2,1)S(1)}, u32[]{:S(2)}, u32[]{:S(2)}) collective-permute-start(bf16[256,2,2,128]{0,3,2,1:T(8,128)(2,1)} %collective-permute-done.34), channel_id=1, source_target_pairs={{8,0},{16,8},{24,16},{32,24},{40,32},{48,40},{56,48},{64,56},{72,6... | collective-permute-start | bytes 786440 | tf_op jit(solution)/shard_map/ppermute | solution.py:137
  343.1 6.3 %copy.59 = bf16[15,256,2,2,128]{4,1,3,2,0:T(8,128)(2,1)} copy(bf16[15,256,2,2,128]{1,4,3,2,0:T(8,128)(2,1)} %bitcast_dynamic-update-slice_fusion) | data formatting | bytes 7864320
  349.4 34.4 %while.24 = (s32[]{:T(128)}, f32[2,256,1]{1,0,2:T(2,128)S(1)}, f32[2,256,1]{1,0,2:T(2,128)S(1)}, pred[256]{0:T(512)(128)(4,1)S(1)}, pred[15,256]{1,0:T(8,128)(4,...) while((s32[]{:T(128)}, f32[2,256,1]{1,0,2:T(2,128)S(1)}, ...), condition=%wide.region_9.10_spmd.clone, body=%wide.region_6.9_spmd.clone.sunk | while | flops 34540032 | bytes 2063492 | solution.py:99
  383.9 36.2 %while.25 = (s32[]{:T(128)}, f32[256,2,128]{0,2,1:T(8,128)S(1)}, bf16[15,256,2,2,128]{4,1,3,2,0:T(8,128)(2,1)}, pred[256]{0:T(512)(128)(4,1)S(1)}, pred[15,256]{...) while((s32[]{:T(128)}, f32[256,2,128]{0,2,1:T(8,128)S(1)}, ...), condition=%wide.region_11.12_spmd.clone, body=%wide.region_10.11_spmd.clone.sunk | while | flops 68222976 | bytes 1582219 | solution.py:122
  437.6 6.9 %collective-permute-done.56 = bf16[256,2,512]{2,0,1:T(8,128)(2,1)} collective-permute-done((bf16[256,2,512]{2,0,1:T(8,128)(2,1)}, bf16[256,2,512]{2,0,1:T(8,128)(2,1)}, u32[]{:S(2)}, u32[]{:S(2)}) %collective-permute-start.56) | collective-permute-done | bytes 524320 | tf_op jit(solution)/shard_map/ppermute | solution.py:132
  448.4 13.6 %collective-permute-done.57 = bf16[256,512]{1,0:T(8,128)(2,1)S(1)} collective-permute-done((bf16[256,512]{1,0:T(8,128)(2,1)S(1)}, bf16[256,512]{1,0:T(8,128)(2,1)S(1)}, u32[]{:S(2)}, u32[]{:S(2)}) %collective-permute-start.57) | collective-permute-done | bytes 262176 | tf_op jit(solution)/shard_map/ppermute | solution.py:132
  462.1 13.6 %collective-permute-start.58 = (bf16[48,512]{1,0:T(8,128)(2,1)S(1)}, bf16[48,512]{1,0:T(8,128)(2,1)S(1)}, u32[]{:S(2)}, u32[]{:S(2)}) collective-permute-start(bf16[48,512]{1,0:T(8,128)(2,1)S(1)} %slice.104), channel_id=1, source_target_pairs={{8,0},{16,8},{24,16},{32,24},{40,32},{48,40},{56,48},{64,56},{72,6... | collective-permute-start | bytes 147464 | tf_op jit(solution)/shard_map/ppermute | solution.py:137
  (525 shorter events, 278.8 us)
Async XLA Ops:
  0.0 59.4 %collective-permute-start.4 = (bf16[64,2,3,128]{3,1,2,0:T(2,128)(2,1)}, bf16[64,2,3,128]{3,1,2,0:T(2,128)(2,1)S(1)}, u32[]{:S(2)}, u32[]{:S(2)}) collective-permute-start(bf16[64,2,3,128]{3,1,2,0:T(2,128)(2,1)} %param.15), channel_id=1, source_target_pairs={{0,16},{16,32},{32,48},{48,64},{64,80},{80,96},{96,112},{1,17},{17... | collective-permute-start | bytes 294920 | tf_op jit(solution)/shard_map/ppermute | solution.py:137
  3.7 63.5 %collective-permute-start.11 = (bf16[64,2,3,128]{3,1,2,0:T(2,128)(2,1)}, bf16[64,2,3,128]{3,1,2,0:T(2,128)(2,1)S(1)}, u32[]{:S(2)}, u32[]{:S(2)}) collective-permute-start(bf16[64,2,3,128]{3,1,2,0:T(2,128)(2,1)} %param.15), channel_id=1, source_target_pairs={{16,0},{32,16},{48,32},{64,48},{80,64},{96,80},{112,96},{17,1},{33... | collective-permute-start | bytes 294920 | tf_op jit(solution)/shard_map/ppermute | solution.py:137
  5.0 22.6 %collective-permute-start.36 = (bf16[2,128,64]{1,2,0:T(8,128)(2,1)}, bf16[2,128,64]{1,2,0:T(8,128)(2,1)S(1)}, u32[]{:S(2)}, u32[]{:S(2)}) collective-permute-start(bf16[2,128,64]{1,2,0:T(8,128)(2,1)} %param.16), channel_id=1, source_target_pairs={{0,16},{16,32},{32,48},{48,64},{64,80},{80,96},{96,112},{1,17},{17... | collective-permute-start | bytes 98312 | tf_op jit(solution)/shard_map/ppermute | solution.py:137
  9.2 22.5 %collective-permute-start.43 = (bf16[2,128,64]{1,2,0:T(8,128)(2,1)}, bf16[2,128,64]{1,2,0:T(8,128)(2,1)S(1)}, u32[]{:S(2)}, u32[]{:S(2)}) collective-permute-start(bf16[2,128,64]{1,2,0:T(8,128)(2,1)} %param.16), channel_id=1, source_target_pairs={{16,0},{32,16},{48,32},{64,48},{80,64},{96,80},{112,96},{17,1},{33... | collective-permute-start | bytes 98312 | tf_op jit(solution)/shard_map/ppermute | solution.py:137
  10.5 124.4 %collective-permute-start = (bf16[256,512]{1,0:T(8,128)(2,1)}, bf16[256,512]{1,0:T(8,128)(2,1)S(1)}, u32[]{:S(2)}, u32[]{:S(2)}) collective-permute-start(bf16[256,512]{1,0:T(8,128)(2,1)} %param.12), channel_id=1, source_target_pairs={{0,4},{4,0},{1,5},{5,1},{2,6},{6,2},{3,7},{7,3},{8,12},{12,8},{9,1... | collective-permute-start | bytes 786440 | tf_op jit(solution)/shard_map/ppermute | solution.py:132
  27.6 20.9 %collective-permute-start.37 = (bf16[2,128,64]{1,2,0:T(8,128)(2,1)S(1)}, bf16[2,128,64]{1,2,0:T(8,128)(2,1)S(1)}, u32[]{:S(2)}, u32[]{:S(2)}) collective-permute-start(bf16[2,128,64]{1,2,0:T(8,128)(2,1)S(1)} %collective-permute-done.36), channel_id=1, source_target_pairs={{0,16},{16,32},{32,48},{48,64},{64,80},{80,96},{96,112},{1,17},{17... | collective-permute-start | bytes 98312 | tf_op jit(solution)/shard_map/ppermute | solution.py:137
  31.7 21.0 %collective-permute-start.44 = (bf16[2,128,64]{1,2,0:T(8,128)(2,1)S(1)}, bf16[2,128,64]{1,2,0:T(8,128)(2,1)S(1)}, u32[]{:S(2)}, u32[]{:S(2)}) collective-permute-start(bf16[2,128,64]{1,2,0:T(8,128)(2,1)S(1)} %collective-permute-done.43), channel_id=1, source_target_pairs={{16,0},{32,16},{48,32},{64,48},{80,64},{96,80},{112,96},{17,1},{33... | collective-permute-start | bytes 98312 | tf_op jit(solution)/shard_map/ppermute | solution.py:137
  83.0 19.4 %collective-permute-start.42 = (bf16[2,128,64]{1,2,0:T(8,128)(2,1)S(1)}, bf16[2,128,64]{1,2,0:T(8,128)(2,1)S(1)}, u32[]{:S(2)}, u32[]{:S(2)}) collective-permute-start(bf16[2,128,64]{1,2,0:T(8,128)(2,1)S(1)} %collective-permute-done.41), channel_id=1, source_target_pairs={{0,16},{16,32},{32,48},{48,64},{64,80},{80,96},{96,112},{1,17},{17... | collective-permute-start | bytes 98312 | tf_op jit(solution)/shard_map/ppermute | solution.py:137
  95.1 156.5 %collective-permute-start.49 = (bf16[2,128,64]{1,2,0:T(8,128)(2,1)}, bf16[2,128,64]{1,2,0:T(8,128)(2,1)}, u32[]{:S(2)}, u32[]{:S(2)}) collective-permute-start(bf16[2,128,64]{1,2,0:T(8,128)(2,1)} %collective-permute-done.48), channel_id=1, source_target_pairs={{16,0},{32,16},{48,32},{64,48},{80,64},{96,80},{112,96},{17,1},{33... | collective-permute-start | bytes 98312 | tf_op jit(solution)/shard_map/ppermute | solution.py:137
  129.1 37.2 %collective-permute-start.20 = (bf16[8,64,2,3,128]{4,2,3,1,0:T(2,128)(2,1)S(1)}, bf16[8,64,2,3,128]{4,2,3,1,0:T(2,128)(2,1)S(1)}, u32[]{:S(2)}, u32[]{:S(2)}) collective-permute-start(bf16[8,64,2,3,128]{4,2,3,1,0:T(2,128)(2,1)S(1)} %constant_dynamic-slice_fusion.7), channel_id=1, source_target_pairs={{0,384},{128,0},{256,128},{384,256},{1,385},{129,1},{257,129},{385... | collective-permute-start | bytes 2359304 | tf_op jit(solution)/shard_map/ppermute | solution.py:132
  135.9 51.4 %collective-permute-start.1 = (bf16[2,256,512]{2,1,0:T(8,128)(2,1)}, bf16[2,256,512]{2,1,0:T(8,128)(2,1)}, u32[]{:S(2)}, u32[]{:S(2)}) collective-permute-start(bf16[2,256,512]{2,1,0:T(8,128)(2,1)} %get-tuple-element.303), channel_id=1, source_target_pairs={{0,1},{1,2},{2,3},{3,0},{4,5},{5,6},{6,7},{7,4},{8,9},{9,10},{10,1... | collective-permute-start | bytes 1572872 | tf_op jit(solution)/shard_map/ppermute | solution.py:132
  138.6 48.7 %collective-permute-start.2 = (bf16[2,256,512]{2,1,0:T(8,128)(2,1)}, bf16[2,256,512]{2,1,0:T(8,128)(2,1)}, u32[]{:S(2)}, u32[]{:S(2)}) collective-permute-start(bf16[2,256,512]{2,1,0:T(8,128)(2,1)} %get-tuple-element.303), channel_id=1, source_target_pairs={{0,2},{1,3},{2,0},{3,1},{4,6},{5,7},{6,4},{7,5},{8,10},{9,11},{10,... | collective-permute-start | bytes 1572872 | tf_op jit(solution)/shard_map/ppermute | solution.py:132
  142.6 44.7 %collective-permute-start.3 = (bf16[2,256,512]{2,1,0:T(8,128)(2,1)}, bf16[2,256,512]{2,1,0:T(8,128)(2,1)}, u32[]{:S(2)}, u32[]{:S(2)}) collective-permute-start(bf16[2,256,512]{2,1,0:T(8,128)(2,1)} %get-tuple-element.303), channel_id=1, source_target_pairs={{0,3},{1,0},{2,1},{3,2},{4,7},{5,4},{6,5},{7,6},{8,11},{9,8},{10,9... | collective-permute-start | bytes 1572872 | tf_op jit(solution)/shard_map/ppermute | solution.py:132
  184.8 22.9 %collective-permute-start.21 = (bf16[32,64,2,3,128]{4,1,0,3,2:T(8,128)(2,1)}, bf16[32,64,2,3,128]{4,1,0,3,2:T(8,128)(2,1)}, u32[]{:S(2)}, u32[]{:S(2)}) collective-permute-start(bf16[32,64,2,3,128]{4,1,0,3,2:T(8,128)(2,1)} %broadcast_select_fusion.1), channel_id=1, source_target_pairs={{0,8},{8,0},{1,9},{9,1},{2,10},{10,2},{3,11},{11,3},{4,12},{12,4},... | collective-permute-start | bytes 9437192 | tf_op jit(solution)/shard_map/ppermute | solution.py:132
  236.3 24.5 %collective-permute-start.31 = (bf16[256,2,2,128]{0,3,2,1:T(8,128)(2,1)S(1)}, bf16[256,2,2,128]{0,3,2,1:T(8,128)(2,1)S(1)}, u32[]{:S(2)}, u32[]{:S(2)}) collective-permute-start(bf16[256,2,2,128]{0,3,2,1:T(8,128)(2,1)S(1)} %collective-permute-done.30), channel_id=1, source_target_pairs={{8,0},{16,8},{24,16},{32,24},{40,32},{48,40},{56,48},{64,56},{72,6... | collective-permute-start | bytes 786440 | tf_op jit(solution)/shard_map/ppermute | solution.py:137
  249.7 24.3 %collective-permute-start.25 = (bf16[256,2,2,128]{0,3,2,1:T(8,128)(2,1)S(1)}, bf16[256,2,2,128]{0,3,2,1:T(8,128)(2,1)S(1)}, u32[]{:S(2)}, u32[]{:S(2)}) collective-permute-start(bf16[256,2,2,128]{0,3,2,1:T(8,128)(2,1)S(1)} %collective-permute-done.24), channel_id=1, source_target_pairs={{0,8},{8,16},{16,24},{24,32},{32,40},{40,48},{48,56},{56,64},{64,7... | collective-permute-start | bytes 786440 | tf_op jit(solution)/shard_map/ppermute | solution.py:137
  252.4 24.2 %collective-permute-start.50 = (bf16[8,2,128,64]{2,3,1,0:T(8,128)(2,1)S(1)}, bf16[8,2,128,64]{2,3,1,0:T(8,128)(2,1)S(1)}, u32[]{:S(2)}, u32[]{:S(2)}) collective-permute-start(bf16[8,2,128,64]{2,3,1,0:T(8,128)(2,1)S(1)} %constant_dynamic-slice_fusion.6), channel_id=1, source_target_pairs={{0,128},{128,256},{256,384},{384,0},{1,129},{129,257},{257,385},{3... | collective-permute-start | bytes 786440 | tf_op jit(solution)/shard_map/ppermute | solution.py:132
  255.2 21.5 %collective-permute-start.51 = (bf16[8,2,128,64]{2,3,1,0:T(8,128)(2,1)S(1)}, bf16[8,2,128,64]{2,3,1,0:T(8,128)(2,1)S(1)}, u32[]{:S(2)}, u32[]{:S(2)}) collective-permute-start(bf16[8,2,128,64]{2,3,1,0:T(8,128)(2,1)S(1)} %constant_dynamic-slice_fusion.6), channel_id=1, source_target_pairs={{0,256},{128,384},{256,0},{384,128},{1,257},{129,385},{257,1},{385... | collective-permute-start | bytes 786440 | tf_op jit(solution)/shard_map/ppermute | solution.py:132
  257.1 19.6 %collective-permute-start.52 = (bf16[8,2,128,64]{2,3,1,0:T(8,128)(2,1)S(1)}, bf16[8,2,128,64]{2,3,1,0:T(8,128)(2,1)S(1)}, u32[]{:S(2)}, u32[]{:S(2)}) collective-permute-start(bf16[8,2,128,64]{2,3,1,0:T(8,128)(2,1)S(1)} %constant_dynamic-slice_fusion.6), channel_id=1, source_target_pairs={{0,384},{128,0},{256,128},{384,256},{1,385},{129,1},{257,129},{385... | collective-permute-start | bytes 786440 | tf_op jit(solution)/shard_map/ppermute | solution.py:132
  260.8 18.8 %collective-permute-start.32 = (bf16[256,2,2,128]{0,3,2,1:T(8,128)(2,1)S(1)}, bf16[256,2,2,128]{0,3,2,1:T(8,128)(2,1)}, u32[]{:S(2)}, u32[]{:S(2)}) collective-permute-start(bf16[256,2,2,128]{0,3,2,1:T(8,128)(2,1)S(1)} %collective-permute-done.31), channel_id=1, source_target_pairs={{8,0},{16,8},{24,16},{32,24},{40,32},{48,40},{56,48},{64,56},{72,6... | collective-permute-start | bytes 786440 | tf_op jit(solution)/shard_map/ppermute | solution.py:137
  279.7 24.7 %collective-permute-start.33 = (bf16[256,2,2,128]{0,3,2,1:T(8,128)(2,1)}, bf16[256,2,2,128]{0,3,2,1:T(8,128)(2,1)}, u32[]{:S(2)}, u32[]{:S(2)}) collective-permute-start(bf16[256,2,2,128]{0,3,2,1:T(8,128)(2,1)} %collective-permute-done.32), channel_id=1, source_target_pairs={{8,0},{16,8},{24,16},{32,24},{40,32},{48,40},{56,48},{64,56},{72,6... | collective-permute-start | bytes 786440 | tf_op jit(solution)/shard_map/ppermute | solution.py:137
  293.0 127.0 %collective-permute-start.53 = (bf16[2,128,32,64]{1,3,0,2:T(8,128)(2,1)S(1)}, bf16[2,128,32,64]{1,3,0,2:T(8,128)(2,1)S(1)}, u32[]{:S(2)}, u32[]{:S(2)}) collective-permute-start(bf16[2,128,32,64]{1,3,0,2:T(8,128)(2,1)S(1)} %bitcast.301), channel_id=1, source_target_pairs={{0,8},{8,0},{1,9},{9,1},{2,10},{10,2},{3,11},{11,3},{4,12},{12,4},... | collective-permute-start | bytes 3145736 | tf_op jit(solution)/shard_map/ppermute | solution.py:132
  315.2 27.2 %collective-permute-start.35 = (bf16[256,2,2,128]{0,3,2,1:T(8,128)(2,1)}, bf16[256,2,2,128]{0,3,2,1:T(8,128)(2,1)S(1)}, u32[]{:S(2)}, u32[]{:S(2)}) collective-permute-start(bf16[256,2,2,128]{0,3,2,1:T(8,128)(2,1)} %collective-permute-done.34), channel_id=1, source_target_pairs={{8,0},{16,8},{24,16},{32,24},{40,32},{48,40},{56,48},{64,56},{72,6... | collective-permute-start | bytes 786440 | tf_op jit(solution)/shard_map/ppermute | solution.py:137
  462.1 17.7 %collective-permute-start.58 = (bf16[48,512]{1,0:T(8,128)(2,1)S(1)}, bf16[48,512]{1,0:T(8,128)(2,1)S(1)}, u32[]{:S(2)}, u32[]{:S(2)}) collective-permute-start(bf16[48,512]{1,0:T(8,128)(2,1)S(1)} %slice.104), channel_id=1, source_target_pairs={{8,0},{16,8},{24,16},{32,24},{40,32},{48,40},{56,48},{64,56},{72,6... | collective-permute-start | bytes 147464 | tf_op jit(solution)/shard_map/ppermute | solution.py:137
  (79 other events, 2511.0 us)

commit v3 on v2

--- a/solution.py
+++ b/solution.py
@@ -63,63 +63,26 @@
     )
 
 
-def attend_blocks(query_matrix, kv_blocks, key_segment, key_inside, query_segment, query_inside):
+def attend_all(query_matrix, block_of_keys, block_of_values, query_segment, query_inside, key_segment, key_inside):
     logit_scale_factor = 1.0 / math.sqrt(query_matrix.shape[-1])
-    rows_here = query_matrix.shape[0]
-    heads_here = query_matrix.shape[1]
-
-    def block_scores(block_of_keys, segment_block, inside_block):
-        attention_logits = (
-            jnp.einsum(
-                "ecn,dcn->ced", query_matrix, block_of_keys, preferred_element_type=jnp.float32
-            )
-            * logit_scale_factor
-        )
-        allowed = (
-            query_inside[:, None]
-            & inside_block[None, :]
-            & (query_segment[:, None] == segment_block[None, :])
-        )
-        return (jnp.where(allowed[None], attention_logits, -1e30), allowed)
-
-    def max_step(carry, input_block_rows):
-        row_max, row_total = carry
-        masked, allowed = block_scores(
-            input_block_rows[0][:, 0], input_block_rows[1], input_block_rows[2]
-        )
-        new_max = jnp.maximum(row_max, jnp.max(masked, axis=2, keepdims=True))
-        exp_terms = jnp.where(allowed[None], jnp.exp(masked - new_max), 0.0)
-        row_total = row_total * jnp.exp(row_max - new_max) + jnp.sum(
-            exp_terms, axis=2, keepdims=True
-        )
-        return ((new_max, row_total), None)
-
-    start_max = jnp.full((heads_here, rows_here, 1), -1e30, jnp.float32)
-    start_total = jnp.zeros((heads_here, rows_here, 1), jnp.float32)
-    (row_max, row_total), _ = lax.scan(
-        max_step, (start_max, start_total), (kv_blocks, key_segment, key_inside)
-    )
+    attention_logits = (
+        jnp.einsum("ecn,dcn->ced", query_matrix, block_of_keys, preferred_element_type=jnp.float32)
+        * logit_scale_factor
+    )
+    allowed = (
+        query_inside[:, None]
+        & key_inside[None, :]
+        & (query_segment[:, None] == key_segment[None, :])
+    )
+    masked = jnp.where(allowed[None], attention_logits, -1e30)
+    row_max = jnp.max(masked, axis=2, keepdims=True)
+    exp_terms = jnp.where(allowed[None], jnp.exp(masked - row_max), 0.0)
+    row_total = jnp.sum(exp_terms, axis=2, keepdims=True)
     row_total = jnp.where(query_inside[None, :, None], row_total, 1.0)
-
-    def sum_step(running, input_block_rows):
-        masked, allowed = block_scores(
-            input_block_rows[0][:, 0], input_block_rows[1], input_block_rows[2]
-        )
-        exp_terms = jnp.where(allowed[None], jnp.exp(masked - row_max), 0.0)
-        softmax_probabilities = (exp_terms / row_total).astype(jnp.bfloat16)
-        return (
-            running
-            + jnp.einsum(
-                "vgm,mvb->gvb",
-                softmax_probabilities,
-                input_block_rows[0][:, 1],
-                preferred_element_type=jnp.float32,
-            ),
-            None,
-        )
-
-    start_sum = jnp.zeros((rows_here, heads_here, query_matrix.shape[2]), jnp.float32)
-    attended_output, _ = lax.scan(sum_step, start_sum, (kv_blocks, key_segment, key_inside))
+    softmax_probabilities = (exp_terms / row_total).astype(jnp.bfloat16)
+    attended_output = jnp.einsum(
+        "vgm,mvb->gvb", softmax_probabilities, block_of_values, preferred_element_type=jnp.float32
+    )
     attended_output = jnp.where(query_inside[:, None, None], attended_output, 0.0)
     return attended_output.astype(jnp.bfloat16)
 
@@ -165,10 +128,19 @@
     seq_index = (lax.axis_index("y") * n_zl + lax.axis_index("zl")) * n_c + c
     first_row = seq_index * rows_here
 
-    wq_mine = gather_seq_blocks(w_qkv, n_y, n_zl)
-    wo_mine = jnp.transpose(gather_seq_blocks(w_out, n_y, n_zl), (1, 2, 0, 3))
-    wq_other = ring(wq_mine, "c", n_c, 1)
-    wo_other = ring(wo_mine, "c", n_c, 1)
+    both = jnp.concatenate([w_qkv.reshape(-1), w_out.reshape(-1)])
+    both_mine = gather_seq_blocks(both, n_y, n_zl)
+    both_other = ring(both_mine, "c", n_c, 1)
+    split_at = w_qkv.size
+    n_j = n_y * n_zl
+
+    def unpack(gathered):
+        wq = gathered[:, :split_at].reshape(n_j, *w_qkv.shape)
+        wo = jnp.transpose(gathered[:, split_at:].reshape(n_j, *w_out.shape), (1, 2, 0, 3))
+        return wq, wo
+
+    wq_mine, wo_mine = unpack(both_mine)
+    wq_other, wo_other = unpack(both_other)
 
     partner = ring(tokens, "zh", n_zh, 1)
     pair = jnp.stack([tokens, partner])
@@ -212,13 +184,11 @@
         from_right = chain(from_right, SEQ, n_seq, -1)
         pieces[REACH - distance] = from_left
         pieces[REACH + distance] = from_right
-    kv_blocks = jnp.stack(pieces, axis=0)
+    kv_all = jnp.concatenate(pieces, axis=0)
     key_rows = first_row - REACH * rows_here + jnp.arange(block_count * rows_here, dtype=jnp.int32)
     key_layout = layout_rows(key_rows, offsets, grids, row_count)
-    key_segment = key_layout[0].reshape(block_count, rows_here)
-    key_inside = key_layout[1].reshape(block_count, rows_here)
-    attended_output = attend_blocks(
-        query_matrix, kv_blocks, key_segment, key_inside, segment, inside
+    attended_output = attend_all(
+        query_matrix, kv_all[:, 0], kv_all[:, 1], segment, inside, key_layout[0], key_layout[1]
     )
     proj_mine = jnp.einsum(
         "thf,hfjd->tjd", attended_output, wo_mine, preferred_element_type=jnp.float32

time: 492 us -> 441 us (0.90)
  the two profiles are of different devices: /device:TPU:15 before, /device:TPU:26 now
where the time goes in v3:
time: 441 us; the launch traced here: 438 us
  starting transfers between devices  189 us (43%)
  waiting for transfers between devices  116 us (26%)
  local copies, waits for them, and re-layouts  80.8 us (18%)
  other arithmetic  26.6 us (6%)
  matrix products  23.6 us (5%)
    ppermute x29, starting transfers between devices, chain(): return lax.ppermute(shard, axis, pairs)  137 us
    ppermute x12, waiting for transfers between devices, ring(): lax.ppermute(shard, axis, [(i, (i + by) % size) for i in range(size)])  80.4 us
    ppermute x12, starting transfers between devices, ring(): lax.ppermute(shard, axis, [(i, (i + by) % size) for i in range(size)])  51.8 us
    ppermute x29, waiting for transfers between devices, chain(): return lax.ppermute(shard, axis, pairs)  35.8 us
    another operation x16, local copies, waits for them, and re-layouts, gather_seq_blocks(): every = jnp.stack(lefts[::-1] + [local] + rights)  19.3 us
    unnamed x92, local copies, waits for them, and re-layouts  15 us
    reshape x2, local copies, waits for them, and re-layouts, unpack(): wq = gathered[:, :split_at].reshape(n_j, *w_qkv.shape)  11 us
  transfers between devices with their start and end apart: 41, of which 28 were waited for; matrix products, arithmetic and copies ran while one was open for 20% of the time, Pallas kernels for 0%

profile of v3, /device:TPU:26, one launch (start us, length us, event | category | flops | bytes accessed | tf_op | source)
XLA Modules:
  0.0 437.7 jit_solution(1342786414308872904)
XLA Ops:
  24.6 5.3 %collective-permute-start.7 = (bf16[65536]{0:T(1024)(128)(2,1)S(1)}, bf16[65536]{0:T(1024)(128)(2,1)S(1)}, u32[]{:S(2)}, u32[]{:S(2)}) collective-permute-start(bf16[65536]{0:T(1024)(128)(2,1)S(1)} %collective-permute-done.6), channel_id=1, source_target_pairs={{0,16},{16,32},{32,48},{48,64},{64,80},{80,96},{96,112},{1,17},{17... | collective-permute-start | bytes 393224 | tf_op jit(solution)/shard_map/ppermute | solution.py:100
  29.8 14.6 %collective-permute-start = (bf16[256,512]{1,0:T(8,128)(2,1)}, bf16[256,512]{1,0:T(8,128)(2,1)}, u32[]{:S(2)}, u32[]{:S(2)}) collective-permute-start(bf16[256,512]{1,0:T(8,128)(2,1)} %param.8), channel_id=1, source_target_pairs={{0,4},{4,0},{1,5},{5,1},{2,6},{6,2},{3,7},{7,3},{8,12},{12,8},{9,1... | collective-permute-start | bytes 786440 | tf_op jit(solution)/shard_map/ppermute | solution.py:95
  51.6 17.0 %collective-permute-done.15 = bf16[65536]{0:T(1024)(128)(2,1)S(1)} collective-permute-done((bf16[65536]{0:T(1024)(128)(2,1)S(1)}, bf16[65536]{0:T(1024)(128)(2,1)S(1)}, u32[]{:S(2)}, u32[]{:S(2)}) %collective-permute-start.15) | collective-permute-done | bytes 131104 | tf_op jit(solution)/shard_map/ppermute | solution.py:100
  90.7 10.2 %stack.140 = bf16[15,65536]{1,0:T(8,128)(2,1)S(1)} concatenate(bf16[1,65536]{1,0:T(2,128)(2,1)} %stack.125, bf16[1,65536]{1,0:T(2,128)(2,1)} %stack.126, bf16[1,65536]{1,0:T(2,128)(2,1)} %stack.127, bf16[1,65536]{1,0:T(2,128)(2,1)} %stack.128, bf16[1,65536]{1,0:T(2,128)(2,1)} %stack.129, bf16[1,65536]{1,0:T(2,128)(2,1)S(1)} %stack.130, bf16[1,65536]{1,0:T(2,128)(2,1)S(1)} %stack.131, ...), dimensions={0} | concatenate | bytes 3932160 | tf_op jit(solution)/shard_map/stack | solution.py:113
  110.8 20.0 %collective-permute-done.19 = bf16[8,65536]{1,0:T(8,128)(2,1)S(1)} collective-permute-done((bf16[8,65536]{1,0:T(8,128)(2,1)S(1)}, bf16[8,65536]{1,0:T(8,128)(2,1)S(1)}, u32[]{:S(2)}, u32[]{:S(2)}) %collective-permute-start.19) | collective-permute-done | bytes 1048608 | tf_op jit(solution)/shard_map/ppermute | solution.py:95
  130.8 16.7 %collective-permute-done.18 = bf16[8,65536]{1,0:T(8,128)(2,1)S(1)} collective-permute-done((bf16[8,65536]{1,0:T(8,128)(2,1)S(1)}, bf16[8,65536]{1,0:T(8,128)(2,1)S(1)}, u32[]{:S(2)}, u32[]{:S(2)}) %collective-permute-start.18) | collective-permute-done | bytes 1048608 | tf_op jit(solution)/shard_map/ppermute | solution.py:95
  152.1 5.0 %gather_fusion.1 = bf16[4,8,65536]{2,1,0:T(8,128)(2,1)} fusion(bf16[4,8,65536]{2,1,0:T(8,128)(2,1)} %pad_maximum_fusion, s32[1024]{0:T(1024)S(1)} %pad_clamp_fusion), kind=kCustom, calls=%fused_computation.1 | custom fusion | bytes 8388624 | tf_op jit(solution)/shard_map/jit(_take)/gather | solution.py:116
  176.8 7.2 %collective-permute-done.2 = bf16[2,256,512]{2,1,0:T(8,128)(2,1)S(1)} collective-permute-done((bf16[2,256,512]{2,1,0:T(8,128)(2,1)S(1)}, bf16[2,256,512]{2,1,0:T(8,128)(2,1)S(1)}, u32[]{:S(2)}, u32[]{:S(2)}) %collective-permute-start.2) | collective-permute-done | bytes 524320 | tf_op jit(solution)/shard_map/ppermute | solution.py:95
  184.0 10.8 %collective-permute-done.1 = bf16[2,256,512]{2,1,0:T(8,128)(2,1)S(1)} collective-permute-done((bf16[2,256,512]{2,1,0:T(8,128)(2,1)S(1)}, bf16[2,256,512]{2,1,0:T(8,128)(2,1)S(1)}, u32[]{:S(2)}, u32[]{:S(2)}) %collective-permute-start.1) | collective-permute-done | bytes 524320 | tf_op jit(solution)/shard_map/ppermute | solution.py:95
  201.6 5.2 %copy.54 = f32[256,2,4,512]{0,3,2,1:T(8,128)} copy(f32[256,2,4,512]{3,0,1,2:T(8,128)} %convert_bitcast_fusion) | data formatting | bytes 8388608 | tf_op jit(solution)/shard_map/convert_element_type | solution.py:153
  213.3 5.5 %reshape.742 = bf16[32,64,2,3,128]{4,3,2,1,0:T(4,128)(2,1)} reshape(bf16[32,49152]{1,0:T(8,128)(2,1)S(1)} %slice.100) | data formatting | bytes 6291456 | tf_op jit(solution)/shard_map/reshape | solution.py:138
  225.7 5.5 %reshape.743 = bf16[32,64,2,3,128]{4,3,2,1,0:T(4,128)(2,1)} reshape(bf16[32,49152]{1,0:T(8,128)(2,1)S(1)} %slice.101) | data formatting | bytes 6291456 | tf_op jit(solution)/shard_map/reshape | solution.py:138
  238.8 11.1 %collective-permute-start.29 = (bf16[256,2,2,128]{0,3,2,1:T(8,128)(2,1)S(1)}, bf16[256,2,2,128]{0,3,2,1:T(8,128)(2,1)S(1)}, u32[]{:S(2)}, u32[]{:S(2)}) collective-permute-start(bf16[256,2,2,128]{0,3,2,1:T(8,128)(2,1)S(1)} %pad_maximum_fusion.5), channel_id=1, source_target_pairs={{8,0},{16,8},{24,16},{32,24},{40,32},{48,40},{56,48},{64,56},{72,6... | collective-permute-start | bytes 786440 | tf_op jit(solution)/shard_map/ppermute | solution.py:100
  255.6 11.1 %collective-permute-start.30 = (bf16[256,2,2,128]{0,3,2,1:T(8,128)(2,1)S(1)}, bf16[256,2,2,128]{0,3,2,1:T(8,128)(2,1)S(1)}, u32[]{:S(2)}, u32[]{:S(2)}) collective-permute-start(bf16[256,2,2,128]{0,3,2,1:T(8,128)(2,1)S(1)} %collective-permute-done.29), channel_id=1, source_target_pairs={{8,0},{16,8},{24,16},{32,24},{40,32},{48,40},{56,48},{64,56},{72,6... | collective-permute-start | bytes 786440 | tf_op jit(solution)/shard_map/ppermute | solution.py:100
  270.6 11.5 %collective-permute-start.31 = (bf16[256,2,2,128]{0,3,2,1:T(8,128)(2,1)S(1)}, bf16[256,2,2,128]{0,3,2,1:T(8,128)(2,1)S(1)}, u32[]{:S(2)}, u32[]{:S(2)}) collective-permute-start(bf16[256,2,2,128]{0,3,2,1:T(8,128)(2,1)S(1)} %collective-permute-done.30), channel_id=1, source_target_pairs={{8,0},{16,8},{24,16},{32,24},{40,32},{48,40},{56,48},{64,56},{72,6... | collective-permute-start | bytes 786440 | tf_op jit(solution)/shard_map/ppermute | solution.py:100
  286.0 11.4 %collective-permute-start.32 = (bf16[256,2,2,128]{0,3,2,1:T(8,128)(2,1)S(1)}, bf16[256,2,2,128]{0,3,2,1:T(8,128)(2,1)S(1)}, u32[]{:S(2)}, u32[]{:S(2)}) collective-permute-start(bf16[256,2,2,128]{0,3,2,1:T(8,128)(2,1)S(1)} %collective-permute-done.31), channel_id=1, source_target_pairs={{8,0},{16,8},{24,16},{32,24},{40,32},{48,40},{56,48},{64,56},{72,6... | collective-permute-start | bytes 786440 | tf_op jit(solution)/shard_map/ppermute | solution.py:100
  301.3 11.4 %collective-permute-start.33 = (bf16[256,2,2,128]{0,3,2,1:T(8,128)(2,1)S(1)}, bf16[256,2,2,128]{0,3,2,1:T(8,128)(2,1)}, u32[]{:S(2)}, u32[]{:S(2)}) collective-permute-start(bf16[256,2,2,128]{0,3,2,1:T(8,128)(2,1)S(1)} %collective-permute-done.32), channel_id=1, source_target_pairs={{8,0},{16,8},{24,16},{32,24},{40,32},{48,40},{56,48},{64,56},{72,6... | collective-permute-start | bytes 786440 | tf_op jit(solution)/shard_map/ppermute | solution.py:100
  316.6 11.4 %collective-permute-start.34 = (bf16[256,2,2,128]{0,3,2,1:T(8,128)(2,1)}, bf16[256,2,2,128]{0,3,2,1:T(8,128)(2,1)}, u32[]{:S(2)}, u32[]{:S(2)}) collective-permute-start(bf16[256,2,2,128]{0,3,2,1:T(8,128)(2,1)} %collective-permute-done.33), channel_id=1, source_target_pairs={{8,0},{16,8},{24,16},{32,24},{40,32},{48,40},{56,48},{64,56},{72,6... | collective-permute-start | bytes 786440 | tf_op jit(solution)/shard_map/ppermute | solution.py:100
  344.5 11.3 %collective-permute-start.35 = (bf16[256,2,2,128]{0,3,2,1:T(8,128)(2,1)}, bf16[256,2,2,128]{0,3,2,1:T(8,128)(2,1)S(1)}, u32[]{:S(2)}, u32[]{:S(2)}) collective-permute-start(bf16[256,2,2,128]{0,3,2,1:T(8,128)(2,1)} %collective-permute-done.34), channel_id=1, source_target_pairs={{8,0},{16,8},{24,16},{32,24},{40,32},{48,40},{56,48},{64,56},{72,6... | collective-permute-start | bytes 786440 | tf_op jit(solution)/shard_map/ppermute | solution.py:100
  366.7 8.6 %fusion.69 = (f32[2,256]{1,0:T(2,128)S(1)}, f32[2,256,3840]{2,1,0:T(8,128)}) fusion(pred[256,3840]{1,0:T(8,128)(4,1)S(1)} %copy-done.3, bf16[3840,2,2,128]{0,3,2,1:T(8,128)(2,1)} %copy-done.30, bf16[256,2,32]{0,2,1:T(8,128)(2,1)S(1)} %get-tuple-element.30, bf16[256,2,32]{0,2,1:T(8,128)(2,1)S(1)} %get-tuple-element.31, ...), kind=kOutput, calls=%fused_computation.185 | convolution fusion | flops 513675008 | bytes 11929600 | tf_op jit(solution)/shard_map/sub | solution.py:79
  375.3 5.4 %fusion.24 = bf16[256,2,128,1]{0,2,1,3:T(8,128)(2,1)S(1)} fusion(f32[2,256,3840]{2,1,0:T(8,128)} %get-tuple-element.49, f32[2,256]{1,0:T(2,128)S(1)} %broadcast_select_fusion.1, bf16[3840,2,2,128]{0,3,2,1:T(8,128)(2,1)} %copy-done.30, pred[256]{0:T(512)(128)(4,1)S(1)} %get-tuple-element.11), kind=kOutput, calls=%fused_computation.39 | convolution fusion | flops 507379712 | bytes 9963776 | tf_op jit(solution)/shard_map/vgm,mvb->gvb/dot_general | solution.py:83
  401.2 5.5 %collective-permute-done.38 = bf16[256,2,512]{2,0,1:T(8,128)(2,1)} collective-permute-done((bf16[256,2,512]{2,0,1:T(8,128)(2,1)S(1)}, bf16[256,2,512]{2,0,1:T(8,128)(2,1)}, u32[]{:S(2)}, u32[]{:S(2)}) %collective-permute-start.38) | collective-permute-done | bytes 524320 | tf_op jit(solution)/shard_map/ppermute | solution.py:95
  408.3 5.6 %collective-permute-start.39 = (bf16[256,512]{1,0:T(8,128)(2,1)S(1)}, bf16[256,512]{1,0:T(8,128)(2,1)S(1)}, u32[]{:S(2)}, u32[]{:S(2)}) collective-permute-start(bf16[256,512]{1,0:T(8,128)(2,1)S(1)} %fusion.36), channel_id=1, source_target_pairs={{0,4},{4,0},{1,5},{5,1},{2,6},{6,2},{3,7},{7,3},{8,12},{12,8},{9,1... | collective-permute-start | bytes 786440 | tf_op jit(solution)/shard_map/ppermute | solution.py:95
  414.3 11.1 %collective-permute-done.39 = bf16[256,512]{1,0:T(8,128)(2,1)S(1)} collective-permute-done((bf16[256,512]{1,0:T(8,128)(2,1)S(1)}, bf16[256,512]{1,0:T(8,128)(2,1)S(1)}, u32[]{:S(2)}, u32[]{:S(2)}) %collective-permute-start.39) | collective-permute-done | bytes 262176 | tf_op jit(solution)/shard_map/ppermute | solution.py:95
  (255 shorter events, 198.0 us)
Async XLA Ops:
  23.0 21.4 %collective-permute-start.14 = (bf16[65536]{0:T(1024)(128)(2,1)S(1)}, bf16[65536]{0:T(1024)(128)(2,1)S(1)}, u32[]{:S(2)}, u32[]{:S(2)}) collective-permute-start(bf16[65536]{0:T(1024)(128)(2,1)S(1)} %collective-permute-done.13), channel_id=1, source_target_pairs={{16,0},{32,16},{48,32},{64,48},{80,64},{96,80},{112,96},{17,1},{33... | collective-permute-start | bytes 393224 | tf_op jit(solution)/shard_map/ppermute | solution.py:100
  24.6 21.2 %collective-permute-start.7 = (bf16[65536]{0:T(1024)(128)(2,1)S(1)}, bf16[65536]{0:T(1024)(128)(2,1)S(1)}, u32[]{:S(2)}, u32[]{:S(2)}) collective-permute-start(bf16[65536]{0:T(1024)(128)(2,1)S(1)} %collective-permute-done.6), channel_id=1, source_target_pairs={{0,16},{16,32},{32,48},{48,64},{64,80},{80,96},{96,112},{1,17},{17... | collective-permute-start | bytes 393224 | tf_op jit(solution)/shard_map/ppermute | solution.py:100
  29.8 134.9 %collective-permute-start = (bf16[256,512]{1,0:T(8,128)(2,1)}, bf16[256,512]{1,0:T(8,128)(2,1)}, u32[]{:S(2)}, u32[]{:S(2)}) collective-permute-start(bf16[256,512]{1,0:T(8,128)(2,1)} %param.8), channel_id=1, source_target_pairs={{0,4},{4,0},{1,5},{5,1},{2,6},{6,2},{3,7},{7,3},{8,12},{12,8},{9,1... | collective-permute-start | bytes 786440 | tf_op jit(solution)/shard_map/ppermute | solution.py:95
  44.5 24.2 %collective-permute-start.15 = (bf16[65536]{0:T(1024)(128)(2,1)S(1)}, bf16[65536]{0:T(1024)(128)(2,1)S(1)}, u32[]{:S(2)}, u32[]{:S(2)}) collective-permute-start(bf16[65536]{0:T(1024)(128)(2,1)S(1)} %collective-permute-done.14), channel_id=1, source_target_pairs={{16,0},{32,16},{48,32},{64,48},{80,64},{96,80},{112,96},{17,1},{33... | collective-permute-start | bytes 393224 | tf_op jit(solution)/shard_map/ppermute | solution.py:100
  45.8 24.1 %collective-permute-start.8 = (bf16[65536]{0:T(1024)(128)(2,1)S(1)}, bf16[65536]{0:T(1024)(128)(2,1)S(1)}, u32[]{:S(2)}, u32[]{:S(2)}) collective-permute-start(bf16[65536]{0:T(1024)(128)(2,1)S(1)} %collective-permute-done.7), channel_id=1, source_target_pairs={{0,16},{16,32},{32,48},{48,64},{64,80},{80,96},{96,112},{1,17},{17... | collective-permute-start | bytes 393224 | tf_op jit(solution)/shard_map/ppermute | solution.py:100
  101.3 29.5 %collective-permute-start.19 = (bf16[8,65536]{1,0:T(8,128)(2,1)S(1)}, bf16[8,65536]{1,0:T(8,128)(2,1)S(1)}, u32[]{:S(2)}, u32[]{:S(2)}) collective-permute-start(bf16[8,65536]{1,0:T(8,128)(2,1)S(1)} %constant_dynamic-slice_fusion.4), channel_id=1, source_target_pairs={{0,256},{128,384},{256,0},{384,128},{1,257},{129,385},{257,1},{385... | collective-permute-start | bytes 3145736 | tf_op jit(solution)/shard_map/ppermute | solution.py:95
  104.4 43.0 %collective-permute-start.18 = (bf16[8,65536]{1,0:T(8,128)(2,1)S(1)}, bf16[8,65536]{1,0:T(8,128)(2,1)S(1)}, u32[]{:S(2)}, u32[]{:S(2)}) collective-permute-start(bf16[8,65536]{1,0:T(8,128)(2,1)S(1)} %constant_dynamic-slice_fusion.4), channel_id=1, source_target_pairs={{0,128},{128,256},{256,384},{384,0},{1,129},{129,257},{257,385},{3... | collective-permute-start | bytes 3145736 | tf_op jit(solution)/shard_map/ppermute | solution.py:95
  108.5 41.3 %collective-permute-start.20 = (bf16[8,65536]{1,0:T(8,128)(2,1)S(1)}, bf16[8,65536]{1,0:T(8,128)(2,1)S(1)}, u32[]{:S(2)}, u32[]{:S(2)}) collective-permute-start(bf16[8,65536]{1,0:T(8,128)(2,1)S(1)} %constant_dynamic-slice_fusion.4), channel_id=1, source_target_pairs={{0,384},{128,0},{256,128},{384,256},{1,385},{129,1},{257,129},{385... | collective-permute-start | bytes 3145736 | tf_op jit(solution)/shard_map/ppermute | solution.py:95
  161.8 61.8 %collective-permute-start.21 = (bf16[32,65536]{1,0:T(8,128)(2,1)}, bf16[32,65536]{1,0:T(8,128)(2,1)}, u32[]{:S(2)}, u32[]{:S(2)}) collective-permute-start(bf16[32,65536]{1,0:T(8,128)(2,1)} %bitcast_select_fusion), channel_id=1, source_target_pairs={{0,8},{8,0},{1,9},{9,1},{2,10},{10,2},{3,11},{11,3},{4,12},{12,4},... | collective-permute-start | bytes 12582920 | tf_op jit(solution)/shard_map/ppermute | solution.py:95
  165.8 18.2 %collective-permute-start.2 = (bf16[2,256,512]{2,1,0:T(8,128)(2,1)S(1)}, bf16[2,256,512]{2,1,0:T(8,128)(2,1)S(1)}, u32[]{:S(2)}, u32[]{:S(2)}) collective-permute-start(bf16[2,256,512]{2,1,0:T(8,128)(2,1)S(1)} %get-tuple-element.21), channel_id=1, source_target_pairs={{0,2},{1,3},{2,0},{3,1},{4,6},{5,7},{6,4},{7,5},{8,10},{9,11},{10,... | collective-permute-start | bytes 1572872 | tf_op jit(solution)/shard_map/ppermute | solution.py:95
  169.8 25.0 %collective-permute-start.1 = (bf16[2,256,512]{2,1,0:T(8,128)(2,1)S(1)}, bf16[2,256,512]{2,1,0:T(8,128)(2,1)S(1)}, u32[]{:S(2)}, u32[]{:S(2)}) collective-permute-start(bf16[2,256,512]{2,1,0:T(8,128)(2,1)S(1)} %get-tuple-element.21), channel_id=1, source_target_pairs={{0,1},{1,2},{2,3},{3,0},{4,5},{5,6},{6,7},{7,4},{8,9},{9,10},{10,1... | collective-permute-start | bytes 1572872 | tf_op jit(solution)/shard_map/ppermute | solution.py:95
  171.7 23.1 %collective-permute-start.3 = (bf16[2,256,512]{2,1,0:T(8,128)(2,1)S(1)}, bf16[2,256,512]{2,1,0:T(8,128)(2,1)S(1)}, u32[]{:S(2)}, u32[]{:S(2)}) collective-permute-start(bf16[2,256,512]{2,1,0:T(8,128)(2,1)S(1)} %get-tuple-element.21), channel_id=1, source_target_pairs={{0,3},{1,0},{2,1},{3,2},{4,7},{5,4},{6,5},{7,6},{8,11},{9,8},{10,9... | collective-permute-start | bytes 1572872 | tf_op jit(solution)/shard_map/ppermute | solution.py:95
  236.8 16.1 %collective-permute-start.22 = (bf16[256,2,2,128]{0,3,2,1:T(8,128)(2,1)S(1)}, bf16[256,2,2,128]{0,3,2,1:T(8,128)(2,1)S(1)}, u32[]{:S(2)}, u32[]{:S(2)}) collective-permute-start(bf16[256,2,2,128]{0,3,2,1:T(8,128)(2,1)S(1)} %pad_maximum_fusion.5), channel_id=1, source_target_pairs={{0,8},{8,16},{16,24},{24,32},{32,40},{40,48},{48,56},{56,64},{64,7... | collective-permute-start | bytes 786440 | tf_op jit(solution)/shard_map/ppermute | solution.py:100
  238.8 16.1 %collective-permute-start.29 = (bf16[256,2,2,128]{0,3,2,1:T(8,128)(2,1)S(1)}, bf16[256,2,2,128]{0,3,2,1:T(8,128)(2,1)S(1)}, u32[]{:S(2)}, u32[]{:S(2)}) collective-permute-start(bf16[256,2,2,128]{0,3,2,1:T(8,128)(2,1)S(1)} %pad_maximum_fusion.5), channel_id=1, source_target_pairs={{8,0},{16,8},{24,16},{32,24},{40,32},{48,40},{56,48},{64,56},{72,6... | collective-permute-start | bytes 786440 | tf_op jit(solution)/shard_map/ppermute | solution.py:100
  253.0 15.3 %collective-permute-start.23 = (bf16[256,2,2,128]{0,3,2,1:T(8,128)(2,1)S(1)}, bf16[256,2,2,128]{0,3,2,1:T(8,128)(2,1)S(1)}, u32[]{:S(2)}, u32[]{:S(2)}) collective-permute-start(bf16[256,2,2,128]{0,3,2,1:T(8,128)(2,1)S(1)} %collective-permute-done.22), channel_id=1, source_target_pairs={{0,8},{8,16},{16,24},{24,32},{32,40},{40,48},{48,56},{56,64},{64,7... | collective-permute-start | bytes 786440 | tf_op jit(solution)/shard_map/ppermute | solution.py:100
  268.3 15.4 %collective-permute-start.24 = (bf16[256,2,2,128]{0,3,2,1:T(8,128)(2,1)S(1)}, bf16[256,2,2,128]{0,3,2,1:T(8,128)(2,1)S(1)}, u32[]{:S(2)}, u32[]{:S(2)}) collective-permute-start(bf16[256,2,2,128]{0,3,2,1:T(8,128)(2,1)S(1)} %collective-permute-done.23), channel_id=1, source_target_pairs={{0,8},{8,16},{16,24},{24,32},{32,40},{40,48},{48,56},{56,64},{64,7... | collective-permute-start | bytes 786440 | tf_op jit(solution)/shard_map/ppermute | solution.py:100
  270.6 15.4 %collective-permute-start.31 = (bf16[256,2,2,128]{0,3,2,1:T(8,128)(2,1)S(1)}, bf16[256,2,2,128]{0,3,2,1:T(8,128)(2,1)S(1)}, u32[]{:S(2)}, u32[]{:S(2)}) collective-permute-start(bf16[256,2,2,128]{0,3,2,1:T(8,128)(2,1)S(1)} %collective-permute-done.30), channel_id=1, source_target_pairs={{8,0},{16,8},{24,16},{32,24},{40,32},{48,40},{56,48},{64,56},{72,6... | collective-permute-start | bytes 786440 | tf_op jit(solution)/shard_map/ppermute | solution.py:100
  283.7 15.3 %collective-permute-start.25 = (bf16[256,2,2,128]{0,3,2,1:T(8,128)(2,1)S(1)}, bf16[256,2,2,128]{0,3,2,1:T(8,128)(2,1)S(1)}, u32[]{:S(2)}, u32[]{:S(2)}) collective-permute-start(bf16[256,2,2,128]{0,3,2,1:T(8,128)(2,1)S(1)} %collective-permute-done.24), channel_id=1, source_target_pairs={{0,8},{8,16},{16,24},{24,32},{32,40},{40,48},{48,56},{56,64},{64,7... | collective-permute-start | bytes 786440 | tf_op jit(solution)/shard_map/ppermute | solution.py:100
  314.3 15.3 %collective-permute-start.27 = (bf16[256,2,2,128]{0,3,2,1:T(8,128)(2,1)S(1)}, bf16[256,2,2,128]{0,3,2,1:T(8,128)(2,1)}, u32[]{:S(2)}, u32[]{:S(2)}) collective-permute-start(bf16[256,2,2,128]{0,3,2,1:T(8,128)(2,1)S(1)} %collective-permute-done.26), channel_id=1, source_target_pairs={{0,8},{8,16},{16,24},{24,32},{32,40},{40,48},{48,56},{56,64},{64,7... | collective-permute-start | bytes 786440 | tf_op jit(solution)/shard_map/ppermute | solution.py:100
  316.6 28.0 %collective-permute-start.34 = (bf16[256,2,2,128]{0,3,2,1:T(8,128)(2,1)}, bf16[256,2,2,128]{0,3,2,1:T(8,128)(2,1)}, u32[]{:S(2)}, u32[]{:S(2)}) collective-permute-start(bf16[256,2,2,128]{0,3,2,1:T(8,128)(2,1)} %collective-permute-done.33), channel_id=1, source_target_pairs={{8,0},{16,8},{24,16},{32,24},{40,32},{48,40},{56,48},{64,56},{72,6... | collective-permute-start | bytes 786440 | tf_op jit(solution)/shard_map/ppermute | solution.py:100
  329.6 26.3 %collective-permute-start.28 = (bf16[256,2,2,128]{0,3,2,1:T(8,128)(2,1)}, bf16[256,2,2,128]{0,3,2,1:T(8,128)(2,1)}, u32[]{:S(2)}, u32[]{:S(2)}) collective-permute-start(bf16[256,2,2,128]{0,3,2,1:T(8,128)(2,1)} %collective-permute-done.27), channel_id=1, source_target_pairs={{0,8},{8,16},{16,24},{24,32},{32,40},{40,48},{48,56},{56,64},{64,7... | collective-permute-start | bytes 786440 | tf_op jit(solution)/shard_map/ppermute | solution.py:100
  344.5 20.3 %collective-permute-start.35 = (bf16[256,2,2,128]{0,3,2,1:T(8,128)(2,1)}, bf16[256,2,2,128]{0,3,2,1:T(8,128)(2,1)S(1)}, u32[]{:S(2)}, u32[]{:S(2)}) collective-permute-start(bf16[256,2,2,128]{0,3,2,1:T(8,128)(2,1)} %collective-permute-done.34), channel_id=1, source_target_pairs={{8,0},{16,8},{24,16},{32,24},{40,32},{48,40},{56,48},{64,56},{72,6... | collective-permute-start | bytes 786440 | tf_op jit(solution)/shard_map/ppermute | solution.py:100
  390.1 16.6 %collective-permute-start.38 = (bf16[256,2,512]{2,0,1:T(8,128)(2,1)S(1)}, bf16[256,2,512]{2,0,1:T(8,128)(2,1)}, u32[]{:S(2)}, u32[]{:S(2)}) collective-permute-start(bf16[256,2,512]{2,0,1:T(8,128)(2,1)S(1)} %bitcast.142), channel_id=1, source_target_pairs={{0,3},{1,0},{2,1},{3,2},{4,7},{5,4},{6,5},{7,6},{8,11},{9,8},{10,9... | collective-permute-start | bytes 1572872 | tf_op jit(solution)/shard_map/ppermute | solution.py:95
  408.3 17.0 %collective-permute-start.39 = (bf16[256,512]{1,0:T(8,128)(2,1)S(1)}, bf16[256,512]{1,0:T(8,128)(2,1)S(1)}, u32[]{:S(2)}, u32[]{:S(2)}) collective-permute-start(bf16[256,512]{1,0:T(8,128)(2,1)S(1)} %fusion.36), channel_id=1, source_target_pairs={{0,4},{4,0},{1,5},{5,1},{2,6},{6,2},{3,7},{7,3},{8,12},{12,8},{9,1... | collective-permute-start | bytes 786440 | tf_op jit(solution)/shard_map/ppermute | solution.py:95
  (54 other events, 712.5 us)

commit v4 on v3

--- a/solution.py
+++ b/solution.py
@@ -100,21 +100,14 @@
     return lax.ppermute(shard, axis, pairs)
 
 
+def everyone(block, axis, size):
+    repeated = jnp.broadcast_to(block[None], (size, *block.shape))
+    return lax.all_to_all(repeated, axis, 0, 0, tiled=True)
+
+
 def gather_seq_blocks(local, n_y, n_zl):
-    zl = lax.axis_index("zl")
-    y = lax.axis_index("y")
-    left, right = local, local
-    lefts, rights = [], []
-    for _ in range(1, n_zl):
-        left = chain(left, "zl", n_zl, 1)
-        right = chain(right, "zl", n_zl, -1)
-        lefts.append(left)
-        rights.append(right)
-    every = jnp.stack(lefts[::-1] + [local] + rights)
-    line = lax.dynamic_slice_in_dim(every, n_zl - 1 - zl, n_zl, axis=0)
-    by_shift = jnp.stack([line] + [ring(line, "y", n_y, s) for s in range(1, n_y)])
-    by_y = jnp.take(by_shift, (y - jnp.arange(n_y)) % n_y, axis=0)
-    return by_y.reshape(n_y * n_zl, *local.shape)
+    line = everyone(local, "zl", n_zl)
+    return everyone(line, "y", n_y).reshape(n_y * n_zl, *local.shape)
 
 
 def body(sizes, tokens, ln_gain, ln_bias, w_qkv, w_out, layer_scale, grids, offsets):
@@ -128,25 +121,16 @@
     seq_index = (lax.axis_index("y") * n_zl + lax.axis_index("zl")) * n_c + c
     first_row = seq_index * rows_here
 
-    both = jnp.concatenate([w_qkv.reshape(-1), w_out.reshape(-1)])
-    both_mine = gather_seq_blocks(both, n_y, n_zl)
-    both_other = ring(both_mine, "c", n_c, 1)
-    split_at = w_qkv.size
-    n_j = n_y * n_zl
-
-    def unpack(gathered):
-        wq = gathered[:, :split_at].reshape(n_j, *w_qkv.shape)
-        wo = jnp.transpose(gathered[:, split_at:].reshape(n_j, *w_out.shape), (1, 2, 0, 3))
-        return wq, wo
-
-    wq_mine, wo_mine = unpack(both_mine)
-    wq_other, wo_other = unpack(both_other)
+    wq_local = w_qkv.reshape(w_qkv.shape[0], -1)
+    wo_local = w_out.reshape(-1, w_out.shape[-1])
+    wq_mine = gather_seq_blocks(wq_local, n_y, n_zl)
+    wo_mine = gather_seq_blocks(wo_local, n_y, n_zl)
+    wq_other = ring(wq_mine, "c", n_c, 1)
+    wo_other = ring(wo_mine, "c", n_c, 1)
 
     partner = ring(tokens, "zh", n_zh, 1)
     pair = jnp.stack([tokens, partner])
-    received = [pair] + [ring(pair, "x", n_x, s) for s in range(1, n_x)]
-    by_shift = jnp.stack(received)
-    by_x = jnp.take(by_shift, (x - jnp.arange(n_x)) % n_x, axis=0)
+    by_x = everyone(pair, "x", n_x).reshape(n_x, *pair.shape)
     by_zh = jnp.where(zh == 0, by_x, by_x[:, ::-1])
     gathered = jnp.transpose(by_zh, (2, 1, 0, 3)).reshape(rows_here, -1)
 
@@ -159,9 +143,10 @@
     normed_v = normed.reshape(rows_here, n_y * n_zl, n_c, -1)
     normed_mine = lax.dynamic_index_in_dim(normed_v, c, axis=2, keepdims=False)
     normed_other = lax.dynamic_index_in_dim(normed_v, 1 - c, axis=2, keepdims=False)
-    qkv_sums = jnp.einsum(
-        "tjd,jdhcf->thcf", normed_mine, wq_mine, preferred_element_type=jnp.float32
-    ) + jnp.einsum("tjd,jdhcf->thcf", normed_other, wq_other, preferred_element_type=jnp.float32)
+    qkv_sums = (
+        jnp.einsum("tjd,jdo->to", normed_mine, wq_mine, preferred_element_type=jnp.float32)
+        + jnp.einsum("tjd,jdo->to", normed_other, wq_other, preferred_element_type=jnp.float32)
+    ).reshape(rows_here, *w_qkv.shape[1:])
     row_ids = first_row + jnp.arange(rows_here, dtype=jnp.int32)
     segment, inside, is_patch, grid_row, grid_col, grid_side = layout_rows(
         row_ids, offsets, grids, row_count
@@ -175,35 +160,35 @@
     values = qkv_sums[:, :, 2].astype(jnp.bfloat16)
     key_value = jnp.stack([roped_keys, values], axis=1)
     block_count = 2 * REACH + 1
-    pieces = [None] * block_count
-    pieces[REACH] = key_value
-    from_left = key_value
-    from_right = key_value
-    for distance in range(1, REACH + 1):
-        from_left = chain(from_left, SEQ, n_seq, 1)
-        from_right = chain(from_right, SEQ, n_seq, -1)
-        pieces[REACH - distance] = from_left
-        pieces[REACH + distance] = from_right
-    kv_all = jnp.concatenate(pieces, axis=0)
+    behind = key_value[None]
+    ahead = key_value[None]
+    width = 1
+    while width <= REACH:
+        behind = jnp.concatenate([chain(behind, SEQ, n_seq, width), behind], axis=0)
+        ahead = jnp.concatenate([ahead, chain(ahead, SEQ, n_seq, -width)], axis=0)
+        width *= 2
+    kv_all = jnp.concatenate(
+        [behind[behind.shape[0] - 1 - REACH :], ahead[1 : REACH + 1]], axis=0
+    ).reshape(block_count * rows_here, *key_value.shape[1:])
     key_rows = first_row - REACH * rows_here + jnp.arange(block_count * rows_here, dtype=jnp.int32)
     key_layout = layout_rows(key_rows, offsets, grids, row_count)
     attended_output = attend_all(
         query_matrix, kv_all[:, 0], kv_all[:, 1], segment, inside, key_layout[0], key_layout[1]
     )
+    attended_flat = attended_output.reshape(rows_here, -1)
     proj_mine = jnp.einsum(
-        "thf,hfjd->tjd", attended_output, wo_mine, preferred_element_type=jnp.float32
+        "tk,jkd->tjd", attended_flat, wo_mine, preferred_element_type=jnp.float32
     ).astype(jnp.bfloat16)
     proj_other = jnp.einsum(
-        "thf,hfjd->tjd", attended_output, wo_other, preferred_element_type=jnp.float32
+        "tk,jkd->tjd", attended_flat, wo_other, preferred_element_type=jnp.float32
     ).astype(jnp.bfloat16)
     first_half = jnp.where(c == 0, proj_mine, proj_other)
     second_half = jnp.where(c == 0, proj_other, proj_mine)
     share = jnp.stack([first_half, second_half], axis=2).reshape(rows_here, n_zh, n_x, -1)
 
-    total = lax.dynamic_index_in_dim(share, x, axis=2, keepdims=False).astype(jnp.float32)
-    for s in range(1, n_x):
-        outgoing = lax.dynamic_index_in_dim(share, (x + s) % n_x, axis=2, keepdims=False)
-        total = total + ring(outgoing, "x", n_x, s).astype(jnp.float32)
+    by_target = jnp.transpose(share, (2, 0, 1, 3))
+    from_peers = lax.all_to_all(by_target, "x", 0, 0, tiled=True)
+    total = jnp.sum(from_peers.astype(jnp.float32), axis=0)
     keep = lax.dynamic_index_in_dim(total, zh, axis=1, keepdims=False)
     give = lax.dynamic_index_in_dim(total, 1 - zh, axis=1, keepdims=False)
     head_share = keep + ring(give.astype(jnp.bfloat16), "zh", n_zh, 1).astype(jnp.float32)

time: 441 us -> 387 us (0.88)
  the two profiles are of different devices: /device:TPU:26 before, /device:TPU:1 now
where the time goes in v4:
time: 387 us; the launch traced here: 380 us
  waiting for transfers between devices  195 us (50%)
  starting transfers between devices  74.4 us (19%)
  blocking collectives  50.2 us (13%)
  local copies, waits for them, and re-layouts  23.4 us (6%)
  matrix products  19.9 us (5%)
  other arithmetic  16.2 us (4%)
    ppermute x7, waiting for transfers between devices, chain(): return lax.ppermute(shard, axis, pairs)  96.6 us
    all_to_all x1, blocking collectives, everyone(): return lax.all_to_all(repeated, axis, 0, 0, tiled=True)  50.2 us
    ppermute x4, waiting for transfers between devices, ring(): lax.ppermute(shard, axis, [(i, (i + by) % size) for i in range(size)])  43.1 us
    all_to_all x4, waiting for transfers between devices, everyone(): return lax.all_to_all(repeated, axis, 0, 0, tiled=True)  29.6 us
    all_to_all x1, waiting for transfers between devices, body(): from_peers = lax.all_to_all(by_target, 'x', 0, 0, tiled=True)  25.5 us
    ppermute x4, starting transfers between devices, ring(): lax.ppermute(shard, axis, [(i, (i + by) % size) for i in range(size)])  24.4 us
    ppermute x7, starting transfers between devices, chain(): return lax.ppermute(shard, axis, pairs)  23.5 us
    all_to_all x4, starting transfers between devices, everyone(): return lax.all_to_all(repeated, axis, 0, 0, tiled=True)  22.9 us
  transfers between devices with their start and end apart: 16, of which 9 were waited for; matrix products, arithmetic and copies ran while one was open for 10% of the time, Pallas kernels for 0%

profile of v4, /device:TPU:1, one launch (start us, length us, event | category | flops | bytes accessed | tf_op | source)
XLA Modules:
  0.0 379.6 jit_solution(15391573064614315053)
XLA Ops:
  1.1 50.2 %all_to_all.30 = bf16[8,64,768]{2,1,0:T(8,128)(2,1)S(1)} all-to-all(bf16[8,64,768]{2,1,0:T(8,128)(2,1)S(1)} %broadcast_in_dim.106), channel_id=1, replica_groups=mesh['y'=4,'zl'=8,'c'=2,'zh'=2,'x'=4] {'zl'}, dimensions={0} | all-to-all | bytes 1572864 | tf_op jit(solution)/shard_map/all_to_all | solution.py:105
  53.3 4.3 %all-to-all-start.2 = ((bf16[4,8,64,768]{3,2,1,0:T(8,128)(2,1)}), bf16[4,8,64,768]{3,2,1,0:T(8,128)(2,1)S(1)}, u32[]{:S(2)}, u32[]{:S(2)}) async-start(bf16[4,8,64,768]{3,2,1,0:T(8,128)(2,1)} %broadcast_in_dim.107), calls=%async_computation.2 | async-start | bytes 6291456 | tf_op jit(solution)/shard_map/all_to_all | solution.py:105
  57.6 7.9 %collective-permute-start = (bf16[256,512]{1,0:T(8,128)(2,1)S(1)}, bf16[256,512]{1,0:T(8,128)(2,1)}, u32[]{:S(2)}, u32[]{:S(2)}) collective-permute-start(bf16[256,512]{1,0:T(8,128)(2,1)S(1)} %copy-done.4), channel_id=1, source_target_pairs={{0,4},{4,0},{1,5},{5,1},{2,6},{6,2},{3,7},{7,3},{8,12},{12,8},{9,1... | collective-permute-start | bytes 786440 | tf_op jit(solution)/shard_map/ppermute | solution.py:95
  65.5 26.4 %collective-permute-done = bf16[256,512]{1,0:T(8,128)(2,1)} collective-permute-done((bf16[256,512]{1,0:T(8,128)(2,1)S(1)}, bf16[256,512]{1,0:T(8,128)(2,1)}, u32[]{:S(2)}, u32[]{:S(2)}) %collective-permute-start) | collective-permute-done | bytes 262176 | tf_op jit(solution)/shard_map/ppermute | solution.py:95
  98.7 4.0 %all-to-all-start = ((bf16[4,2,256,512]{2,3,1,0:T(8,128)(2,1)}), bf16[4,2,256,512]{2,3,1,0:T(8,128)(2,1)S(1)}, u32[]{:S(2)}, u32[]{:S(2)}) async-start(bf16[4,2,256,512]{2,3,1,0:T(8,128)(2,1)} %broadcast_in_dim.104), calls=%async_computation | async-start | bytes 4194304 | tf_op jit(solution)/shard_map/all_to_all | solution.py:105
  102.9 4.2 %collective-permute-start.1 = (bf16[32,64,768]{2,1,0:T(8,128)(2,1)}, bf16[32,64,768]{2,1,0:T(8,128)(2,1)}, u32[]{:S(2)}, u32[]{:S(2)}) collective-permute-start(bf16[32,64,768]{2,1,0:T(8,128)(2,1)} %bitcast.117), channel_id=1, source_target_pairs={{0,8},{8,0},{1,9},{9,1},{2,10},{10,2},{3,11},{11,3},{4,12},{12,4},... | collective-permute-start | bytes 9437192 | tf_op jit(solution)/shard_map/ppermute | solution.py:95
  108.6 18.2 %all-to-all-done = bf16[4,2,256,512]{2,3,1,0:T(8,128)(2,1)S(1)} async-done(((bf16[4,2,256,512]{2,3,1,0:T(8,128)(2,1)}), bf16[4,2,256,512]{2,3,1,0:T(8,128)(2,1)S(1)}, u32[]{:S(2)}, u32[]{:S(2)}) %all-to-all-start) | async-done | bytes 2097184 | tf_op jit(solution)/shard_map/all_to_all | solution.py:105
  138.8 4.4 %collective-permute-start.5 = (bf16[1,256,2,2,128]{4,1,3,2,0:T(8,128)(2,1)S(1)}, bf16[1,256,2,2,128]{4,1,3,2,0:T(8,128)(2,1)S(1)}, u32[]{:S(2)}, u32[]{:S(2)}) collective-permute-start(bf16[1,256,2,2,128]{4,1,3,2,0:T(8,128)(2,1)S(1)} %maximum_bitcast_fusion), channel_id=1, source_target_pairs={{8,0},{16,8},{24,16},{32,24},{40,32},{48,40},{56,48},{64,56},{72,6... | collective-permute-start | bytes 786440 | tf_op jit(solution)/shard_map/ppermute | solution.py:100
  144.0 11.0 %all-to-all-start.3 = ((bf16[8,256,64]{1,2,0:T(8,128)(2,1)}), bf16[8,256,64]{1,2,0:T(8,128)(2,1)S(1)}, u32[]{:S(2)}, u32[]{:S(2)}) async-start(bf16[8,256,64]{1,2,0:T(8,128)(2,1)} %broadcast_in_dim.186), calls=%async_computation.3 | async-start | bytes 524288 | tf_op jit(solution)/shard_map/all_to_all | solution.py:105
  155.9 3.4 collective-permute-start.3
  160.7 10.9 %collective-permute-done.3 = bf16[2,256,2,2,128]{4,1,3,2,0:T(8,128)(2,1)S(1)} collective-permute-done((bf16[2,256,2,2,128]{4,1,3,2,0:T(8,128)(2,1)}, bf16[2,256,2,2,128]{4,1,3,2,0:T(8,128)(2,1)S(1)}, u32[]{:S(2)}, u32[]{:S(2)}) %collective-permute-start.3) | collective-permute-done | bytes 524320 | tf_op jit(solution)/shard_map/ppermute | solution.py:100
  171.6 16.8 %collective-permute-done.6 = bf16[2,256,2,2,128]{4,1,3,2,0:T(8,128)(2,1)S(1)} collective-permute-done((bf16[2,256,2,2,128]{4,1,3,2,0:T(8,128)(2,1)S(1)}, bf16[2,256,2,2,128]{4,1,3,2,0:T(8,128)(2,1)S(1)}, u32[]{:S(2)}, u32[]{:S(2)}) %collective-permute-start.6) | collective-permute-done | bytes 524320 | tf_op jit(solution)/shard_map/ppermute | solution.py:100
  190.0 8.7 %collective-permute-start.4 = (bf16[4,256,2,2,128]{4,1,3,2,0:T(8,128)(2,1)}, bf16[4,256,2,2,128]{4,1,3,2,0:T(8,128)(2,1)}, u32[]{:S(2)}, u32[]{:S(2)}) collective-permute-start(bf16[4,256,2,2,128]{4,1,3,2,0:T(8,128)(2,1)} %get-tuple-element.25), channel_id=1, source_target_pairs={{0,32},{8,40},{16,48},{24,56},{32,64},{40,72},{48,80},{56,88},{64,... | collective-permute-start | bytes 3145736 | tf_op jit(solution)/shard_map/ppermute | solution.py:100
  199.8 3.5 all-to-all-start.4
  206.5 11.3 %all-to-all-done.4 = bf16[4,8,256,64]{2,3,1,0:T(8,128)(2,1)S(1)} async-done(((bf16[4,8,256,64]{2,3,1,0:T(8,128)(2,1)}), bf16[4,8,256,64]{2,3,1,0:T(8,128)(2,1)S(1)}, u32[]{:S(2)}, u32[]{:S(2)}) %all-to-all-start.4) | async-done | bytes 1048608 | tf_op jit(solution)/shard_map/all_to_all | solution.py:105
  217.8 3.6 collective-permute-start.8
  223.2 66.1 %collective-permute-done.7 = bf16[4,256,2,2,128]{4,1,3,2,0:T(8,128)(2,1)} collective-permute-done((bf16[4,256,2,2,128]{4,1,3,2,0:T(8,128)(2,1)}, bf16[4,256,2,2,128]{4,1,3,2,0:T(8,128)(2,1)}, u32[]{:S(2)}, u32[]{:S(2)}) %collective-permute-start.7) | collective-permute-done | bytes 1048608 | tf_op jit(solution)/shard_map/ppermute | solution.py:100
  293.0 8.6 %fusion.41 = (f32[2,256]{1,0:T(2,128)S(1)}, f32[2,256,3840]{2,1,0:T(8,128)}) fusion(pred[256,3840]{1,0:T(8,128)(4,1)S(1)} %copy-done.6, bf16[3840,2,2,128]{3,0,2,1:T(8,128)(2,1)} %bitcast.115, bf16[256,2,32]{2,0,1:T(8,128)(2,1)S(1)} %copy-done.8, bf16[256,2,32]{2,0,1:T(8,128)(2,1)S(1)} %copy-done.9, bf16[256,2,32]{2,0,1:T(8,128)(2,1)S(1)} %get-tuple-element.28, ...), kind=kOutput, calls=%fused_computation.126 | convolution fusion | flops 513675008 | bytes 12322816 | tf_op jit(solution)/shard_map/sub | solution.py:79
  301.6 5.3 %fusion.10 = bf16[2,128,256]{2,1,0:T(8,128)(2,1)S(1)} fusion(f32[2,256,3840]{2,1,0:T(8,128)} %get-tuple-element.47, f32[2,256]{1,0:T(2,128)S(1)} %broadcast_select_fusion, bf16[3840,2,2,128]{3,0,2,1:T(8,128)(2,1)} %bitcast.116, pred[256]{0:T(512)(128)(4,1)S(1)} %get-tuple-element.11), kind=kOutput, calls=%fused_computation.24 | convolution fusion | flops 507379712 | bytes 9963776 | tf_op jit(solution)/shard_map/vgm,mvb->gvb/dot_general | solution.py:83
  311.2 3.6 all-to-all-start.5
  315.2 25.5 %all-to-all-done.5 = bf16[4,256,2,512]{1,3,2,0:T(8,128)(2,1)S(1)} async-done(((bf16[4,256,2,512]{1,3,2,0:T(8,128)(2,1)}), bf16[4,256,2,512]{1,3,2,0:T(8,128)(2,1)S(1)}, u32[]{:S(2)}, u32[]{:S(2)}) %all-to-all-start.5) | async-done | bytes 2097184 | tf_op jit(solution)/shard_map/all_to_all | solution.py:190
  341.2 8.7 %collective-permute-start.9 = (bf16[256,512]{1,0:T(8,128)(2,1)S(1)}, bf16[256,512]{1,0:T(8,128)(2,1)S(1)}, u32[]{:S(2)}, u32[]{:S(2)}) collective-permute-start(bf16[256,512]{1,0:T(8,128)(2,1)S(1)} %bitcast.126), channel_id=1, source_target_pairs={{0,4},{4,0},{1,5},{5,1},{2,6},{6,2},{3,7},{7,3},{8,12},{12,8},{9,1... | collective-permute-start | bytes 786440 | tf_op jit(solution)/shard_map/ppermute | solution.py:95
  350.2 16.8 %collective-permute-done.9 = bf16[256,512]{1,0:T(8,128)(2,1)S(1)} collective-permute-done((bf16[256,512]{1,0:T(8,128)(2,1)S(1)}, bf16[256,512]{1,0:T(8,128)(2,1)S(1)}, u32[]{:S(2)}, u32[]{:S(2)}) %collective-permute-start.9) | collective-permute-done | bytes 262176 | tf_op jit(solution)/shard_map/ppermute | solution.py:95
  372.5 4.0 %gather_fusion = bf16[1024,512]{1,0:T(8,128)(2,1)S(1)} fusion(bf16[304,512]{1,0:T(8,128)(2,1)S(1)} %pad_maximum_fusion.6, s32[1024]{0:T(1024)S(1)} %broadcast_clamp_fusion), kind=kCustom, calls=%fused_computation | custom fusion | bytes 2101248 | tf_op jit(solution)/shard_map/jit(_take)/gather | solution.py:205
  (122 shorter events, 51.4 us)
Async XLA Ops:
  0.0 143.2 %copy-start = (bf16[2,128,64]{1,2,0:T(8,128)(2,1)S(1)}, bf16[2,128,64]{1,2,0:T(8,128)(2,1)}, u32[]{:S(2)}) copy-start(bf16[2,128,64]{1,2,0:T(8,128)(2,1)} %param.12) | copy-start | bytes 98308
  53.3 42.5 %all-to-all-start.2 = ((bf16[4,8,64,768]{3,2,1,0:T(8,128)(2,1)}), bf16[4,8,64,768]{3,2,1,0:T(8,128)(2,1)S(1)}, u32[]{:S(2)}, u32[]{:S(2)}) async-start(bf16[4,8,64,768]{3,2,1,0:T(8,128)(2,1)} %broadcast_in_dim.107), calls=%async_computation.2 | async-start | bytes 6291456 | tf_op jit(solution)/shard_map/all_to_all | solution.py:105
  57.6 34.3 %collective-permute-start = (bf16[256,512]{1,0:T(8,128)(2,1)S(1)}, bf16[256,512]{1,0:T(8,128)(2,1)}, u32[]{:S(2)}, u32[]{:S(2)}) collective-permute-start(bf16[256,512]{1,0:T(8,128)(2,1)S(1)} %copy-done.4), channel_id=1, source_target_pairs={{0,4},{4,0},{1,5},{5,1},{2,6},{6,2},{3,7},{7,3},{8,12},{12,8},{9,1... | collective-permute-start | bytes 786440 | tf_op jit(solution)/shard_map/ppermute | solution.py:95
  93.7 9.0 %copy-start.13 = (s32[15]{0:T(128)S(1)}, s32[15]{0:T(128)}, u32[]{:S(2)}) copy-start(s32[15]{0:T(128)} %param.15) | copy-start | bytes 184
  93.7 13.4 %copy-start.10 = (f32[4096]{0:T(1024)S(1)}, f32[4096]{0:T(1024)}, u32[]{:S(2)}) copy-start(f32[4096]{0:T(1024)} %param.10) | copy-start | bytes 49156
  93.7 13.5 %copy-start.11 = (f32[4096]{0:T(1024)S(1)}, f32[4096]{0:T(1024)}, u32[]{:S(2)}) copy-start(f32[4096]{0:T(1024)} %param.9) | copy-start | bytes 49156
  93.7 13.6 %copy-start.14 = (s32[14]{0:T(128)S(1)}, s32[14]{0:T(128)}, u32[]{:S(2)}) copy-start(s32[14]{0:T(128)} %param.14) | copy-start | bytes 172
  98.7 28.1 %all-to-all-start = ((bf16[4,2,256,512]{2,3,1,0:T(8,128)(2,1)}), bf16[4,2,256,512]{2,3,1,0:T(8,128)(2,1)S(1)}, u32[]{:S(2)}, u32[]{:S(2)}) async-start(bf16[4,2,256,512]{2,3,1,0:T(8,128)(2,1)} %broadcast_in_dim.104), calls=%async_computation | async-start | bytes 4194304 | tf_op jit(solution)/shard_map/all_to_all | solution.py:105
  102.9 28.7 %collective-permute-start.1 = (bf16[32,64,768]{2,1,0:T(8,128)(2,1)}, bf16[32,64,768]{2,1,0:T(8,128)(2,1)}, u32[]{:S(2)}, u32[]{:S(2)}) collective-permute-start(bf16[32,64,768]{2,1,0:T(8,128)(2,1)} %bitcast.117), channel_id=1, source_target_pairs={{0,8},{8,0},{1,9},{9,1},{2,10},{10,2},{3,11},{11,3},{4,12},{12,4},... | collective-permute-start | bytes 9437192 | tf_op jit(solution)/shard_map/ppermute | solution.py:95
  136.8 18.2 %collective-permute-start.2 = (bf16[1,256,2,2,128]{4,1,3,2,0:T(8,128)(2,1)S(1)}, bf16[1,256,2,2,128]{4,1,3,2,0:T(8,128)(2,1)S(1)}, u32[]{:S(2)}, u32[]{:S(2)}) collective-permute-start(bf16[1,256,2,2,128]{4,1,3,2,0:T(8,128)(2,1)S(1)} %maximum_bitcast_fusion), channel_id=1, source_target_pairs={{0,8},{8,16},{16,24},{24,32},{32,40},{40,48},{48,56},{56,64},{64,7... | collective-permute-start | bytes 786440 | tf_op jit(solution)/shard_map/ppermute | solution.py:100
  138.8 16.2 %collective-permute-start.5 = (bf16[1,256,2,2,128]{4,1,3,2,0:T(8,128)(2,1)S(1)}, bf16[1,256,2,2,128]{4,1,3,2,0:T(8,128)(2,1)S(1)}, u32[]{:S(2)}, u32[]{:S(2)}) collective-permute-start(bf16[1,256,2,2,128]{4,1,3,2,0:T(8,128)(2,1)S(1)} %maximum_bitcast_fusion), channel_id=1, source_target_pairs={{8,0},{16,8},{24,16},{32,24},{40,32},{48,40},{56,48},{64,56},{72,6... | collective-permute-start | bytes 786440 | tf_op jit(solution)/shard_map/ppermute | solution.py:100
  144.0 54.8 %all-to-all-start.3 = ((bf16[8,256,64]{1,2,0:T(8,128)(2,1)}), bf16[8,256,64]{1,2,0:T(8,128)(2,1)S(1)}, u32[]{:S(2)}, u32[]{:S(2)}) async-start(bf16[8,256,64]{1,2,0:T(8,128)(2,1)} %broadcast_in_dim.186), calls=%async_computation.3 | async-start | bytes 524288 | tf_op jit(solution)/shard_map/all_to_all | solution.py:105
  155.9 15.7 %collective-permute-start.3 = (bf16[2,256,2,2,128]{4,1,3,2,0:T(8,128)(2,1)}, bf16[2,256,2,2,128]{4,1,3,2,0:T(8,128)(2,1)S(1)}, u32[]{:S(2)}, u32[]{:S(2)}) collective-permute-start(bf16[2,256,2,2,128]{4,1,3,2,0:T(8,128)(2,1)} %get-tuple-element.27), channel_id=1, source_target_pairs={{0,16},{8,24},{16,32},{24,40},{32,48},{40,56},{48,64},{56,72},{64,... | collective-permute-start | bytes 1572872 | tf_op jit(solution)/shard_map/ppermute | solution.py:100
  159.3 29.2 %collective-permute-start.6 = (bf16[2,256,2,2,128]{4,1,3,2,0:T(8,128)(2,1)S(1)}, bf16[2,256,2,2,128]{4,1,3,2,0:T(8,128)(2,1)S(1)}, u32[]{:S(2)}, u32[]{:S(2)}) collective-permute-start(bf16[2,256,2,2,128]{4,1,3,2,0:T(8,128)(2,1)S(1)} %get-tuple-element.26), channel_id=1, source_target_pairs={{16,0},{24,8},{32,16},{40,24},{48,32},{56,40},{64,48},{72,56},{80,... | collective-permute-start | bytes 1572872 | tf_op jit(solution)/shard_map/ppermute | solution.py:100
  190.0 31.4 %collective-permute-start.4 = (bf16[4,256,2,2,128]{4,1,3,2,0:T(8,128)(2,1)}, bf16[4,256,2,2,128]{4,1,3,2,0:T(8,128)(2,1)}, u32[]{:S(2)}, u32[]{:S(2)}) collective-permute-start(bf16[4,256,2,2,128]{4,1,3,2,0:T(8,128)(2,1)} %get-tuple-element.25), channel_id=1, source_target_pairs={{0,32},{8,40},{16,48},{24,56},{32,64},{40,72},{48,80},{56,88},{64,... | collective-permute-start | bytes 3145736 | tf_op jit(solution)/shard_map/ppermute | solution.py:100
  199.8 18.0 %all-to-all-start.4 = ((bf16[4,8,256,64]{2,3,1,0:T(8,128)(2,1)}), bf16[4,8,256,64]{2,3,1,0:T(8,128)(2,1)S(1)}, u32[]{:S(2)}, u32[]{:S(2)}) async-start(bf16[4,8,256,64]{2,3,1,0:T(8,128)(2,1)} %broadcast_in_dim.187), calls=%async_computation.4 | async-start | bytes 2097152 | tf_op jit(solution)/shard_map/all_to_all | solution.py:105
  203.4 86.0 %collective-permute-start.7 = (bf16[4,256,2,2,128]{4,1,3,2,0:T(8,128)(2,1)}, bf16[4,256,2,2,128]{4,1,3,2,0:T(8,128)(2,1)}, u32[]{:S(2)}, u32[]{:S(2)}) collective-permute-start(bf16[4,256,2,2,128]{4,1,3,2,0:T(8,128)(2,1)} %get-tuple-element.24), channel_id=1, source_target_pairs={{32,0},{40,8},{48,16},{56,24},{64,32},{72,40},{80,48},{88,56},{96,... | collective-permute-start | bytes 3145736 | tf_op jit(solution)/shard_map/ppermute | solution.py:100
  217.8 89.6 %collective-permute-start.8 = (bf16[32,256,64]{1,2,0:T(8,128)(2,1)S(1)}, bf16[32,256,64]{1,2,0:T(8,128)(2,1)}, u32[]{:S(2)}, u32[]{:S(2)}) collective-permute-start(bf16[32,256,64]{1,2,0:T(8,128)(2,1)S(1)} %bitcast.113), channel_id=1, source_target_pairs={{0,8},{8,0},{1,9},{9,1},{2,10},{10,2},{3,11},{11,3},{4,12},{12,4},... | collective-permute-start | bytes 3145736 | tf_op jit(solution)/shard_map/ppermute | solution.py:95
  311.2 29.5 %all-to-all-start.5 = ((bf16[4,256,2,512]{1,3,2,0:T(8,128)(2,1)}), bf16[4,256,2,512]{1,3,2,0:T(8,128)(2,1)S(1)}, u32[]{:S(2)}, u32[]{:S(2)}) async-start(bf16[4,256,2,512]{1,3,2,0:T(8,128)(2,1)} %copy.78), calls=%async_computation.5 | async-start | bytes 4194304 | tf_op jit(solution)/shard_map/all_to_all | solution.py:190
  314.8 52.1 %copy-start.5 = (bf16[256,512]{1,0:T(8,128)(2,1)S(1)}, bf16[256,512]{1,0:T(8,128)(2,1)}, u32[]{:S(2)}) copy-start(bf16[256,512]{1,0:T(8,128)(2,1)} %param.8) | copy-start | bytes 786436
  314.8 52.1 %copy-start.12 = (f32[512]{0:T(512)S(1)}, f32[512]{0:T(512)}, u32[]{:S(2)}) copy-start(f32[512]{0:T(512)} %param.13) | copy-start | bytes 6148
  341.2 25.7 %collective-permute-start.9 = (bf16[256,512]{1,0:T(8,128)(2,1)S(1)}, bf16[256,512]{1,0:T(8,128)(2,1)S(1)}, u32[]{:S(2)}, u32[]{:S(2)}) collective-permute-start(bf16[256,512]{1,0:T(8,128)(2,1)S(1)} %bitcast.126), channel_id=1, source_target_pairs={{0,4},{4,0},{1,5},{5,1},{2,6},{6,2},{3,7},{7,3},{8,12},{12,8},{9,1... | collective-permute-start | bytes 786440 | tf_op jit(solution)/shard_map/ppermute | solution.py:95
  367.1 5.4 %collective-permute-start.10 = (bf16[48,512]{1,0:T(8,128)(2,1)S(1)}, bf16[48,512]{1,0:T(8,128)(2,1)S(1)}, u32[]{:S(2)}, u32[]{:S(2)}) collective-permute-start(bf16[48,512]{1,0:T(8,128)(2,1)S(1)} %slice.95), channel_id=1, source_target_pairs={{8,0},{16,8},{24,16},{32,24},{40,32},{48,40},{56,48},{64,56},{72,6... | collective-permute-start | bytes 147464 | tf_op jit(solution)/shard_map/ppermute | solution.py:100
  372.5 7.1 %copy-start.1 = (bf16[2,128,64]{1,2,0:T(8,128)(2,1)S(1)}, bf16[2,128,64]{1,2,0:T(8,128)(2,1)}, u32[]{:S(2)}) copy-start(bf16[2,128,64]{1,2,0:T(8,128)(2,1)} %param.12) | copy-start | bytes 98308
  (7 other events, 18.0 us)

commit v5 on v4

--- a/solution.py
+++ b/solution.py
@@ -160,16 +160,12 @@
     values = qkv_sums[:, :, 2].astype(jnp.bfloat16)
     key_value = jnp.stack([roped_keys, values], axis=1)
     block_count = 2 * REACH + 1
-    behind = key_value[None]
-    ahead = key_value[None]
-    width = 1
-    while width <= REACH:
-        behind = jnp.concatenate([chain(behind, SEQ, n_seq, width), behind], axis=0)
-        ahead = jnp.concatenate([ahead, chain(ahead, SEQ, n_seq, -width)], axis=0)
-        width *= 2
-    kv_all = jnp.concatenate(
-        [behind[behind.shape[0] - 1 - REACH :], ahead[1 : REACH + 1]], axis=0
-    ).reshape(block_count * rows_here, *key_value.shape[1:])
+    behind = [key_value]
+    ahead = [key_value]
+    for _ in range(REACH):
+        behind.insert(0, chain(behind[0], SEQ, n_seq, 1))
+        ahead.append(chain(ahead[-1], SEQ, n_seq, -1))
+    kv_all = jnp.concatenate(behind + ahead[1:], axis=0)
     key_rows = first_row - REACH * rows_here + jnp.arange(block_count * rows_here, dtype=jnp.int32)
     key_layout = layout_rows(key_rows, offsets, grids, row_count)
     attended_output = attend_all(

time: 387 us -> 353 us (0.912)
  waiting for transfers between devices: 195 us -> 93.2 us
  starting transfers between devices: 74.4 us -> 140 us
  local copies, waits for them, and re-layouts: 23.4 us -> 30.2 us
    ppermute x7 -> x15, waiting for transfers between devices: 96.6 us -> 9.45 us  [chain(): return lax.ppermute(shard, axis, pairs)]
    all_to_all x4, starting transfers between devices: 22.9 us -> 53.3 us  [everyone(): return lax.all_to_all(repeated, axis, 0, 0, tiled=True)]
    ppermute x7 -> x15, starting transfers between devices: 23.5 us -> 51.5 us  [chain(): return lax.ppermute(shard, axis, pairs)]
    all_to_all x4, waiting for transfers between devices: 29.6 us -> 17.4 us  [everyone(): return lax.all_to_all(repeated, axis, 0, 0, tiled=True)]
    unnamed x40 -> x60, local copies, waits for them, and re-layouts: 3.47 us -> 13.8 us
    ppermute x4, starting transfers between devices: 24.4 us -> 31.8 us  [ring(): lax.ppermute(shard, axis, [(i, (i + by) % size) for i in range(size)])]
  transfers between devices with their start and end apart: 16 -> 24, of which waited for: 9 -> 8; matrix products, arithmetic and copies ran while one was open for 10% -> 12% of each run, Pallas kernels for 0% -> 0%
where the time goes in v5:
time: 353 us; the launch traced here: 349 us
  starting transfers between devices  140 us (40%)
  waiting for transfers between devices  93.2 us (26%)
  blocking collectives  50.2 us (14%)
  local copies, waits for them, and re-layouts  30.2 us (9%)
  matrix products  19.4 us (5%)
  other arithmetic  14.6 us (4%)
    all_to_all x4, starting transfers between devices, everyone(): return lax.all_to_all(repeated, axis, 0, 0, tiled=True)  53.3 us
    ppermute x15, starting transfers between devices, chain(): return lax.ppermute(shard, axis, pairs)  51.5 us
    all_to_all x1, blocking collectives, everyone(): return lax.all_to_all(repeated, axis, 0, 0, tiled=True)  50.2 us
    ppermute x4, waiting for transfers between devices, ring(): lax.ppermute(shard, axis, [(i, (i + by) % size) for i in range(size)])  40.1 us
    ppermute x4, starting transfers between devices, ring(): lax.ppermute(shard, axis, [(i, (i + by) % size) for i in range(size)])  31.8 us
    all_to_all x1, waiting for transfers between devices, body(): from_peers = lax.all_to_all(by_target, 'x', 0, 0, tiled=True)  26.2 us
    all_to_all x4, waiting for transfers between devices, everyone(): return lax.all_to_all(repeated, axis, 0, 0, tiled=True)  17.4 us
    unnamed x60, local copies, waits for them, and re-layouts  13.8 us
  transfers between devices with their start and end apart: 24, of which 8 were waited for; matrix products, arithmetic and copies ran while one was open for 12% of the time, Pallas kernels for 0%

profile of v5, /device:TPU:1, one launch (start us, length us, event | category | flops | bytes accessed | tf_op | source)
XLA Modules:
  0.0 348.7 jit_solution(9709215359215064589)
XLA Ops:
  1.1 50.2 %all_to_all.30 = bf16[8,64,768]{2,1,0:T(8,128)(2,1)S(1)} all-to-all(bf16[8,64,768]{2,1,0:T(8,128)(2,1)S(1)} %broadcast_in_dim.104), channel_id=1, replica_groups=mesh['y'=4,'zl'=8,'c'=2,'zh'=2,'x'=4] {'zl'}, dimensions={0} | all-to-all | bytes 1572864 | tf_op jit(solution)/shard_map/all_to_all | solution.py:105
  53.3 4.3 %all-to-all-start.2 = ((bf16[4,8,64,768]{3,2,1,0:T(8,128)(2,1)}), bf16[4,8,64,768]{3,2,1,0:T(8,128)(2,1)S(1)}, u32[]{:S(2)}, u32[]{:S(2)}) async-start(bf16[4,8,64,768]{3,2,1,0:T(8,128)(2,1)} %broadcast_in_dim.105), calls=%async_computation.2 | async-start | bytes 6291456 | tf_op jit(solution)/shard_map/all_to_all | solution.py:105
  57.6 7.9 %collective-permute-start = (bf16[256,512]{1,0:T(8,128)(2,1)S(1)}, bf16[256,512]{1,0:T(8,128)(2,1)}, u32[]{:S(2)}, u32[]{:S(2)}) collective-permute-start(bf16[256,512]{1,0:T(8,128)(2,1)S(1)} %copy-done.4), channel_id=1, source_target_pairs={{0,4},{4,0},{1,5},{5,1},{2,6},{6,2},{3,7},{7,3},{8,12},{12,8},{9,1... | collective-permute-start | bytes 786440 | tf_op jit(solution)/shard_map/ppermute | solution.py:95
  65.5 26.4 %collective-permute-done = bf16[256,512]{1,0:T(8,128)(2,1)} collective-permute-done((bf16[256,512]{1,0:T(8,128)(2,1)S(1)}, bf16[256,512]{1,0:T(8,128)(2,1)}, u32[]{:S(2)}, u32[]{:S(2)}) %collective-permute-start) | collective-permute-done | bytes 262176 | tf_op jit(solution)/shard_map/ppermute | solution.py:95
  98.7 4.0 %all-to-all-start = ((bf16[4,2,256,512]{2,3,1,0:T(8,128)(2,1)}), bf16[4,2,256,512]{2,3,1,0:T(8,128)(2,1)S(1)}, u32[]{:S(2)}, u32[]{:S(2)}) async-start(bf16[4,2,256,512]{2,3,1,0:T(8,128)(2,1)} %broadcast_in_dim.102), calls=%async_computation | async-start | bytes 4194304 | tf_op jit(solution)/shard_map/all_to_all | solution.py:105
  102.9 4.2 %collective-permute-start.1 = (bf16[32,64,768]{2,1,0:T(8,128)(2,1)}, bf16[32,64,768]{2,1,0:T(8,128)(2,1)}, u32[]{:S(2)}, u32[]{:S(2)}) collective-permute-start(bf16[32,64,768]{2,1,0:T(8,128)(2,1)} %bitcast.110), channel_id=1, source_target_pairs={{0,8},{8,0},{1,9},{9,1},{2,10},{10,2},{3,11},{11,3},{4,12},{12,4},... | collective-permute-start | bytes 9437192 | tf_op jit(solution)/shard_map/ppermute | solution.py:95
  109.4 17.4 %all-to-all-done = bf16[4,2,256,512]{2,3,1,0:T(8,128)(2,1)S(1)} async-done(((bf16[4,2,256,512]{2,3,1,0:T(8,128)(2,1)}), bf16[4,2,256,512]{2,3,1,0:T(8,128)(2,1)S(1)}, u32[]{:S(2)}, u32[]{:S(2)}) %all-to-all-start) | async-done | bytes 2097184 | tf_op jit(solution)/shard_map/all_to_all | solution.py:105
  138.9 4.4 %collective-permute-start.9 = (bf16[256,2,2,128]{3,0,2,1:T(8,128)(2,1)S(1)}, bf16[256,2,2,128]{3,0,2,1:T(8,128)(2,1)S(1)}, u32[]{:S(2)}, u32[]{:S(2)}) collective-permute-start(bf16[256,2,2,128]{3,0,2,1:T(8,128)(2,1)S(1)} %pad_maximum_fusion.3), channel_id=1, source_target_pairs={{8,0},{16,8},{24,16},{32,24},{40,32},{48,40},{56,48},{64,56},{72,6... | collective-permute-start | bytes 786440 | tf_op jit(solution)/shard_map/ppermute | solution.py:100
  143.3 3.2 collective-permute-start.3
  149.8 4.4 %collective-permute-start.4 = (bf16[256,2,2,128]{3,0,2,1:T(8,128)(2,1)S(1)}, bf16[256,2,2,128]{3,0,2,1:T(8,128)(2,1)S(1)}, u32[]{:S(2)}, u32[]{:S(2)}) collective-permute-start(bf16[256,2,2,128]{3,0,2,1:T(8,128)(2,1)S(1)} %collective-permute-done.3), channel_id=1, source_target_pairs={{0,8},{8,16},{16,24},{24,32},{32,40},{40,48},{48,56},{56,64},{64,7... | collective-permute-start | bytes 786440 | tf_op jit(solution)/shard_map/ppermute | solution.py:100
  155.0 30.1 %all-to-all-start.3 = ((bf16[8,256,64]{1,2,0:T(8,128)(2,1)}), bf16[8,256,64]{1,2,0:T(8,128)(2,1)S(1)}, u32[]{:S(2)}, u32[]{:S(2)}) async-start(bf16[8,256,64]{1,2,0:T(8,128)(2,1)} %broadcast_in_dim.181), calls=%async_computation.3 | async-start | bytes 524288 | tf_op jit(solution)/shard_map/all_to_all | solution.py:105
  187.0 3.6 %collective-permute-start.5 = (bf16[256,2,2,128]{3,0,2,1:T(8,128)(2,1)S(1)}, bf16[256,2,2,128]{3,0,2,1:T(8,128)(2,1)S(1)}, u32[]{:S(2)}, u32[]{:S(2)}) collective-permute-start(bf16[256,2,2,128]{3,0,2,1:T(8,128)(2,1)S(1)} %collective-permute-done.4), channel_id=1, source_target_pairs={{0,8},{8,16},{16,24},{24,32},{32,40},{40,48},{48,56},{56,64},{64,7... | collective-permute-start | bytes 786440 | tf_op jit(solution)/shard_map/ppermute | solution.py:100
  195.7 3.6 %collective-permute-start.6 = (bf16[256,2,2,128]{3,0,2,1:T(8,128)(2,1)S(1)}, bf16[256,2,2,128]{3,0,2,1:T(8,128)(2,1)}, u32[]{:S(2)}, u32[]{:S(2)}) collective-permute-start(bf16[256,2,2,128]{3,0,2,1:T(8,128)(2,1)S(1)} %collective-permute-done.5), channel_id=1, source_target_pairs={{0,8},{8,16},{16,24},{24,32},{32,40},{40,48},{48,56},{56,64},{64,7... | collective-permute-start | bytes 786440 | tf_op jit(solution)/shard_map/ppermute | solution.py:100
  203.5 3.7 %collective-permute-start.7 = (bf16[256,2,2,128]{3,0,2,1:T(8,128)(2,1)}, bf16[256,2,2,128]{3,0,2,1:T(8,128)(2,1)}, u32[]{:S(2)}, u32[]{:S(2)}) collective-permute-start(bf16[256,2,2,128]{3,0,2,1:T(8,128)(2,1)} %collective-permute-done.6), channel_id=1, source_target_pairs={{0,8},{8,16},{16,24},{24,32},{32,40},{40,48},{48,56},{56,64},{64,7... | collective-permute-start | bytes 786440 | tf_op jit(solution)/shard_map/ppermute | solution.py:100
  208.4 14.9 %all-to-all-start.4 = ((bf16[4,8,256,64]{2,3,1,0:T(8,128)(2,1)}), bf16[4,8,256,64]{2,3,1,0:T(8,128)(2,1)S(1)}, u32[]{:S(2)}, u32[]{:S(2)}) async-start(bf16[4,8,256,64]{2,3,1,0:T(8,128)(2,1)} %broadcast_in_dim.182), calls=%async_computation.4 | async-start | bytes 2097152 | tf_op jit(solution)/shard_map/all_to_all | solution.py:105
  223.3 12.5 %collective-permute-start.14 = (bf16[256,2,2,128]{3,0,2,1:T(8,128)(2,1)}, bf16[256,2,2,128]{3,0,2,1:T(8,128)(2,1)}, u32[]{:S(2)}, u32[]{:S(2)}) collective-permute-start(bf16[256,2,2,128]{3,0,2,1:T(8,128)(2,1)} %collective-permute-done.13), channel_id=1, source_target_pairs={{8,0},{16,8},{24,16},{32,24},{40,32},{48,40},{56,48},{64,56},{72,6... | collective-permute-start | bytes 786440 | tf_op jit(solution)/shard_map/ppermute | solution.py:100
  239.7 10.0 %collective-permute-start.16 = (bf16[32,256,64]{1,2,0:T(8,128)(2,1)S(1)}, bf16[32,256,64]{1,2,0:T(8,128)(2,1)S(1)}, u32[]{:S(2)}, u32[]{:S(2)}) collective-permute-start(bf16[32,256,64]{1,2,0:T(8,128)(2,1)S(1)} %bitcast.108), channel_id=1, source_target_pairs={{0,8},{8,0},{1,9},{9,1},{2,10},{10,2},{3,11},{11,3},{4,12},{12,4},... | collective-permute-start | bytes 3145736 | tf_op jit(solution)/shard_map/ppermute | solution.py:95
  264.0 9.3 %fusion.41 = (f32[2,256]{1,0:T(2,128)S(1)}, f32[2,256,3840]{2,1,0:T(8,128)}) fusion(pred[256,3840]{1,0:T(8,128)(4,1)} %compare_and_fusion, bf16[3840,2,2,128]{3,0,2,1:T(8,128)(2,1)} %copy-done.15, bf16[256,2,32]{2,0,1:T(8,128)(2,1)} %get-tuple-element.26, bf16[256,2,32]{2,0,1:T(8,128)(2,1)} %get-tuple-element.27, ...), kind=kOutput, calls=%fused_computation.130 | convolution fusion | flops 513675008 | bytes 12224512 | tf_op jit(solution)/shard_map/sub | solution.py:79
  273.3 5.4 %fusion.10 = bf16[2,128,256]{2,1,0:T(8,128)(2,1)S(1)} fusion(f32[2,256,3840]{2,1,0:T(8,128)} %get-tuple-element.43, f32[2,256]{1,0:T(2,128)S(1)} %broadcast_select_fusion, bf16[3840,2,2,128]{3,0,2,1:T(8,128)(2,1)} %copy-done.15, pred[256]{0:T(512)(128)(4,1)S(1)} %get-tuple-element.11), kind=kOutput, calls=%fused_computation.24 | convolution fusion | flops 507379712 | bytes 9963776 | tf_op jit(solution)/shard_map/vgm,mvb->gvb/dot_general | solution.py:83
  281.7 3.6 %all-to-all-start.5 = ((bf16[4,256,2,512]{1,3,2,0:T(8,128)(2,1)}), bf16[4,256,2,512]{1,3,2,0:T(8,128)(2,1)S(1)}, u32[]{:S(2)}, u32[]{:S(2)}) async-start(bf16[4,256,2,512]{1,3,2,0:T(8,128)(2,1)} %copy.73), calls=%async_computation.5 | async-start | bytes 4194304 | tf_op jit(solution)/shard_map/all_to_all | solution.py:186
  285.7 26.2 %all-to-all-done.5 = bf16[4,256,2,512]{1,3,2,0:T(8,128)(2,1)S(1)} async-done(((bf16[4,256,2,512]{1,3,2,0:T(8,128)(2,1)}), bf16[4,256,2,512]{1,3,2,0:T(8,128)(2,1)S(1)}, u32[]{:S(2)}, u32[]{:S(2)}) %all-to-all-start.5) | async-done | bytes 2097184 | tf_op jit(solution)/shard_map/all_to_all | solution.py:186
  312.3 9.7 %collective-permute-start.17 = (bf16[256,512]{1,0:T(8,128)(2,1)S(1)}, bf16[256,512]{1,0:T(8,128)(2,1)S(1)}, u32[]{:S(2)}, u32[]{:S(2)}) collective-permute-start(bf16[256,512]{1,0:T(8,128)(2,1)S(1)} %bitcast.120), channel_id=1, source_target_pairs={{0,4},{4,0},{1,5},{5,1},{2,6},{6,2},{3,7},{7,3},{8,12},{12,8},{9,1... | collective-permute-start | bytes 786440 | tf_op jit(solution)/shard_map/ppermute | solution.py:95
  322.3 13.7 %collective-permute-done.17 = bf16[256,512]{1,0:T(8,128)(2,1)S(1)} collective-permute-done((bf16[256,512]{1,0:T(8,128)(2,1)S(1)}, bf16[256,512]{1,0:T(8,128)(2,1)S(1)}, u32[]{:S(2)}, u32[]{:S(2)}) %collective-permute-start.17) | collective-permute-done | bytes 262176 | tf_op jit(solution)/shard_map/ppermute | solution.py:95
  341.6 4.0 %gather_fusion = bf16[1024,512]{1,0:T(8,128)(2,1)S(1)} fusion(bf16[304,512]{1,0:T(8,128)(2,1)S(1)} %pad_maximum_fusion.2, s32[1024]{0:T(1024)S(1)} %broadcast_clamp_fusion), kind=kCustom, calls=%fused_computation | custom fusion | bytes 2101248 | tf_op jit(solution)/shard_map/jit(_take)/gather | solution.py:201
  (155 shorter events, 71.2 us)
Async XLA Ops:
  53.3 42.5 %all-to-all-start.2 = ((bf16[4,8,64,768]{3,2,1,0:T(8,128)(2,1)}), bf16[4,8,64,768]{3,2,1,0:T(8,128)(2,1)S(1)}, u32[]{:S(2)}, u32[]{:S(2)}) async-start(bf16[4,8,64,768]{3,2,1,0:T(8,128)(2,1)} %broadcast_in_dim.105), calls=%async_computation.2 | async-start | bytes 6291456 | tf_op jit(solution)/shard_map/all_to_all | solution.py:105
  57.6 34.3 %collective-permute-start = (bf16[256,512]{1,0:T(8,128)(2,1)S(1)}, bf16[256,512]{1,0:T(8,128)(2,1)}, u32[]{:S(2)}, u32[]{:S(2)}) collective-permute-start(bf16[256,512]{1,0:T(8,128)(2,1)S(1)} %copy-done.4), channel_id=1, source_target_pairs={{0,4},{4,0},{1,5},{5,1},{2,6},{6,2},{3,7},{7,3},{8,12},{12,8},{9,1... | collective-permute-start | bytes 786440 | tf_op jit(solution)/shard_map/ppermute | solution.py:95
  98.7 28.1 %all-to-all-start = ((bf16[4,2,256,512]{2,3,1,0:T(8,128)(2,1)}), bf16[4,2,256,512]{2,3,1,0:T(8,128)(2,1)S(1)}, u32[]{:S(2)}, u32[]{:S(2)}) async-start(bf16[4,2,256,512]{2,3,1,0:T(8,128)(2,1)} %broadcast_in_dim.102), calls=%async_computation | async-start | bytes 4194304 | tf_op jit(solution)/shard_map/all_to_all | solution.py:105
  102.9 28.8 %collective-permute-start.1 = (bf16[32,64,768]{2,1,0:T(8,128)(2,1)}, bf16[32,64,768]{2,1,0:T(8,128)(2,1)}, u32[]{:S(2)}, u32[]{:S(2)}) collective-permute-start(bf16[32,64,768]{2,1,0:T(8,128)(2,1)} %bitcast.110), channel_id=1, source_target_pairs={{0,8},{8,0},{1,9},{9,1},{2,10},{10,2},{3,11},{11,3},{4,12},{12,4},... | collective-permute-start | bytes 9437192 | tf_op jit(solution)/shard_map/ppermute | solution.py:95
  136.9 6.4 %collective-permute-start.2 = (bf16[256,2,2,128]{3,0,2,1:T(8,128)(2,1)S(1)}, bf16[256,2,2,128]{3,0,2,1:T(8,128)(2,1)S(1)}, u32[]{:S(2)}, u32[]{:S(2)}) collective-permute-start(bf16[256,2,2,128]{3,0,2,1:T(8,128)(2,1)S(1)} %pad_maximum_fusion.3), channel_id=1, source_target_pairs={{0,8},{8,16},{16,24},{24,32},{32,40},{40,48},{48,56},{56,64},{64,7... | collective-permute-start | bytes 786440 | tf_op jit(solution)/shard_map/ppermute | solution.py:100
  138.9 7.7 %collective-permute-start.9 = (bf16[256,2,2,128]{3,0,2,1:T(8,128)(2,1)S(1)}, bf16[256,2,2,128]{3,0,2,1:T(8,128)(2,1)S(1)}, u32[]{:S(2)}, u32[]{:S(2)}) collective-permute-start(bf16[256,2,2,128]{3,0,2,1:T(8,128)(2,1)S(1)} %pad_maximum_fusion.3), channel_id=1, source_target_pairs={{8,0},{16,8},{24,16},{32,24},{40,32},{48,40},{56,48},{64,56},{72,6... | collective-permute-start | bytes 786440 | tf_op jit(solution)/shard_map/ppermute | solution.py:100
  143.3 6.5 %collective-permute-start.3 = (bf16[256,2,2,128]{3,0,2,1:T(8,128)(2,1)S(1)}, bf16[256,2,2,128]{3,0,2,1:T(8,128)(2,1)S(1)}, u32[]{:S(2)}, u32[]{:S(2)}) collective-permute-start(bf16[256,2,2,128]{3,0,2,1:T(8,128)(2,1)S(1)} %collective-permute-done.2), channel_id=1, source_target_pairs={{0,8},{8,16},{16,24},{24,32},{32,40},{40,48},{48,56},{56,64},{64,7... | collective-permute-start | bytes 786440 | tf_op jit(solution)/shard_map/ppermute | solution.py:100
  146.5 38.5 %collective-permute-start.10 = (bf16[256,2,2,128]{3,0,2,1:T(8,128)(2,1)S(1)}, bf16[256,2,2,128]{3,0,2,1:T(8,128)(2,1)S(1)}, u32[]{:S(2)}, u32[]{:S(2)}) collective-permute-start(bf16[256,2,2,128]{3,0,2,1:T(8,128)(2,1)S(1)} %collective-permute-done.9), channel_id=1, source_target_pairs={{8,0},{16,8},{24,16},{32,24},{40,32},{48,40},{56,48},{64,56},{72,6... | collective-permute-start | bytes 786440 | tf_op jit(solution)/shard_map/ppermute | solution.py:100
  149.8 37.1 %collective-permute-start.4 = (bf16[256,2,2,128]{3,0,2,1:T(8,128)(2,1)S(1)}, bf16[256,2,2,128]{3,0,2,1:T(8,128)(2,1)S(1)}, u32[]{:S(2)}, u32[]{:S(2)}) collective-permute-start(bf16[256,2,2,128]{3,0,2,1:T(8,128)(2,1)S(1)} %collective-permute-done.3), channel_id=1, source_target_pairs={{0,8},{8,16},{16,24},{24,32},{32,40},{40,48},{48,56},{56,64},{64,7... | collective-permute-start | bytes 786440 | tf_op jit(solution)/shard_map/ppermute | solution.py:100
  155.0 52.3 %all-to-all-start.3 = ((bf16[8,256,64]{1,2,0:T(8,128)(2,1)}), bf16[8,256,64]{1,2,0:T(8,128)(2,1)S(1)}, u32[]{:S(2)}, u32[]{:S(2)}) async-start(bf16[8,256,64]{1,2,0:T(8,128)(2,1)} %broadcast_in_dim.181), calls=%async_computation.3 | async-start | bytes 524288 | tf_op jit(solution)/shard_map/all_to_all | solution.py:105
  185.0 8.7 %collective-permute-start.11 = (bf16[256,2,2,128]{3,0,2,1:T(8,128)(2,1)S(1)}, bf16[256,2,2,128]{3,0,2,1:T(8,128)(2,1)S(1)}, u32[]{:S(2)}, u32[]{:S(2)}) collective-permute-start(bf16[256,2,2,128]{3,0,2,1:T(8,128)(2,1)S(1)} %collective-permute-done.10), channel_id=1, source_target_pairs={{8,0},{16,8},{24,16},{32,24},{40,32},{48,40},{56,48},{64,56},{72,6... | collective-permute-start | bytes 786440 | tf_op jit(solution)/shard_map/ppermute | solution.py:100
  187.0 8.7 %collective-permute-start.5 = (bf16[256,2,2,128]{3,0,2,1:T(8,128)(2,1)S(1)}, bf16[256,2,2,128]{3,0,2,1:T(8,128)(2,1)S(1)}, u32[]{:S(2)}, u32[]{:S(2)}) collective-permute-start(bf16[256,2,2,128]{3,0,2,1:T(8,128)(2,1)S(1)} %collective-permute-done.4), channel_id=1, source_target_pairs={{0,8},{8,16},{16,24},{24,32},{32,40},{40,48},{48,56},{56,64},{64,7... | collective-permute-start | bytes 786440 | tf_op jit(solution)/shard_map/ppermute | solution.py:100
  193.8 7.8 %collective-permute-start.12 = (bf16[256,2,2,128]{3,0,2,1:T(8,128)(2,1)S(1)}, bf16[256,2,2,128]{3,0,2,1:T(8,128)(2,1)}, u32[]{:S(2)}, u32[]{:S(2)}) collective-permute-start(bf16[256,2,2,128]{3,0,2,1:T(8,128)(2,1)S(1)} %collective-permute-done.11), channel_id=1, source_target_pairs={{8,0},{16,8},{24,16},{32,24},{40,32},{48,40},{56,48},{64,56},{72,6... | collective-permute-start | bytes 786440 | tf_op jit(solution)/shard_map/ppermute | solution.py:100
  195.7 7.8 %collective-permute-start.6 = (bf16[256,2,2,128]{3,0,2,1:T(8,128)(2,1)S(1)}, bf16[256,2,2,128]{3,0,2,1:T(8,128)(2,1)}, u32[]{:S(2)}, u32[]{:S(2)}) collective-permute-start(bf16[256,2,2,128]{3,0,2,1:T(8,128)(2,1)S(1)} %collective-permute-done.5), channel_id=1, source_target_pairs={{0,8},{8,16},{16,24},{24,32},{32,40},{40,48},{48,56},{56,64},{64,7... | collective-permute-start | bytes 786440 | tf_op jit(solution)/shard_map/ppermute | solution.py:100
  201.6 21.8 %collective-permute-start.13 = (bf16[256,2,2,128]{3,0,2,1:T(8,128)(2,1)}, bf16[256,2,2,128]{3,0,2,1:T(8,128)(2,1)}, u32[]{:S(2)}, u32[]{:S(2)}) collective-permute-start(bf16[256,2,2,128]{3,0,2,1:T(8,128)(2,1)} %collective-permute-done.12), channel_id=1, source_target_pairs={{8,0},{16,8},{24,16},{32,24},{40,32},{48,40},{56,48},{64,56},{72,6... | collective-permute-start | bytes 786440 | tf_op jit(solution)/shard_map/ppermute | solution.py:100
  203.5 32.3 %collective-permute-start.7 = (bf16[256,2,2,128]{3,0,2,1:T(8,128)(2,1)}, bf16[256,2,2,128]{3,0,2,1:T(8,128)(2,1)}, u32[]{:S(2)}, u32[]{:S(2)}) collective-permute-start(bf16[256,2,2,128]{3,0,2,1:T(8,128)(2,1)} %collective-permute-done.6), channel_id=1, source_target_pairs={{0,8},{8,16},{16,24},{24,32},{32,40},{40,48},{48,56},{56,64},{64,7... | collective-permute-start | bytes 786440 | tf_op jit(solution)/shard_map/ppermute | solution.py:100
  208.4 31.2 %all-to-all-start.4 = ((bf16[4,8,256,64]{2,3,1,0:T(8,128)(2,1)}), bf16[4,8,256,64]{2,3,1,0:T(8,128)(2,1)S(1)}, u32[]{:S(2)}, u32[]{:S(2)}) async-start(bf16[4,8,256,64]{2,3,1,0:T(8,128)(2,1)} %broadcast_in_dim.182), calls=%async_computation.4 | async-start | bytes 2097152 | tf_op jit(solution)/shard_map/all_to_all | solution.py:105
  223.3 26.4 %collective-permute-start.14 = (bf16[256,2,2,128]{3,0,2,1:T(8,128)(2,1)}, bf16[256,2,2,128]{3,0,2,1:T(8,128)(2,1)}, u32[]{:S(2)}, u32[]{:S(2)}) collective-permute-start(bf16[256,2,2,128]{3,0,2,1:T(8,128)(2,1)} %collective-permute-done.13), channel_id=1, source_target_pairs={{8,0},{16,8},{24,16},{32,24},{40,32},{48,40},{56,48},{64,56},{72,6... | collective-permute-start | bytes 786440 | tf_op jit(solution)/shard_map/ppermute | solution.py:100
  235.8 16.0 %collective-permute-start.8 = (bf16[256,2,2,128]{3,0,2,1:T(8,128)(2,1)}, bf16[256,2,2,128]{3,0,2,1:T(8,128)(2,1)}, u32[]{:S(2)}, u32[]{:S(2)}) collective-permute-start(bf16[256,2,2,128]{3,0,2,1:T(8,128)(2,1)} %collective-permute-done.7), channel_id=1, source_target_pairs={{0,8},{8,16},{16,24},{24,32},{32,40},{40,48},{48,56},{56,64},{64,7... | collective-permute-start | bytes 786440 | tf_op jit(solution)/shard_map/ppermute | solution.py:100
  239.7 39.4 %collective-permute-start.16 = (bf16[32,256,64]{1,2,0:T(8,128)(2,1)S(1)}, bf16[32,256,64]{1,2,0:T(8,128)(2,1)S(1)}, u32[]{:S(2)}, u32[]{:S(2)}) collective-permute-start(bf16[32,256,64]{1,2,0:T(8,128)(2,1)S(1)} %bitcast.108), channel_id=1, source_target_pairs={{0,8},{8,0},{1,9},{9,1},{2,10},{10,2},{3,11},{11,3},{4,12},{12,4},... | collective-permute-start | bytes 3145736 | tf_op jit(solution)/shard_map/ppermute | solution.py:95
  249.7 12.4 %collective-permute-start.15 = (bf16[256,2,2,128]{3,0,2,1:T(8,128)(2,1)}, bf16[256,2,2,128]{3,0,2,1:T(8,128)(2,1)S(1)}, u32[]{:S(2)}, u32[]{:S(2)}) collective-permute-start(bf16[256,2,2,128]{3,0,2,1:T(8,128)(2,1)} %collective-permute-done.14), channel_id=1, source_target_pairs={{8,0},{16,8},{24,16},{32,24},{40,32},{48,40},{56,48},{64,56},{72,6... | collective-permute-start | bytes 786440 | tf_op jit(solution)/shard_map/ppermute | solution.py:100
  281.7 30.1 %all-to-all-start.5 = ((bf16[4,256,2,512]{1,3,2,0:T(8,128)(2,1)}), bf16[4,256,2,512]{1,3,2,0:T(8,128)(2,1)S(1)}, u32[]{:S(2)}, u32[]{:S(2)}) async-start(bf16[4,256,2,512]{1,3,2,0:T(8,128)(2,1)} %copy.73), calls=%async_computation.5 | async-start | bytes 4194304 | tf_op jit(solution)/shard_map/all_to_all | solution.py:186
  312.3 23.7 %collective-permute-start.17 = (bf16[256,512]{1,0:T(8,128)(2,1)S(1)}, bf16[256,512]{1,0:T(8,128)(2,1)S(1)}, u32[]{:S(2)}, u32[]{:S(2)}) collective-permute-start(bf16[256,512]{1,0:T(8,128)(2,1)S(1)} %bitcast.120), channel_id=1, source_target_pairs={{0,4},{4,0},{1,5},{5,1},{2,6},{6,2},{3,7},{7,3},{8,12},{12,8},{9,1... | collective-permute-start | bytes 786440 | tf_op jit(solution)/shard_map/ppermute | solution.py:95
  336.2 5.4 %collective-permute-start.18 = (bf16[48,512]{1,0:T(8,128)(2,1)S(1)}, bf16[48,512]{1,0:T(8,128)(2,1)S(1)}, u32[]{:S(2)}, u32[]{:S(2)}) collective-permute-start(bf16[48,512]{1,0:T(8,128)(2,1)S(1)} %slice.93), channel_id=1, source_target_pairs={{8,0},{16,8},{24,16},{32,24},{40,32},{48,40},{56,48},{64,56},{72,6... | collective-permute-start | bytes 147464 | tf_op jit(solution)/shard_map/ppermute | solution.py:100
  (21 other events, 634.2 us)

commit v6 on v5

--- a/solution.py
+++ b/solution.py
@@ -122,11 +122,22 @@
     first_row = seq_index * rows_here
 
     wq_local = w_qkv.reshape(w_qkv.shape[0], -1)
-    wo_local = w_out.reshape(-1, w_out.shape[-1])
-    wq_mine = gather_seq_blocks(wq_local, n_y, n_zl)
-    wo_mine = gather_seq_blocks(wo_local, n_y, n_zl)
-    wq_other = ring(wq_mine, "c", n_c, 1)
-    wo_other = ring(wo_mine, "c", n_c, 1)
+    width = wq_local.shape[1]
+    wo_rows = -(-w_out.size // (8 * width)) * 8
+    wo_padded = jnp.pad(w_out.reshape(-1), (0, wo_rows * width - w_out.size))
+    both = jnp.concatenate([wq_local, wo_padded.reshape(wo_rows, width)], axis=0)
+    both_mine = gather_seq_blocks(both, n_y, n_zl)
+    both_other = ring(both_mine, "c", n_c, 1)
+    n_j = n_y * n_zl
+    wo_shape = (n_j, w_out.shape[0] * w_out.shape[1], w_out.shape[2])
+
+    def unpack(gathered):
+        wq = gathered[:, : wq_local.shape[0]]
+        wo = gathered[:, wq_local.shape[0] :].reshape(n_j, -1)[:, : w_out.size].reshape(wo_shape)
+        return wq, wo
+
+    wq_mine, wo_mine = unpack(both_mine)
+    wq_other, wo_other = unpack(both_other)
 
     partner = ring(tokens, "zh", n_zh, 1)
     pair = jnp.stack([tokens, partner])

time: 353 us -> 405 us (1.15)
  the two profiles are of different devices: /device:TPU:1 before, /device:TPU:8 now
where the time goes in v6:
time: 405 us; the launch traced here: 403 us
  starting transfers between devices  121 us (30%)
  blocking collectives  117 us (29%)
  waiting for transfers between devices  93.1 us (23%)
  local copies, waits for them, and re-layouts  36.6 us (9%)
  matrix products  20.6 us (5%)
  other arithmetic  13.1 us (3%)
    all_to_all x2, blocking collectives, everyone(): return lax.all_to_all(repeated, axis, 0, 0, tiled=True)  117 us
    ppermute x15, starting transfers between devices, chain(): return lax.ppermute(shard, axis, pairs)  94.8 us
    ppermute x3, waiting for transfers between devices, ring(): lax.ppermute(shard, axis, [(i, (i + by) % size) for i in range(size)])  36.1 us
    all_to_all x1, waiting for transfers between devices, everyone(): return lax.all_to_all(repeated, axis, 0, 0, tiled=True)  24.6 us
    ppermute x3, starting transfers between devices, ring(): lax.ppermute(shard, axis, [(i, (i + by) % size) for i in range(size)])  18.6 us
    all_to_all x1, waiting for transfers between devices, body(): from_peers = lax.all_to_all(by_target, 'x', 0, 0, tiled=True)  17.4 us
    unnamed x79, local copies, waits for them, and re-layouts  15.4 us
    ppermute x15, waiting for transfers between devices, chain(): return lax.ppermute(shard, axis, pairs)  15 us
  transfers between devices with their start and end apart: 20, of which 15 were waited for; matrix products, arithmetic and copies ran while one was open for 9% of the time, Pallas kernels for 0%

profile of v6, /device:TPU:8, one launch (start us, length us, event | category | flops | bytes accessed | tf_op | source)
XLA Modules:
  0.0 403.1 jit_solution(9655810750482137817)
XLA Ops:
  2.2 64.9 %all_to_all.20 = bf16[8,88,768]{2,1,0:T(8,128)(2,1)S(1)} all-to-all(bf16[8,88,768]{2,1,0:T(8,128)(2,1)S(1)} %broadcast_in_dim.92), channel_id=1, replica_groups=mesh['y'=4,'zl'=8,'c'=2,'zh'=2,'x'=4] {'zl'}, dimensions={0} | all-to-all | bytes 2162688 | tf_op jit(solution)/shard_map/all_to_all | solution.py:105
  67.4 52.3 %all_to_all.21 = bf16[4,8,88,768]{3,2,1,0:T(8,128)(2,1)} all-to-all(bf16[4,8,88,768]{3,2,1,0:T(8,128)(2,1)S(1)} %broadcast_in_dim.96), channel_id=1, replica_groups=mesh['y'=4,'zl'=8,'c'=2,'zh'=2,'x'=4] {'y'}, dimensions={0} | all-to-all | bytes 8650752 | tf_op jit(solution)/shard_map/all_to_all | solution.py:105
  121.7 8.2 %collective-permute-start = (bf16[256,512]{1,0:T(8,128)(2,1)S(1)}, bf16[256,512]{1,0:T(8,128)(2,1)S(1)}, u32[]{:S(2)}, u32[]{:S(2)}) collective-permute-start(bf16[256,512]{1,0:T(8,128)(2,1)S(1)} %copy-done.3), channel_id=1, source_target_pairs={{0,4},{4,0},{1,5},{5,1},{2,6},{6,2},{3,7},{7,3},{8,12},{12,8},{9,1... | collective-permute-start | bytes 786440 | tf_op jit(solution)/shard_map/ppermute | solution.py:95
  130.1 27.8 %collective-permute-done = bf16[256,512]{1,0:T(8,128)(2,1)S(1)} collective-permute-done((bf16[256,512]{1,0:T(8,128)(2,1)S(1)}, bf16[256,512]{1,0:T(8,128)(2,1)S(1)}, u32[]{:S(2)}, u32[]{:S(2)}) %collective-permute-start) | collective-permute-done | bytes 262176 | tf_op jit(solution)/shard_map/ppermute | solution.py:95
  159.7 4.3 %all-to-all-start = ((bf16[4,2,256,512]{2,3,1,0:T(8,128)(2,1)}), bf16[4,2,256,512]{2,3,1,0:T(8,128)(2,1)S(1)}, u32[]{:S(2)}, u32[]{:S(2)}) async-start(bf16[4,2,256,512]{2,3,1,0:T(8,128)(2,1)} %broadcast_in_dim.91), calls=%async_computation | async-start | bytes 4194304 | tf_op jit(solution)/shard_map/all_to_all | solution.py:105
  165.4 24.6 %all-to-all-done = bf16[4,2,256,512]{2,3,1,0:T(8,128)(2,1)S(1)} async-done(((bf16[4,2,256,512]{2,3,1,0:T(8,128)(2,1)}), bf16[4,2,256,512]{2,3,1,0:T(8,128)(2,1)S(1)}, u32[]{:S(2)}, u32[]{:S(2)}) %all-to-all-start) | async-done | bytes 2097184 | tf_op jit(solution)/shard_map/all_to_all | solution.py:105
  193.4 2.9 fusion.12
  196.3 2.9 fusion.18
  203.5 11.1 %collective-permute-start.9 = (bf16[256,2,2,128]{3,0,2,1:T(8,128)(2,1)S(1)}, bf16[256,2,2,128]{3,0,2,1:T(8,128)(2,1)S(1)}, u32[]{:S(2)}, u32[]{:S(2)}) collective-permute-start(bf16[256,2,2,128]{3,0,2,1:T(8,128)(2,1)S(1)} %pad_maximum_fusion.3), channel_id=1, source_target_pairs={{8,0},{16,8},{24,16},{32,24},{40,32},{48,40},{56,48},{64,56},{72,6... | collective-permute-start | bytes 786440 | tf_op jit(solution)/shard_map/ppermute | solution.py:100
  214.6 4.3 %collective-permute-done.2 = bf16[256,2,2,128]{3,0,2,1:T(8,128)(2,1)S(1)} collective-permute-done((bf16[256,2,2,128]{3,0,2,1:T(8,128)(2,1)S(1)}, bf16[256,2,2,128]{3,0,2,1:T(8,128)(2,1)S(1)}, u32[]{:S(2)}, u32[]{:S(2)}) %collective-permute-start.2) | collective-permute-done | bytes 262176 | tf_op jit(solution)/shard_map/ppermute | solution.py:100
  221.6 11.1 %collective-permute-start.10 = (bf16[256,2,2,128]{3,0,2,1:T(8,128)(2,1)S(1)}, bf16[256,2,2,128]{3,0,2,1:T(8,128)(2,1)S(1)}, u32[]{:S(2)}, u32[]{:S(2)}) collective-permute-start(bf16[256,2,2,128]{3,0,2,1:T(8,128)(2,1)S(1)} %collective-permute-done.9), channel_id=1, source_target_pairs={{8,0},{16,8},{24,16},{32,24},{40,32},{48,40},{56,48},{64,56},{72,6... | collective-permute-start | bytes 786440 | tf_op jit(solution)/shard_map/ppermute | solution.py:100
  236.6 11.4 %collective-permute-start.11 = (bf16[256,2,2,128]{3,0,2,1:T(8,128)(2,1)S(1)}, bf16[256,2,2,128]{3,0,2,1:T(8,128)(2,1)S(1)}, u32[]{:S(2)}, u32[]{:S(2)}) collective-permute-start(bf16[256,2,2,128]{3,0,2,1:T(8,128)(2,1)S(1)} %collective-permute-done.10), channel_id=1, source_target_pairs={{8,0},{16,8},{24,16},{32,24},{40,32},{48,40},{56,48},{64,56},{72,6... | collective-permute-start | bytes 786440 | tf_op jit(solution)/shard_map/ppermute | solution.py:100
  251.9 11.4 %collective-permute-start.12 = (bf16[256,2,2,128]{3,0,2,1:T(8,128)(2,1)S(1)}, bf16[256,2,2,128]{3,0,2,1:T(8,128)(2,1)S(1)}, u32[]{:S(2)}, u32[]{:S(2)}) collective-permute-start(bf16[256,2,2,128]{3,0,2,1:T(8,128)(2,1)S(1)} %collective-permute-done.11), channel_id=1, source_target_pairs={{8,0},{16,8},{24,16},{32,24},{40,32},{48,40},{56,48},{64,56},{72,6... | collective-permute-start | bytes 786440 | tf_op jit(solution)/shard_map/ppermute | solution.py:100
  267.2 11.4 %collective-permute-start.13 = (bf16[256,2,2,128]{3,0,2,1:T(8,128)(2,1)S(1)}, bf16[256,2,2,128]{3,0,2,1:T(8,128)(2,1)}, u32[]{:S(2)}, u32[]{:S(2)}) collective-permute-start(bf16[256,2,2,128]{3,0,2,1:T(8,128)(2,1)S(1)} %collective-permute-done.12), channel_id=1, source_target_pairs={{8,0},{16,8},{24,16},{32,24},{40,32},{48,40},{56,48},{64,56},{72,6... | collective-permute-start | bytes 786440 | tf_op jit(solution)/shard_map/ppermute | solution.py:100
  282.4 11.5 %collective-permute-start.14 = (bf16[256,2,2,128]{3,0,2,1:T(8,128)(2,1)}, bf16[256,2,2,128]{3,0,2,1:T(8,128)(2,1)}, u32[]{:S(2)}, u32[]{:S(2)}) collective-permute-start(bf16[256,2,2,128]{3,0,2,1:T(8,128)(2,1)} %collective-permute-done.13), channel_id=1, source_target_pairs={{8,0},{16,8},{24,16},{32,24},{40,32},{48,40},{56,48},{64,56},{72,6... | collective-permute-start | bytes 786440 | tf_op jit(solution)/shard_map/ppermute | solution.py:100
  307.0 3.0 reshape.651
  311.6 11.3 %collective-permute-start.15 = (bf16[256,2,2,128]{3,0,2,1:T(8,128)(2,1)}, bf16[256,2,2,128]{3,0,2,1:T(8,128)(2,1)S(1)}, u32[]{:S(2)}, u32[]{:S(2)}) collective-permute-start(bf16[256,2,2,128]{3,0,2,1:T(8,128)(2,1)} %collective-permute-done.14), channel_id=1, source_target_pairs={{8,0},{16,8},{24,16},{32,24},{40,32},{48,40},{56,48},{64,56},{72,6... | collective-permute-start | bytes 786440 | tf_op jit(solution)/shard_map/ppermute | solution.py:100
  335.3 8.6 %fusion.53 = (f32[2,256]{1,0:T(2,128)S(1)}, f32[2,256,3840]{2,1,0:T(8,128)}) fusion(pred[256,3840]{1,0:T(8,128)(4,1)S(1)} %copy-done.5, bf16[3840,2,2,128]{3,0,2,1:T(8,128)(2,1)} %copy-done.23, bf16[256,2,32]{2,0,1:T(8,128)(2,1)S(1)} %copy-done.21, bf16[256,2,32]{2,0,1:T(8,128)(2,1)S(1)} %copy-done.22, bf16[256,2,32]{2,0,1:T(8,128)(2,1)S(1)} %copy-done.19, ...), kind=kOutput, calls=%fused_computation.134 | convolution fusion | flops 513675008 | bytes 12322816 | tf_op jit(solution)/shard_map/sub | solution.py:79
  343.9 5.4 %fusion.22 = bf16[2,128,256]{2,1,0:T(8,128)(2,1)S(1)} fusion(f32[2,256,3840]{2,1,0:T(8,128)} %get-tuple-element.43, f32[2,256]{1,0:T(2,128)S(1)} %broadcast_select_fusion, bf16[3840,2,2,128]{3,0,2,1:T(8,128)(2,1)} %copy-done.23, pred[256]{0:T(512)(128)(4,1)S(1)} %get-tuple-element.11), kind=kOutput, calls=%fused_computation.28 | convolution fusion | flops 507379712 | bytes 9963776 | tf_op jit(solution)/shard_map/vgm,mvb->gvb/dot_general | solution.py:83
  353.1 3.8 all-to-all-start.3
  357.3 17.4 %all-to-all-done.3 = bf16[4,256,2,512]{1,3,2,0:T(8,128)(2,1)S(1)} async-done(((bf16[4,256,2,512]{1,3,2,0:T(8,128)(2,1)}), bf16[4,256,2,512]{1,3,2,0:T(8,128)(2,1)S(1)}, u32[]{:S(2)}, u32[]{:S(2)}) %all-to-all-start.3) | async-done | bytes 2097184 | tf_op jit(solution)/shard_map/all_to_all | solution.py:197
  375.2 8.4 %collective-permute-start.16 = (bf16[256,512]{1,0:T(8,128)(2,1)S(1)}, bf16[256,512]{1,0:T(8,128)(2,1)S(1)}, u32[]{:S(2)}, u32[]{:S(2)}) collective-permute-start(bf16[256,512]{1,0:T(8,128)(2,1)S(1)} %bitcast.116), channel_id=1, source_target_pairs={{0,4},{4,0},{1,5},{5,1},{2,6},{6,2},{3,7},{7,3},{8,12},{12,8},{9,1... | collective-permute-start | bytes 786440 | tf_op jit(solution)/shard_map/ppermute | solution.py:95
  384.0 8.3 %collective-permute-done.16 = bf16[256,512]{1,0:T(8,128)(2,1)S(1)} collective-permute-done((bf16[256,512]{1,0:T(8,128)(2,1)S(1)}, bf16[256,512]{1,0:T(8,128)(2,1)S(1)}, u32[]{:S(2)}, u32[]{:S(2)}) %collective-permute-start.16) | collective-permute-done | bytes 262176 | tf_op jit(solution)/shard_map/ppermute | solution.py:95
  396.1 4.0 gather_fusion
  (176 shorter events, 71.6 us)
Async XLA Ops:
  67.4 54.3 %copy-start.3 = (bf16[256,512]{1,0:T(8,128)(2,1)S(1)}, bf16[256,512]{1,0:T(8,128)(2,1)}, u32[]{:S(2)}) copy-start(bf16[256,512]{1,0:T(8,128)(2,1)} %param.8) | copy-start | bytes 786436
  67.4 62.5 %copy-start.24 = (f32[4096]{0:T(1024)S(1)}, f32[4096]{0:T(1024)}, u32[]{:S(2)}) copy-start(f32[4096]{0:T(1024)} %param.9) | copy-start | bytes 49156
  67.4 62.6 %copy-start.25 = (f32[4096]{0:T(1024)S(1)}, f32[4096]{0:T(1024)}, u32[]{:S(2)}) copy-start(f32[4096]{0:T(1024)} %param.10) | copy-start | bytes 49156
  119.8 76.5 %collective-permute-start.1 = (bf16[32,88,768]{2,1,0:T(8,128)(2,1)}, bf16[32,88,768]{2,1,0:T(8,128)(2,1)}, u32[]{:S(2)}, u32[]{:S(2)}) collective-permute-start(bf16[32,88,768]{2,1,0:T(8,128)(2,1)} %bitcast.6), channel_id=1, source_target_pairs={{0,8},{8,0},{1,9},{9,1},{2,10},{10,2},{3,11},{11,3},{4,12},{12,4},... | collective-permute-start | bytes 12976136 | tf_op jit(solution)/shard_map/ppermute | solution.py:95
  121.7 36.2 %collective-permute-start = (bf16[256,512]{1,0:T(8,128)(2,1)S(1)}, bf16[256,512]{1,0:T(8,128)(2,1)S(1)}, u32[]{:S(2)}, u32[]{:S(2)}) collective-permute-start(bf16[256,512]{1,0:T(8,128)(2,1)S(1)} %copy-done.3), channel_id=1, source_target_pairs={{0,4},{4,0},{1,5},{5,1},{2,6},{6,2},{3,7},{7,3},{8,12},{12,8},{9,1... | collective-permute-start | bytes 786440 | tf_op jit(solution)/shard_map/ppermute | solution.py:95
  159.7 30.4 %all-to-all-start = ((bf16[4,2,256,512]{2,3,1,0:T(8,128)(2,1)}), bf16[4,2,256,512]{2,3,1,0:T(8,128)(2,1)S(1)}, u32[]{:S(2)}, u32[]{:S(2)}) async-start(bf16[4,2,256,512]{2,3,1,0:T(8,128)(2,1)} %broadcast_in_dim.91), calls=%async_computation | async-start | bytes 4194304 | tf_op jit(solution)/shard_map/all_to_all | solution.py:105
  201.5 17.4 %collective-permute-start.2 = (bf16[256,2,2,128]{3,0,2,1:T(8,128)(2,1)S(1)}, bf16[256,2,2,128]{3,0,2,1:T(8,128)(2,1)S(1)}, u32[]{:S(2)}, u32[]{:S(2)}) collective-permute-start(bf16[256,2,2,128]{3,0,2,1:T(8,128)(2,1)S(1)} %pad_maximum_fusion.3), channel_id=1, source_target_pairs={{0,8},{8,16},{16,24},{24,32},{32,40},{40,48},{48,56},{56,64},{64,7... | collective-permute-start | bytes 786440 | tf_op jit(solution)/shard_map/ppermute | solution.py:100
  203.5 17.4 %collective-permute-start.9 = (bf16[256,2,2,128]{3,0,2,1:T(8,128)(2,1)S(1)}, bf16[256,2,2,128]{3,0,2,1:T(8,128)(2,1)S(1)}, u32[]{:S(2)}, u32[]{:S(2)}) collective-permute-start(bf16[256,2,2,128]{3,0,2,1:T(8,128)(2,1)S(1)} %pad_maximum_fusion.3), channel_id=1, source_target_pairs={{8,0},{16,8},{24,16},{32,24},{40,32},{48,40},{56,48},{64,56},{72,6... | collective-permute-start | bytes 786440 | tf_op jit(solution)/shard_map/ppermute | solution.py:100
  218.9 15.4 %collective-permute-start.3 = (bf16[256,2,2,128]{3,0,2,1:T(8,128)(2,1)S(1)}, bf16[256,2,2,128]{3,0,2,1:T(8,128)(2,1)S(1)}, u32[]{:S(2)}, u32[]{:S(2)}) collective-permute-start(bf16[256,2,2,128]{3,0,2,1:T(8,128)(2,1)S(1)} %collective-permute-done.2), channel_id=1, source_target_pairs={{0,8},{8,16},{16,24},{24,32},{32,40},{40,48},{48,56},{56,64},{64,7... | collective-permute-start | bytes 786440 | tf_op jit(solution)/shard_map/ppermute | solution.py:100
  221.6 15.0 %collective-permute-start.10 = (bf16[256,2,2,128]{3,0,2,1:T(8,128)(2,1)S(1)}, bf16[256,2,2,128]{3,0,2,1:T(8,128)(2,1)S(1)}, u32[]{:S(2)}, u32[]{:S(2)}) collective-permute-start(bf16[256,2,2,128]{3,0,2,1:T(8,128)(2,1)S(1)} %collective-permute-done.9), channel_id=1, source_target_pairs={{8,0},{16,8},{24,16},{32,24},{40,32},{48,40},{56,48},{64,56},{72,6... | collective-permute-start | bytes 786440 | tf_op jit(solution)/shard_map/ppermute | solution.py:100
  234.3 15.4 %collective-permute-start.4 = (bf16[256,2,2,128]{3,0,2,1:T(8,128)(2,1)S(1)}, bf16[256,2,2,128]{3,0,2,1:T(8,128)(2,1)S(1)}, u32[]{:S(2)}, u32[]{:S(2)}) collective-permute-start(bf16[256,2,2,128]{3,0,2,1:T(8,128)(2,1)S(1)} %collective-permute-done.3), channel_id=1, source_target_pairs={{0,8},{8,16},{16,24},{24,32},{32,40},{40,48},{48,56},{56,64},{64,7... | collective-permute-start | bytes 786440 | tf_op jit(solution)/shard_map/ppermute | solution.py:100
  236.6 15.3 %collective-permute-start.11 = (bf16[256,2,2,128]{3,0,2,1:T(8,128)(2,1)S(1)}, bf16[256,2,2,128]{3,0,2,1:T(8,128)(2,1)S(1)}, u32[]{:S(2)}, u32[]{:S(2)}) collective-permute-start(bf16[256,2,2,128]{3,0,2,1:T(8,128)(2,1)S(1)} %collective-permute-done.10), channel_id=1, source_target_pairs={{8,0},{16,8},{24,16},{32,24},{40,32},{48,40},{56,48},{64,56},{72,6... | collective-permute-start | bytes 786440 | tf_op jit(solution)/shard_map/ppermute | solution.py:100
  249.7 15.2 %collective-permute-start.5 = (bf16[256,2,2,128]{3,0,2,1:T(8,128)(2,1)S(1)}, bf16[256,2,2,128]{3,0,2,1:T(8,128)(2,1)S(1)}, u32[]{:S(2)}, u32[]{:S(2)}) collective-permute-start(bf16[256,2,2,128]{3,0,2,1:T(8,128)(2,1)S(1)} %collective-permute-done.4), channel_id=1, source_target_pairs={{0,8},{8,16},{16,24},{24,32},{32,40},{40,48},{48,56},{56,64},{64,7... | collective-permute-start | bytes 786440 | tf_op jit(solution)/shard_map/ppermute | solution.py:100
  251.9 49.2 %copy-start.12 = (bf16[256,2,2,128]{3,0,2,1:T(8,128)(2,1)}, bf16[256,2,2,128]{3,0,2,1:T(8,128)(2,1)S(1)}, u32[]{:S(2)}) copy-start(bf16[256,2,2,128]{3,0,2,1:T(8,128)(2,1)S(1)} %collective-permute-done.11) | copy-start | bytes 786436
  251.9 15.3 %collective-permute-start.12 = (bf16[256,2,2,128]{3,0,2,1:T(8,128)(2,1)S(1)}, bf16[256,2,2,128]{3,0,2,1:T(8,128)(2,1)S(1)}, u32[]{:S(2)}, u32[]{:S(2)}) collective-permute-start(bf16[256,2,2,128]{3,0,2,1:T(8,128)(2,1)S(1)} %collective-permute-done.11), channel_id=1, source_target_pairs={{8,0},{16,8},{24,16},{32,24},{40,32},{48,40},{56,48},{64,56},{72,6... | collective-permute-start | bytes 786440 | tf_op jit(solution)/shard_map/ppermute | solution.py:100
  264.9 15.3 %collective-permute-start.6 = (bf16[256,2,2,128]{3,0,2,1:T(8,128)(2,1)S(1)}, bf16[256,2,2,128]{3,0,2,1:T(8,128)(2,1)S(1)}, u32[]{:S(2)}, u32[]{:S(2)}) collective-permute-start(bf16[256,2,2,128]{3,0,2,1:T(8,128)(2,1)S(1)} %collective-permute-done.5), channel_id=1, source_target_pairs={{0,8},{8,16},{16,24},{24,32},{32,40},{40,48},{48,56},{56,64},{64,7... | collective-permute-start | bytes 786440 | tf_op jit(solution)/shard_map/ppermute | solution.py:100
  267.2 15.3 %collective-permute-start.13 = (bf16[256,2,2,128]{3,0,2,1:T(8,128)(2,1)S(1)}, bf16[256,2,2,128]{3,0,2,1:T(8,128)(2,1)}, u32[]{:S(2)}, u32[]{:S(2)}) collective-permute-start(bf16[256,2,2,128]{3,0,2,1:T(8,128)(2,1)S(1)} %collective-permute-done.12), channel_id=1, source_target_pairs={{8,0},{16,8},{24,16},{32,24},{40,32},{48,40},{56,48},{64,56},{72,6... | collective-permute-start | bytes 786440 | tf_op jit(solution)/shard_map/ppermute | solution.py:100
  280.2 15.3 %collective-permute-start.7 = (bf16[256,2,2,128]{3,0,2,1:T(8,128)(2,1)S(1)}, bf16[256,2,2,128]{3,0,2,1:T(8,128)(2,1)}, u32[]{:S(2)}, u32[]{:S(2)}) collective-permute-start(bf16[256,2,2,128]{3,0,2,1:T(8,128)(2,1)S(1)} %collective-permute-done.6), channel_id=1, source_target_pairs={{0,8},{8,16},{16,24},{24,32},{32,40},{40,48},{48,56},{56,64},{64,7... | collective-permute-start | bytes 786440 | tf_op jit(solution)/shard_map/ppermute | solution.py:100
  282.4 29.2 %collective-permute-start.14 = (bf16[256,2,2,128]{3,0,2,1:T(8,128)(2,1)}, bf16[256,2,2,128]{3,0,2,1:T(8,128)(2,1)}, u32[]{:S(2)}, u32[]{:S(2)}) collective-permute-start(bf16[256,2,2,128]{3,0,2,1:T(8,128)(2,1)} %collective-permute-done.13), channel_id=1, source_target_pairs={{8,0},{16,8},{24,16},{32,24},{40,32},{48,40},{56,48},{64,56},{72,6... | collective-permute-start | bytes 786440 | tf_op jit(solution)/shard_map/ppermute | solution.py:100
  295.5 27.4 %collective-permute-start.8 = (bf16[256,2,2,128]{3,0,2,1:T(8,128)(2,1)}, bf16[256,2,2,128]{3,0,2,1:T(8,128)(2,1)}, u32[]{:S(2)}, u32[]{:S(2)}) collective-permute-start(bf16[256,2,2,128]{3,0,2,1:T(8,128)(2,1)} %collective-permute-done.7), channel_id=1, source_target_pairs={{0,8},{8,16},{16,24},{24,32},{32,40},{40,48},{48,56},{56,64},{64,7... | collective-permute-start | bytes 786440 | tf_op jit(solution)/shard_map/ppermute | solution.py:100
  311.6 21.8 %collective-permute-start.15 = (bf16[256,2,2,128]{3,0,2,1:T(8,128)(2,1)}, bf16[256,2,2,128]{3,0,2,1:T(8,128)(2,1)S(1)}, u32[]{:S(2)}, u32[]{:S(2)}) collective-permute-start(bf16[256,2,2,128]{3,0,2,1:T(8,128)(2,1)} %collective-permute-done.14), channel_id=1, source_target_pairs={{8,0},{16,8},{24,16},{32,24},{40,32},{48,40},{56,48},{64,56},{72,6... | collective-permute-start | bytes 786440 | tf_op jit(solution)/shard_map/ppermute | solution.py:100
  353.1 21.6 %all-to-all-start.3 = ((bf16[4,256,2,512]{1,3,2,0:T(8,128)(2,1)}), bf16[4,256,2,512]{1,3,2,0:T(8,128)(2,1)S(1)}, u32[]{:S(2)}, u32[]{:S(2)}) async-start(bf16[4,256,2,512]{1,3,2,0:T(8,128)(2,1)} %copy.81), calls=%async_computation.3 | async-start | bytes 4194304 | tf_op jit(solution)/shard_map/all_to_all | solution.py:197
  375.2 17.0 %collective-permute-start.16 = (bf16[256,512]{1,0:T(8,128)(2,1)S(1)}, bf16[256,512]{1,0:T(8,128)(2,1)S(1)}, u32[]{:S(2)}, u32[]{:S(2)}) collective-permute-start(bf16[256,512]{1,0:T(8,128)(2,1)S(1)} %bitcast.116), channel_id=1, source_target_pairs={{0,4},{4,0},{1,5},{5,1},{2,6},{6,2},{3,7},{7,3},{8,12},{12,8},{9,1... | collective-permute-start | bytes 786440 | tf_op jit(solution)/shard_map/ppermute | solution.py:95
  392.4 3.7 collective-permute-start.17
  (25 other events, 375.9 us)
